TPU v7x, 32 devices: a whole 2x2x4 slice. The times are simulated.
32 devices in a mesh: seq: 4 (over y, x), vocab: 8 (over z, core).
Axes of the slice: x: 2, y: 2, z: 4, core: 2. Of those that a mesh axis runs over, the one named last changes fastest.
Arguments:
- pre_query: bfloat16 [8, 2048, 2560], P('vocab', 'seq')
- pre_fresh: bfloat16 [8, 2048, 512], P('vocab', 'seq'), may hold values from -6 to 6
- pre_cache: bfloat16 [8, 2048, 512], P('vocab', 'seq'), may hold values from -6 to 6
- pre_start: int32 [8], P('vocab'), may hold values from 0 to 6143
- pre_resid: bfloat16 [8, 2048, 2560], P('vocab', 'seq'), may hold values from -0.75 to 0.75
- dec_query: bfloat16 [32, 2560], P(('seq', 'vocab'))
- dec_fresh: bfloat16 [32, 512], P(('seq', 'vocab')), may hold values from -6 to 6
- decode_window_cache: bfloat16 [32, 2048, 512], P(('seq', 'vocab')), may hold values from -6 to 6
- dec_length: int32 [32], P(('seq', 'vocab')), may hold values from 1 to 8192
- dec_resid: bfloat16 [32, 2560], P(('seq', 'vocab')), may hold values from -0.75 to 0.75
- out_weight: bfloat16 [2560, 2560], P('vocab'), may hold values from -0.125 to 0.125
- norm_gain: float32 [2560], replicated, may hold values from 0.5 to 1.5
- embedding: bfloat16 [256000, 2560], P(('seq', 'vocab'))
Outputs:
- pre_out: bfloat16 [8, 2048, 2560], P('vocab', 'seq')
- dec_out: bfloat16 [32, 2560], P(('seq', 'vocab'))
- dec_logp: bfloat16 [32, 256000], P(None, ('seq', 'vocab'))
- pre_logp: bfloat16 [8, 256000], P(None, ('seq', 'vocab'))
All inputs are finite; a program needn't handle non-finite values.
Results may differ from a plain program's by a relative error of at most 0.0065.
Values may be sent and summed in bfloat16 or wider, within the bound.
No kernel may reach another device: no remote copies, remote signals or barrier semaphores. Data moves between devices by JAX's collectives and lax.ppermute only.
A program may use at most 320 MiB of HBM per device.

v0:
```python
import jax
import jax.numpy as jnp
from jax import lax
from jax.sharding import PartitionSpec as P

D = 2560
HQ = 10
HEAD_SIZE = 256
WIN = 2048


NEG_BIG = -1e30
STABILITY_FLOOR = 1e-06


def from_behind(value, axis, steps):
    count = lax.axis_size(axis)
    pairs = [(source, (source + steps) % count) for source in range(count)]
    return lax.ppermute(value, axis, pairs)


def joined(value, axis, join):
    pieces = jax.tree.map(lambda part: lax.all_gather(part, axis), value)
    head = jax.tree.map(lambda part: part[0], pieces)
    tail = jax.tree.map(lambda part: part[1:], pieces)
    so_far, _ = lax.scan(lambda so_far, share: (join(so_far, share), None), head, tail)
    return so_far


def normalize(rows_in, gain):
    values = rows_in.astype(jnp.float32)
    square_mean = jnp.mean(values * values, axis=-1, keepdims=True)
    return (values * lax.rsqrt(square_mean + STABILITY_FLOOR) * gain).astype(jnp.bfloat16)


def combine_totals(first, second):
    peak_new = jnp.maximum(first[0], second[0])
    summed = first[1] * jnp.exp(first[0] - peak_new) + second[1] * jnp.exp(second[0] - peak_new)
    return (peak_new, summed)


def body(
    pre_query,
    pre_fresh,
    pre_cache,
    pre_start,
    pre_resid,
    dec_query,
    dec_fresh,
    decode_window_cache,
    dec_length,
    dec_resid,
    out_weight,
    norm_gain,
    embedding,
):
    seq_count = lax.axis_size("seq")
    seq_index = lax.axis_index("seq")
    local_pre = pre_query.shape[0]
    block_query = pre_query.shape[1]
    block_cache = pre_cache.shape[1]
    score_scale = HEAD_SIZE ** (-0.5)
    query_rows = pre_query.reshape(local_pre, block_query * HQ, HEAD_SIZE)
    query_offset = (seq_index * block_query + jnp.arange(block_query * HQ, dtype=jnp.int32) // HQ)[
        :, None
    ]
    kv_block = jnp.concatenate([pre_cache, pre_fresh], axis=1)

    def absorb(state, block, source_tokens):
        key_offset = jnp.concatenate(
            [
                source_tokens * block_cache - WIN + jnp.arange(block_cache, dtype=jnp.int32),
                source_tokens * block_query + jnp.arange(block_query, dtype=jnp.int32),
            ]
        )
        valid_mask = (key_offset[None, :] <= query_offset) & (
            query_offset - key_offset[None, :] < WIN
        )
        valid_mask = valid_mask[None, :, :] & (
            pre_start[:, None, None] + key_offset[None, None, :] >= 0
        )
        scores = (
            jnp.einsum(
                "pqd,pkd->pqk",
                query_rows,
                block[:, :, :HEAD_SIZE],
                preferred_element_type=jnp.float32,
            )
            * score_scale
        )
        peak_old, denom_sum, accum = state
        peak_new = jnp.maximum(
            peak_old, jnp.max(jnp.where(valid_mask, scores, NEG_BIG), axis=2, keepdims=True)
        )
        weights = jnp.where(valid_mask, jnp.exp(scores - peak_new), 0.0)
        decay_rate = jnp.exp(peak_old - peak_new)
        denom_sum = denom_sum * decay_rate + jnp.sum(weights, axis=2, keepdims=True)
        accum = accum * decay_rate + jnp.einsum(
            "pqk,pkd->pqd",
            weights.astype(jnp.bfloat16),
            block[:, :, HEAD_SIZE:],
            preferred_element_type=jnp.float32,
        )
        return (peak_new, denom_sum, accum)

    start_state = (
        jnp.full((local_pre, block_query * HQ, 1), NEG_BIG, jnp.float32),
        jnp.zeros((local_pre, block_query * HQ, 1), jnp.float32),
        jnp.zeros((local_pre, block_query * HQ, HEAD_SIZE), jnp.float32),
    )
    state = absorb(start_state, kv_block, seq_index)
    moving = kv_block
    for cycle_step in range(1, seq_count):
        moving = from_behind(moving, "seq", 1)
        state = absorb(state, moving, jnp.mod(seq_index - cycle_step, seq_count))
    pre_mixed = (
        (state[2] / state[1]).astype(jnp.bfloat16).reshape(local_pre * block_query, HQ * HEAD_SIZE)
    )
    decode_token_rows = dec_query.reshape(-1, HQ, HEAD_SIZE)
    cache_scores = (
        jnp.einsum(
            "vfx,vzx->vfz",
            decode_token_rows,
            decode_window_cache[:, :, :HEAD_SIZE],
            preferred_element_type=jnp.float32,
        )
        * score_scale
    )
    self_scores = (
        jnp.einsum(
            "bhd,bd->bh",
            decode_token_rows,
            dec_fresh[:, :HEAD_SIZE],
            preferred_element_type=jnp.float32,
        )[:, :, None]
        * score_scale
    )
    slot_index = jnp.arange(WIN, dtype=jnp.int32)[None, :]
    length_col = dec_length[:, None]
    held_pos = length_col - 1 - jnp.mod(length_col - 1 - slot_index, WIN)
    live_mask = ((held_pos >= 0) & (held_pos > length_col - WIN))[:, None, :]
    peak_score = jnp.maximum(
        jnp.max(jnp.where(live_mask, cache_scores, NEG_BIG), axis=2, keepdims=True), self_scores
    )
    cache_attention_weights = jnp.where(live_mask, jnp.exp(cache_scores - peak_score), 0.0)
    self_weights = jnp.exp(self_scores - peak_score)
    denom_sum = jnp.sum(cache_attention_weights, axis=2, keepdims=True) + self_weights
    self_rounded = lax.optimization_barrier(self_weights.astype(jnp.bfloat16)).astype(jnp.float32)
    cache_part = jnp.einsum(
        "ect,ety->ecy",
        cache_attention_weights.astype(jnp.bfloat16),
        decode_window_cache[:, :, HEAD_SIZE:],
        preferred_element_type=jnp.float32,
    )
    self_part = self_rounded * dec_fresh[:, None, HEAD_SIZE:].astype(jnp.float32)
    dec_mixed = (
        ((cache_part + self_part) / denom_sum).astype(jnp.bfloat16).reshape(-1, HQ * HEAD_SIZE)
    )
    mixed_rows = jnp.concatenate([pre_mixed, dec_mixed], axis=0)
    projected = jnp.dot(
        mixed_rows,
        lax.all_gather(out_weight, "vocab", axis=0, tiled=True),
        preferred_element_type=jnp.float32,
    )
    pre_rows = local_pre * block_query
    pre_out = (
        pre_resid.astype(jnp.float32) + projected[:pre_rows].reshape(local_pre, block_query, D)
    ).astype(jnp.bfloat16)
    dec_out = (dec_resid.astype(jnp.float32) + projected[pre_rows:]).astype(jnp.bfloat16)
    head_decode = normalize(dec_out, norm_gain)
    head_prefill = normalize(pre_out[:, block_query - 1, :], norm_gain)
    local_dec = head_decode.shape[0]
    vocab_count = lax.axis_size("vocab")
    local_head = jnp.concatenate([head_decode, head_prefill], axis=0)
    everyone = lax.all_gather(local_head, ("seq", "vocab"), axis=0, tiled=True)
    layout = everyone.reshape(seq_count, vocab_count, local_dec + local_pre, D)
    decode_all = layout[:, :, :local_dec].reshape(-1, D)
    prefill_every_request = layout[seq_count - 1, :, local_dec:].reshape(-1, D)
    head_rows = jnp.concatenate([decode_all, prefill_every_request], axis=0)
    logits = lax.dot_general(
        head_rows, embedding, (((1,), (1,)), ((), ())), preferred_element_type=jnp.float32
    )
    local_peak = jnp.max(logits, axis=1, keepdims=True)
    local_sum = jnp.sum(jnp.exp(logits - local_peak), axis=1, keepdims=True)
    global_peak, global_sum = joined((local_peak, local_sum), ("seq", "vocab"), combine_totals)
    total = global_peak + jnp.log(global_sum)
    log_probs = (logits - total).astype(jnp.bfloat16)
    dec_count = decode_all.shape[0]
    return (pre_out, dec_out, log_probs[:dec_count], log_probs[dec_count:])


def solution(mesh):
    in_specs = (
        P("vocab", "seq", None),
        P("vocab", "seq", None),
        P("vocab", "seq", None),
        P("vocab"),
        P("vocab", "seq", None),
        P(("seq", "vocab"), None),
        P(("seq", "vocab"), None),
        P(("seq", "vocab"), None, None),
        P(("seq", "vocab")),
        P(("seq", "vocab"), None),
        P("vocab", None),
        P(),
        P(("seq", "vocab"), None),
    )
    out_specs = (
        P("vocab", "seq", None),
        P(("seq", "vocab"), None),
        P(None, ("seq", "vocab")),
        P(None, ("seq", "vocab")),
    )
    return jax.shard_map(body, mesh=mesh, in_specs=in_specs, out_specs=out_specs, check_vma=False)
```

profile of v0, /device:TPU:0, one launch (start us, length us, event | category | flops | bytes accessed | tf_op | source)
XLA Modules:
  0.0 362.2 jit_solution(16198304512585942815)
XLA Ops:
  7.2 0.0 copy-start.6
  7.2 0.0 copy-start.9
  7.2 0.0 all-gather.5.cloned.1.call-start
  7.2 1.9 constant_dynamic-update-slice_fusion.1
  9.1 1.9 constant_dynamic-update-slice_fusion
  11.0 2.9 collective-permute-start
  13.9 0.0 all-gather.5.cloned.1.call-update
  14.8 5.0 %reshape.520 = bf16[5120,256]{1,0:T(8,128)(2,1)S(1)} reshape(bf16[1,512,2560]{2,1,0:T(8,128)(2,1)} %param.15) | data formatting | bytes 5242880 | tf_op jit(solution)/shard_map/reshape.2
  20.5 0.0 copy-done.6
  20.6 0.0 copy-done.9
  20.6 0.1 fusion.77
  20.7 1.8 select_reduce_fusion
  22.6 0.2 fusion.90
  22.8 1.6 fusion.76
  24.4 0.6 copy.20
  25.0 9.8 %fusion.85 = f32[1024,5120]{1,0:T(8,128)} fusion(bf16[5120,256]{1,0:T(8,128)(2,1)S(1)} %reshape.520, bf16[1,1024,512]{2,1,0:T(8,128)(2,1)} %constant_dynamic-update-slice_fusion), kind=kOutput, calls=%fused_computation.90 | convolution fusion | flops 2684354560 | bytes 24117248 | tf_op jit(solution)/shard_map/pqd,pkd->pqk/dot_general | solution.py:83
  34.9 3.5 collective-permute-done
  38.3 0.8 collective-permute-start.1
  39.1 9.9 %fusion.84 = f32[1024,5120]{1,0:T(8,128)} fusion(bf16[5120,256]{1,0:T(8,128)(2,1)S(1)} %reshape.520, bf16[1,1024,512]{2,1,0:T(8,128)(2,1)} %collective-permute-done), kind=kOutput, calls=%fused_computation.87 | convolution fusion | flops 2684354560 | bytes 24117248 | tf_op jit(solution)/shard_map/pqd,pkd->pqk/dot_general | solution.py:83
  49.0 14.8 %collective-permute-done.1 = bf16[1,1024,512]{2,1,0:T(8,128)(2,1)S(1)} collective-permute-done((bf16[1,1024,512]{2,1,0:T(8,128)(2,1)}, bf16[1,1024,512]{2,1,0:T(8,128)(2,1)S(1)}, u32[]{:S(2)}, u32[]{:S(2)}) %collective-permute-start.1) | collective-permute-done | bytes 1048608 | tf_op jit(solution)/shard_map/ppermute | solution.py:19
  63.8 0.0 copy-start.2
  63.8 0.2 collective-permute-start.2
  64.0 8.6 %fusion.83 = f32[1024,5120]{1,0:T(8,128)} fusion(bf16[5120,256]{1,0:T(8,128)(2,1)S(1)} %reshape.520, bf16[1,1024,512]{2,1,0:T(8,128)(2,1)S(1)} %collective-permute-done.1), kind=kOutput, calls=%fused_computation.84 | convolution fusion | flops 2684354560 | bytes 24117248 | tf_op jit(solution)/shard_map/pqd,pkd->pqk/dot_general | solution.py:83
  72.6 0.0 copy-done.2
  72.6 15.8 %collective-permute-done.2 = bf16[1,1024,512]{2,1,0:T(8,128)(2,1)S(1)} collective-permute-done((bf16[1,1024,512]{2,1,0:T(8,128)(2,1)S(1)}, bf16[1,1024,512]{2,1,0:T(8,128)(2,1)S(1)}, u32[]{:S(2)}, u32[]{:S(2)}) %collective-permute-start.2) | collective-permute-done | bytes 1048608 | tf_op jit(solution)/shard_map/ppermute | solution.py:19
  88.4 37.9 %fusion.5 = (f32[5120]{0:T(1024)S(1)}, f32[5120]{0:T(1024)S(1)}, f32[5120]{0:T(1024)S(1)}, f32[5120]{0:T(1024)S(1)}, f32[1024,5120]{1,0:T(8,128)}) fusion(pred[1024]{0:T(1024)(128)(4,1)S(1)} %get-tuple-element.74, s32[5120]{0:T(1024)S(1)} %fusion.96, s32[1024]{0:T(1024)S(1)} %get-tuple-element.81, f32[1024,5120]{1,0:T(8,128)} %fusion.85, ...), kind=kOutput, calls=%fused_computation.9 | convolution fusion | flops 2852106240 | bytes 87154688 | tf_op jit(solution)/shard_map/pqd,pkd->pqk/dot_general | solution.py:83
  126.3 0.0 copy-done.10
  126.3 43.5 %fusion.25 = (f32[5120]{0:T(1024)S(1)}, f32[5120]{0:T(1024)S(1)}, f32[5120]{0:T(1024)S(1)}, f32[5120]{0:T(1024)S(1)}) fusion(f32[1024,5120]{1,0:T(8,128)} %fusion.85, f32[5120]{0:T(1024)S(1)} %get-tuple-element.68, pred[1024]{0:T(1024)(128)(4,1)S(1)} %get-tuple-element.77, s32[5120]{0:T(1024)S(1)} %fusion.96, s32[1024]{0:T(1024)S(1)} %get-tuple-element.78, ...), kind=kLoop, calls=%fused_computation.39 | loop fusion | flops 188723200 | bytes 84090880 | tf_op jit(solution)/shard_map/reduce_sum | solution.py:97
  169.8 15.6 %fusion.59 = f32[5120,256]{1,0:T(8,128)S(1)} fusion(f32[1024,5120]{1,0:T(8,128)} %fusion.85, f32[5120]{0:T(1024)S(1)} %get-tuple-element.68, f32[5120]{0:T(1024)S(1)} %get-tuple-element.61, f32[5120]{0:T(1024)S(1)} %get-tuple-element.67, s32[5120]{0:T(1024)S(1)} %fusion.96, s32[1024]{0:T(1024)S(1)} %get-tuple-element.78, ...), kind=kOutput, calls=%fused_computation.57 | convolution fusion | flops 2734161920 | bytes 26825728 | tf_op jit(solution)/shard_map/pqk,pkd->pqd/dot_general | solution.py:98
  185.4 0.0 copy-start.3
  185.4 15.2 %fusion.56 = f32[5120,256]{1,0:T(8,128)S(1)} fusion(f32[5120,256]{1,0:T(8,128)S(1)} %fusion.59, f32[1024,5120]{1,0:T(8,128)} %fusion.84, f32[5120]{0:T(1024)S(1)} %get-tuple-element.64, f32[5120]{0:T(1024)S(1)} %get-tuple-element.60, s32[5120]{0:T(1024)S(1)} %fusion.96, s32[1024]{0:T(1024)S(1)} %get-tuple-element.79, ...), kind=kOutput, calls=%fused_computation.56 | convolution fusion | flops 2734161920 | bytes 32048128 | tf_op jit(solution)/shard_map/pqk,pkd->pqd/dot_general | solution.py:98
  200.6 0.0 copy-done.3
  200.6 0.0 copy-start.11
  200.6 15.0 %fusion.53 = f32[5120,256]{1,0:T(8,128)S(1)} fusion(f32[5120,256]{1,0:T(8,128)S(1)} %fusion.56, f32[1024,5120]{1,0:T(8,128)} %fusion.83, f32[5120]{0:T(1024)S(1)} %get-tuple-element.63, f32[5120]{0:T(1024)S(1)} %get-tuple-element.59, s32[5120]{0:T(1024)S(1)} %fusion.96, s32[1024]{0:T(1024)S(1)} %get-tuple-element.80, ...), kind=kOutput, calls=%fused_computation.55 | convolution fusion | flops 2734161920 | bytes 32048128 | tf_op jit(solution)/shard_map/pqk,pkd->pqd/dot_general | solution.py:98
  215.6 0.0 copy-done.11
  215.6 0.0 copy-start.8
  215.6 14.8 %divide_convert_fusion = bf16[5120,256]{1,0:T(8,128)(2,1)S(1)} fusion(f32[5120,256]{1,0:T(8,128)S(1)} %fusion.53, f32[1024,5120]{1,0:T(8,128)} %get-tuple-element.71, f32[5120]{0:T(1024)S(1)} %get-tuple-element.62, f32[5120]{0:T(1024)S(1)} %get-tuple-element.58, s32[5120]{0:T(1024)S(1)} %fusion.96, s32[1024]{0:T(1024)S(1)} %get-tuple-element.81, ...), kind=kOutput, calls=%fused_computation.61 | convolution fusion | flops 2735472640 | bytes 29426688 | tf_op jit(solution)/shard_map/pqk,pkd->pqd/dot_general | solution.py:98
  230.4 4.0 %reshape.528 = bf16[512,2560]{1,0:T(8,128)(2,1)} reshape(bf16[5120,256]{1,0:T(8,128)(2,1)S(1)} %divide_convert_fusion) | data formatting | bytes 5242880 | tf_op jit(solution)/shard_map/reshape | solution.py:117
  234.4 0.0 copy-done.8
  234.4 10.9 %fusion.66 = f32[513,2560]{1,0:T(8,128)S(1)} fusion(bf16[2560,2560]{1,0:T(8,128)(2,1)} %all-gather.5.cloned.1.call-done, bf16[1,2560]{1,0:T(2,128)(2,1)S(1)} %bitcast.174, bf16[512,2560]{1,0:T(8,128)(2,1)} %reshape.528), kind=kOutput, calls=%fused_computation.62 | convolution fusion | flops 6729246720 | bytes 20986880 | tf_op jit(solution)/shard_map/dot_general | solution.py:160
  245.3 0.0 copy-start
  245.3 2.3 copy-done
  247.6 0.0 copy-done.7
  247.6 0.6 multiply_reduce_fusion.2
  248.9 4.1 %fusion.63 = bf16[1,512,2560]{2,1,0:T(8,128)(2,1)S(1)} fusion(f32[513,2560]{1,0:T(8,128)} %copy-done, bf16[1,512,2560]{2,1,0:T(8,128)(2,1)} %param.19), kind=kLoop, calls=%fused_computation.60 | loop fusion | flops 3932160 | bytes 10485760 | tf_op jit(solution)/shard_map/convert_element_type | solution.py:168
  253.0 0.0 copy-start.1
  253.0 0.7 multiply_reduce_fusion.1
  254.5 0.0 copy-done.4
  254.6 40.5 %all-gather.2 = bf16[32,2,2560]{2,1,0:T(2,128)(2,1)S(1)} all-gather(bf16[1,2,2560]{2,1,0:T(2,128)(2,1)S(1)} %maximum_bitcast_fusion), channel_id=1, replica_groups=mesh['seq'=4,'vocab'=8] {'seq','vocab'}, dimensions={0}, use_global_device_ids=true | all-gather | bytes 337920 | tf_op jit(solution)/shard_map/all_gather | solution.py:175
  295.1 0.0 copy-done.5
  295.2 0.0 copy-done.1
  295.2 18.4 %fusion.129 = (f32[40]{0:T(128)S(1)}, f32[40,8000]{1,0:T(8,128)S(1)}) fusion(bf16[8000,2560]{1,0:T(8,128)(2,1)} %param.27, bf16[8,2560]{1,0:T(8,128)(2,1)S(1)} %slice_bitcast_fusion.18, bf16[32,2560]{1,0:T(8,128)(2,1)S(1)} %slice_bitcast_fusion.17), kind=kOutput, calls=%fused_computation.182 | convolution fusion | flops 1639129600 | bytes 42444960 | tf_op jit(solution)/shard_map/dot_general | solution.py:180
  313.6 0.4 exponential_reduce_fusion
  314.0 0.3 dynamic-update-slice
  314.3 0.3 dynamic-update-slice.1
  314.5 37.1 %all-reduce.2 = (f32[1280]{0:T(1024)S(1)}, f32[1280]{0:T(1024)S(1)}) all-reduce(f32[1280]{0:T(1024)S(1)} %dynamic-update-slice, f32[1280]{0:T(1024)S(1)} %dynamic-update-slice.1), channel_id=2, replica_groups=mesh['seq'=4,'vocab'=8] {'seq','vocab'}, use_global_device_ids=true, to_apply=%add | all-reduce | flops 2560 | bytes 20480
  351.6 0.1 slice.112
  351.7 0.1 slice.111
  351.7 0.1 reshape.545
  351.8 0.1 reshape.546
  351.9 1.2 while.12
  353.2 0.1 subtract_convert_fusion
  353.3 0.8 slice.113
  354.2 0.7 slice.114
  (71 shorter events, 1.2 us)
Async XLA Ops:
  7.2 13.3 %copy-start.6 = (bf16[1,2560]{1,0:T(2,128)(2,1)S(1)}, bf16[1,2560]{1,0:T(2,128)(2,1)}, u32[]{:S(2)}) copy-start(bf16[1,2560]{1,0:T(2,128)(2,1)} %param.20) | copy-start | bytes 15364
  7.2 13.4 %copy-start.9 = (bf16[1,512]{1,0:T(2,128)(2,1)S(1)}, bf16[1,512]{1,0:T(2,128)(2,1)}, u32[]{:S(2)}) copy-start(bf16[1,512]{1,0:T(2,128)(2,1)} %param.21) | copy-start | bytes 3076
  7.2 227.2 %all-gather.5.cloned.1.call-start = ((), (), s32[]{:S(2)}) async-start(), calls=%async_computation | async-start | bytes 14745600 | tf_op jit(solution)/shard_map/all_gather | solution.py:162
  11.0 27.4 %collective-permute-start = (bf16[1,1024,512]{2,1,0:T(8,128)(2,1)}, bf16[1,1024,512]{2,1,0:T(8,128)(2,1)}, u32[]{:S(2)}, u32[]{:S(2)}) collective-permute-start(bf16[1,1024,512]{2,1,0:T(8,128)(2,1)} %constant_dynamic-update-slice_fusion), channel_id=1, source_target_pairs={{0,8},{8,16},{16,24},{24,0},{1,9},{9,17},{17,25},{25,1},{2,10},{10... | collective-permute-start | bytes 3145736 | tf_op jit(solution)/shard_map/ppermute | solution.py:19
  38.3 25.5 %collective-permute-start.1 = (bf16[1,1024,512]{2,1,0:T(8,128)(2,1)}, bf16[1,1024,512]{2,1,0:T(8,128)(2,1)S(1)}, u32[]{:S(2)}, u32[]{:S(2)}) collective-permute-start(bf16[1,1024,512]{2,1,0:T(8,128)(2,1)} %collective-permute-done), channel_id=1, source_target_pairs={{0,8},{8,16},{16,24},{24,0},{1,9},{9,17},{17,25},{25,1},{2,10},{10... | collective-permute-start | bytes 3145736 | tf_op jit(solution)/shard_map/ppermute | solution.py:19
  63.8 8.8 %copy-start.2 = (bf16[1,1024,512]{2,1,0:T(8,128)(2,1)}, bf16[1,1024,512]{2,1,0:T(8,128)(2,1)S(1)}, u32[]{:S(2)}) copy-start(bf16[1,1024,512]{2,1,0:T(8,128)(2,1)S(1)} %collective-permute-done.1) | copy-start | bytes 3145732
  63.8 24.6 %collective-permute-start.2 = (bf16[1,1024,512]{2,1,0:T(8,128)(2,1)S(1)}, bf16[1,1024,512]{2,1,0:T(8,128)(2,1)S(1)}, u32[]{:S(2)}, u32[]{:S(2)}) collective-permute-start(bf16[1,1024,512]{2,1,0:T(8,128)(2,1)S(1)} %collective-permute-done.1), channel_id=1, source_target_pairs={{0,8},{8,16},{16,24},{24,0},{1,9},{9,17},{17,25},{25,1},{2,10},{10... | collective-permute-start | bytes 3145736 | tf_op jit(solution)/shard_map/ppermute | solution.py:19
  88.4 37.9 %copy-start.10 = (bf16[1,1024,512]{2,1,0:T(8,128)(2,1)}, bf16[1,1024,512]{2,1,0:T(8,128)(2,1)S(1)}, u32[]{:S(2)}) copy-start(bf16[1,1024,512]{2,1,0:T(8,128)(2,1)S(1)} %collective-permute-done.2) | copy-start | bytes 3145732
  185.4 15.2 %copy-start.3 = (bf16[1,1024,512]{2,1,0:T(8,128)(2,1)S(1)}, bf16[1,1024,512]{2,1,0:T(8,128)(2,1)}, u32[]{:S(2)}) copy-start(bf16[1,1024,512]{2,1,0:T(8,128)(2,1)} %copy-done.2) | copy-start | bytes 3145732
  200.6 15.0 %copy-start.11 = (bf16[1,1024,512]{2,1,0:T(8,128)(2,1)S(1)}, bf16[1,1024,512]{2,1,0:T(8,128)(2,1)}, u32[]{:S(2)}) copy-start(bf16[1,1024,512]{2,1,0:T(8,128)(2,1)} %copy-done.10) | copy-start | bytes 3145732
  215.6 18.8 %copy-start.8 = (bf16[1,1,10,256]{3,1,2,0:T(2,128)(2,1)S(1)}, bf16[1,1,10,256]{3,1,2,0:T(2,128)(2,1)}, u32[]{:S(2)}) copy-start(bf16[1,1,10,256]{3,1,2,0:T(2,128)(2,1)} %copy.20) | copy-start | bytes 15364
  234.4 13.2 %copy-start.7 = (bf16[1,2560]{1,0:T(2,128)(2,1)S(1)}, bf16[1,2560]{1,0:T(2,128)(2,1)}, u32[]{:S(2)}) copy-start(bf16[1,2560]{1,0:T(2,128)(2,1)} %param.24) | copy-start | bytes 15364
  245.3 2.3 copy-start
  247.6 6.9 %copy-start.4 = (f32[2560]{0:T(1024)S(1)}, f32[2560]{0:T(1024)}, u32[]{:S(2)}) copy-start(f32[2560]{0:T(1024)} %param.26) | copy-start | bytes 30724
  248.2 46.9 %copy-start.5 = (bf16[1,2560]{1,0:T(2,128)(2,1)}, bf16[1,2560]{1,0:T(2,128)(2,1)S(1)}, u32[]{:S(2)}) copy-start(bf16[1,2560]{1,0:T(2,128)(2,1)S(1)} %get-tuple-element.57) | copy-start | bytes 15364
  253.0 42.2 %copy-start.1 = (bf16[1,512,2560]{2,1,0:T(8,128)(2,1)}, bf16[1,512,2560]{2,1,0:T(8,128)(2,1)S(1)}, u32[]{:S(2)}) copy-start(bf16[1,512,2560]{2,1,0:T(8,128)(2,1)S(1)} %fusion.63) | copy-start | bytes 7864324
Sparse Core Ops, SparseCore 0:
  14.1 121.3 all-gather.4
where the time goes:
time: 368 us; the launch traced here: 362 us
  matrix products  160 us (43%)
  blocking collectives  77.6 us (21%)
  other arithmetic  50.8 us (14%)
  waiting for transfers between devices  34.1 us (9%)
  local copies, waits for them, and re-layouts  18.1 us (5%)
  between operations  17.8 us (5%)
  starting transfers between devices  3.92 us (1%)
    dot_general x4, matrix products, absorb(): jnp.einsum('pqd,pkd->pqk', query_rows, block[:, :, :HEAD_SIZE], preferred...  66.2 us
    dot_general x4, matrix products, absorb(): jnp.einsum('pqk,pkd->pqd', weights.astype(jnp.bfloat16), block[:, :, HEAD...  60.5 us
    reduce_sum x1, other arithmetic, absorb(): denom_sum = denom_sum * decay_rate + jnp.sum(weights, axis=2, keepdims=True)  43.5 us
    all_gather x1, blocking collectives, body(): everyone = lax.all_gather(local_head, ('seq', 'vocab'), axis=0, tiled=True)  40.5 us
    unnamed x1, blocking collectives  37.1 us
    ppermute x3, waiting for transfers between devices, from_behind(): return lax.ppermute(value, axis, pairs)  34.1 us
    dot_general x1, matrix products, body(): lax.dot_general(head_rows, embedding, (((1,), (1,)), ((), ())), preferred...  18.4 us
    dot_general x1, matrix products, body(): jnp.dot(mixed_rows, lax.all_gather(out_weight, 'vocab', axis=0, tiled=Tru...  10.9 us
  transfers between devices with their start and end apart: 4, of which 3 were waited for; matrix products, arithmetic and copies ran while one was open for 51% of the time, Pallas kernels for 0%

commit v1 on v0

v1 whole, which is shorter than its diff:
```python
import functools

import jax
import jax.numpy as jnp
from jax import lax
from jax.experimental import pallas as pl
from jax.experimental.pallas import tpu as pltpu
from jax.sharding import PartitionSpec as P

D = 2560
HQ = 10
HEAD_SIZE = 256
WIN = 2048


NEG_BIG = -1e30
STABILITY_FLOOR = 1e-06


def from_behind(value, axis, steps):
    count = lax.axis_size(axis)
    pairs = [(source, (source + steps) % count) for source in range(count)]
    return lax.ppermute(value, axis, pairs)


def gather_all(value):
    inner = lax.all_gather(value, "vocab", axis=0, tiled=True)
    return lax.all_gather(inner, "seq", axis=0, tiled=True)


def normalize(rows_in, gain):
    values = rows_in.astype(jnp.float32)
    square_mean = jnp.mean(values * values, axis=-1, keepdims=True)
    return (values * lax.rsqrt(square_mean + STABILITY_FLOOR) * gain).astype(jnp.bfloat16)


def prefill_kernel(t0_ref, q_ref, *refs, n_blocks, block, tq):
    kv_refs = refs[:n_blocks]
    o_ref = refs[n_blocks]
    r = pl.program_id(0)
    qi = pl.program_id(2)
    t0 = t0_ref[r]
    q = q_ref[0]
    row = qi * tq + lax.broadcasted_iota(jnp.int32, (tq, block), 0)
    col = lax.broadcasted_iota(jnp.int32, (tq, block), 1)
    peak = jnp.full((tq, 1), NEG_BIG, jnp.float32)
    denom = jnp.zeros((tq, 1), jnp.float32)
    accum = jnp.zeros((tq, HEAD_SIZE), jnp.float32)
    scale = HEAD_SIZE ** (-0.5)
    for j in range(n_blocks):
        kv = kv_refs[j]
        keys = kv[0, :, :HEAD_SIZE]
        values = kv[0, :, HEAD_SIZE:]
        scores = (
            lax.dot_general(
                q, keys, (((1,), (1,)), ((), ())), preferred_element_type=jnp.float32
            )
            * scale
        )
        t = j * block + col
        valid = t >= t0
        if j == 0:
            valid = valid & (t > row)
        if j == n_blocks - 1:
            valid = valid & (t <= row + WIN)
        peak_new = jnp.maximum(
            peak, jnp.max(jnp.where(valid, scores, NEG_BIG), axis=1, keepdims=True)
        )
        weights = jnp.where(valid, jnp.exp(scores - peak_new), 0.0)
        decay = jnp.exp(peak - peak_new)
        denom = denom * decay + jnp.sum(weights, axis=1, keepdims=True)
        accum = accum * decay + jnp.dot(
            weights.astype(jnp.bfloat16), values, preferred_element_type=jnp.float32
        )
        peak = peak_new
    o_ref[0] = (accum / denom).astype(o_ref.dtype)


def prefill_attention(pre_query, kv_blocks, first_key):
    local_pre, block_query, _ = pre_query.shape
    block = kv_blocks[0].shape[1]
    n_blocks = len(kv_blocks)
    tq = min(block_query, 512)
    kernel = functools.partial(prefill_kernel, n_blocks=n_blocks, block=block, tq=tq)
    kv_spec = pl.BlockSpec((1, block, 2 * HEAD_SIZE), lambda r, h, qi, t0: (r, 0, 0))
    q_spec = pl.BlockSpec((1, tq, HEAD_SIZE), lambda r, h, qi, t0: (r, qi, h))
    flops = 4 * local_pre * HQ * block_query * block * n_blocks * HEAD_SIZE
    return pl.pallas_call(
        kernel,
        out_shape=jax.ShapeDtypeStruct(pre_query.shape, jnp.bfloat16),
        grid_spec=pltpu.PrefetchScalarGridSpec(
            num_scalar_prefetch=1,
            grid=(local_pre, HQ, block_query // tq),
            in_specs=[q_spec] + [kv_spec] * n_blocks,
            out_specs=q_spec,
        ),
        compiler_params=pltpu.CompilerParams(
            dimension_semantics=("arbitrary", "arbitrary", "arbitrary")
        ),
        cost_estimate=pl.CostEstimate(
            flops=flops,
            transcendentals=local_pre * HQ * block_query * block * n_blocks,
            bytes_accessed=2 * pre_query.size * 2 + sum(b.size for b in kv_blocks) * 2,
        ),
    )(first_key, pre_query, *kv_blocks)


def body(
    pre_query,
    pre_fresh,
    pre_cache,
    pre_start,
    pre_resid,
    dec_query,
    dec_fresh,
    decode_window_cache,
    dec_length,
    dec_resid,
    out_weight,
    norm_gain,
    embedding,
):
    seq_count = lax.axis_size("seq")
    seq_index = lax.axis_index("seq")
    local_pre = pre_query.shape[0]
    block_query = pre_query.shape[1]
    score_scale = HEAD_SIZE ** (-0.5)
    kv_blocks = [None] * (seq_count + 1)
    kv_blocks[0] = pre_cache
    kv_blocks[seq_count] = pre_fresh
    for shift in range(1, seq_count):
        outgoing = jnp.where(seq_index + shift <= seq_count - 1, pre_fresh, pre_cache)
        kv_blocks[seq_count - shift] = from_behind(outgoing, "seq", shift)
    first_key = (WIN - seq_index * block_query - pre_start).astype(jnp.int32)
    pre_mixed = prefill_attention(pre_query, kv_blocks, first_key).reshape(
        local_pre * block_query, HQ * HEAD_SIZE
    )
    decode_token_rows = dec_query.reshape(-1, HQ, HEAD_SIZE)
    cache_scores = (
        jnp.einsum(
            "vfx,vzx->vfz",
            decode_token_rows,
            decode_window_cache[:, :, :HEAD_SIZE],
            preferred_element_type=jnp.float32,
        )
        * score_scale
    )
    self_scores = (
        jnp.einsum(
            "bhd,bd->bh",
            decode_token_rows,
            dec_fresh[:, :HEAD_SIZE],
            preferred_element_type=jnp.float32,
        )[:, :, None]
        * score_scale
    )
    slot_index = jnp.arange(WIN, dtype=jnp.int32)[None, :]
    length_col = dec_length[:, None]
    held_pos = length_col - 1 - jnp.mod(length_col - 1 - slot_index, WIN)
    live_mask = ((held_pos >= 0) & (held_pos > length_col - WIN))[:, None, :]
    peak_score = jnp.maximum(
        jnp.max(jnp.where(live_mask, cache_scores, NEG_BIG), axis=2, keepdims=True), self_scores
    )
    cache_attention_weights = jnp.where(live_mask, jnp.exp(cache_scores - peak_score), 0.0)
    self_weights = jnp.exp(self_scores - peak_score)
    denom_sum = jnp.sum(cache_attention_weights, axis=2, keepdims=True) + self_weights
    self_rounded = lax.optimization_barrier(self_weights.astype(jnp.bfloat16)).astype(jnp.float32)
    cache_part = jnp.einsum(
        "ect,ety->ecy",
        cache_attention_weights.astype(jnp.bfloat16),
        decode_window_cache[:, :, HEAD_SIZE:],
        preferred_element_type=jnp.float32,
    )
    self_part = self_rounded * dec_fresh[:, None, HEAD_SIZE:].astype(jnp.float32)
    dec_mixed = (
        ((cache_part + self_part) / denom_sum).astype(jnp.bfloat16).reshape(-1, HQ * HEAD_SIZE)
    )
    mixed_rows = jnp.concatenate([pre_mixed, dec_mixed], axis=0)
    projected = jnp.dot(
        mixed_rows,
        lax.all_gather(out_weight, "vocab", axis=0, tiled=True),
        preferred_element_type=jnp.float32,
    )
    pre_rows = local_pre * block_query
    pre_out = (
        pre_resid.astype(jnp.float32) + projected[:pre_rows].reshape(local_pre, block_query, D)
    ).astype(jnp.bfloat16)
    dec_out = (dec_resid.astype(jnp.float32) + projected[pre_rows:]).astype(jnp.bfloat16)
    head_decode = normalize(dec_out, norm_gain)
    head_prefill = normalize(pre_out[:, block_query - 1, :], norm_gain)
    local_dec = head_decode.shape[0]
    vocab_count = lax.axis_size("vocab")
    local_head = jnp.concatenate([head_decode, head_prefill], axis=0)
    everyone = gather_all(local_head)
    layout = everyone.reshape(seq_count, vocab_count, local_dec + local_pre, D)
    decode_all = layout[:, :, :local_dec].reshape(-1, D)
    prefill_every_request = layout[seq_count - 1, :, local_dec:].reshape(-1, D)
    head_rows = jnp.concatenate([decode_all, prefill_every_request], axis=0)
    logits = lax.dot_general(
        head_rows, embedding, (((1,), (1,)), ((), ())), preferred_element_type=jnp.float32
    )
    local_peak = jnp.max(logits, axis=1)
    local_sum = jnp.sum(jnp.exp(logits - local_peak[:, None]), axis=1)
    stats = gather_all(jnp.stack([local_peak, local_sum])[None])
    global_peak = jnp.max(stats[:, 0], axis=0)
    global_sum = jnp.sum(stats[:, 1] * jnp.exp(stats[:, 0] - global_peak[None]), axis=0)
    total = (global_peak + jnp.log(global_sum))[:, None]
    log_probs = (logits - total).astype(jnp.bfloat16)
    dec_count = decode_all.shape[0]
    return (pre_out, dec_out, log_probs[:dec_count], log_probs[dec_count:])


def solution(mesh):
    in_specs = (
        P("vocab", "seq", None),
        P("vocab", "seq", None),
        P("vocab", "seq", None),
        P("vocab"),
        P("vocab", "seq", None),
        P(("seq", "vocab"), None),
        P(("seq", "vocab"), None),
        P(("seq", "vocab"), None, None),
        P(("seq", "vocab")),
        P(("seq", "vocab"), None),
        P("vocab", None),
        P(),
        P(("seq", "vocab"), None),
    )
    out_specs = (
        P("vocab", "seq", None),
        P(("seq", "vocab"), None),
        P(None, ("seq", "vocab")),
        P(None, ("seq", "vocab")),
    )
    return jax.shard_map(body, mesh=mesh, in_specs=in_specs, out_specs=out_specs, check_vma=False)
```

time: 368 us -> 222 us (0.60); the launches traced: 362 us -> 221 us
  matrix products: 160 us -> 29.9 us
  waiting for transfers between devices: 34.1 us -> 85.9 us
  other arithmetic: 50.8 us -> 8.53 us
  blocking collectives: 77.6 us -> 40.3 us
  Pallas kernels: 0 us -> 29.6 us
  local copies, waits for them, and re-layouts: 18.1 us -> 4.17 us
    dot_general x8 -> x0, matrix products: 127 us -> none  [the longest x4 66.2 us: absorb(): jnp.einsum('pqd,pkd->pqk', query_rows, block[:, :, :HEAD_SIZE], preferred...]
    all_gather x1, waiting for transfers between devices: 0.01 us -> 66.1 us  [body(): lax.all_gather(out_weight, 'vocab', axis=0, tiled=True)]
    reduce_sum x2, other arithmetic: 43.9 us -> 0.42 us  [the longest x1 0.39 us: body(): local_sum = jnp.sum(jnp.exp(logits - local_peak[:, None]), axis=1)]
    unnamed x1 -> x0, blocking collectives: 37.1 us -> none
    pallas_call x0 -> x1, Pallas kernels: none -> 29.6 us  [prefill_attention(): pl.pallas_call(kernel, out_shape=jax.ShapeDtypeStruct(pre_query.shape, jn...]
    ppermute x3, waiting for transfers between devices: 34.1 us -> 19.2 us  [from_behind(): return lax.ppermute(value, axis, pairs)]
    another operation x3 -> x1, local copies, waits for them, and re-layouts: 5 us -> 0.01 us
    reshape x2 -> x1, local copies, waits for them, and re-layouts: 3.97 us -> 0.12 us  [body(): layout = everyone.reshape(seq_count, vocab_count, local_dec + local_pre, D)]
  transfers between devices with their start and end apart: 4 -> 4, of which waited for: 3 -> 4; matrix products, arithmetic and copies ran while one was open for 51% -> 2% of each run, Pallas kernels for 0% -> 13%
where the time goes in v1:
time: 222 us; the launch traced here: 221 us
  waiting for transfers between devices  85.9 us (39%)
  blocking collectives  40.3 us (18%)
  matrix products  29.9 us (13%)
  Pallas kernels  29.6 us (13%)
  between operations  17 us (8%)
  other arithmetic  8.53 us (4%)
  starting transfers between devices  5.93 us (3%)
  local copies, waits for them, and re-layouts  4.17 us (2%)
    all_gather x1, waiting for transfers between devices, body(): lax.all_gather(out_weight, 'vocab', axis=0, tiled=True)  66.1 us
    pallas_call x1, Pallas kernels, prefill_attention(): pl.pallas_call(kernel, out_shape=jax.ShapeDtypeStruct(pre_query.shape, jn...  29.6 us
    all_gather x2, blocking collectives, gather_all(): inner = lax.all_gather(value, 'vocab', axis=0, tiled=True)  22.9 us
    ppermute x3, waiting for transfers between devices, from_behind(): return lax.ppermute(value, axis, pairs)  19.2 us
    dot_general x1, matrix products, body(): lax.dot_general(head_rows, embedding, (((1,), (1,)), ((), ())), preferred...  18.1 us
    all_gather x2, blocking collectives, gather_all(): return lax.all_gather(inner, 'seq', axis=0, tiled=True)  17.3 us
    dot_general x1, matrix products, body(): jnp.dot(mixed_rows, lax.all_gather(out_weight, 'vocab', axis=0, tiled=Tru...  10.9 us
    ppermute x3, starting transfers between devices, from_behind(): return lax.ppermute(value, axis, pairs)  5.89 us
  transfers between devices with their start and end apart: 4, of which 4 were waited for; matrix products, arithmetic and copies ran while one was open for 2% of the time, Pallas kernels for 13%

profile of v1, /device:TPU:0, one launch (start us, length us, event | category | flops | bytes accessed | tf_op | source)
XLA Modules:
  0.0 221.3 jit_solution(5852955184422381987)
XLA Ops:
  7.2 0.0 copy-start.5
  7.2 0.0 copy-start.7
  7.2 0.0 copy-start.2
  7.2 0.0 all-gather.5.cloned.1.call-start
  7.2 0.7 all-gather.5.cloned.1.call-update
  7.9 2.1 broadcast_select_fusion
  10.0 2.9 %collective-permute-start.2 = (bf16[1,512,512]{2,1,0:T(8,128)(2,1)}, bf16[1,512,512]{2,1,0:T(8,128)(2,1)}, u32[]{:S(2)}, u32[]{:S(2)}) collective-permute-start(bf16[1,512,512]{2,1,0:T(8,128)(2,1)} %get-tuple-element.8), channel_id=1, source_target_pairs={{0,8},{8,16},{16,24},{24,0},{1,9},{9,17},{17,25},{25,1},{2,10},{10... | collective-permute-start | bytes 1572872 | tf_op jit(solution)/shard_map/ppermute | solution.py:23
  13.0 1.5 collective-permute-start.1
  14.5 1.4 collective-permute-start
  16.6 0.0 copy-done.5
  16.7 0.0 copy-done.7
  16.7 0.1 fusion.9
  16.8 0.0 copy-done.2
  16.8 0.5 select_reduce_fusion
  18.0 0.2 fusion.18
  18.2 0.3 fusion.8
  18.5 8.5 %collective-permute-done.2.refs_3_ = bf16[1,512,512]{2,1,0:T(8,128)(2,1)} collective-permute-done((bf16[1,512,512]{2,1,0:T(8,128)(2,1)}, bf16[1,512,512]{2,1,0:T(8,128)(2,1)}, u32[]{:S(2)}, u32[]{:S(2)}) %collective-permute-start.2) | collective-permute-done | bytes 524320 | tf_op jit(solution)/shard_map/ppermute | solution.py:23
  27.0 10.4 %collective-permute-done.1.refs_2_ = bf16[1,512,512]{2,1,0:T(8,128)(2,1)} collective-permute-done((bf16[1,512,512]{2,1,0:T(8,128)(2,1)S(1)}, bf16[1,512,512]{2,1,0:T(8,128)(2,1)}, u32[]{:S(2)}, u32[]{:S(2)}) %collective-permute-start.1) | collective-permute-done | bytes 524320 | tf_op jit(solution)/shard_map/ppermute | solution.py:23
  37.4 0.3 collective-permute-done.refs_1_
  37.7 29.6 %shard_map.156 = bf16[1,512,2560]{2,1,0:T(8,128)(2,1)} custom-call(s32[1]{0:T(128)S(6)} %sub.83.t0_ref, bf16[1,512,2560]{2,1,0:T(8,128)(2,1)} %q_ref.1, bf16[1,512,512]{2,1,0:T(8,128)(2,1)} %refs_0_.1, bf16[1,512,512]{2,1,0:T(8,128)(2,1)} %collective-permute-done.refs_1_, bf16[1,512,512]{2,1,0:T(8,128)(2,1)} %collective-permute-done.1.refs_2_, ...), custom_call_target="tpu_custom_call" | custom-call | flops 13421772800 | bytes 7864320 | tf_op jit(solution)/shard_map/pallas_call | solution.py:88
  67.3 66.1 %all-gather.5.cloned.1.call-done = bf16[2560,2560]{1,0:T(8,128)(2,1)} async-done(((bf16[320,2560]{1,0:T(8,128)(2,1)}), bf16[2560,2560]{1,0:T(8,128)(2,1)}) %all-gather.5.cloned.1.call-update) | async-done | bytes 13107216 | tf_op jit(solution)/shard_map/all_gather | solution.py:181
  133.4 0.0 copy-start.6
  133.4 10.9 %fusion.2 = f32[513,2560]{1,0:T(8,128)S(1)} fusion(bf16[2560,2560]{1,0:T(8,128)(2,1)} %all-gather.5.cloned.1.call-done, bf16[1,2560]{1,0:T(2,128)(2,1)S(1)} %bitcast.62, bf16[512,2560]{1,0:T(8,128)(2,1)} %bitcast.66), kind=kOutput, calls=%fused_computation.3 | convolution fusion | flops 6729246720 | bytes 20986880 | tf_op jit(solution)/shard_map/dot_general | solution.py:179
  144.3 0.0 copy-start
  144.4 2.3 %copy-done = f32[513,2560]{1,0:T(8,128)} copy-done((f32[513,2560]{1,0:T(8,128)}, f32[513,2560]{1,0:T(8,128)S(1)}, u32[]{:S(2)}) %copy-start) | copy-done | bytes 5253144
  146.7 0.0 copy-done.6
  146.7 0.6 multiply_reduce_fusion.3
  147.3 0.0 copy-start.4
  148.0 0.0 copy-start.3
  148.0 4.1 %fusion.1 = bf16[1,512,2560]{2,1,0:T(8,128)(2,1)S(1)} fusion(f32[513,2560]{1,0:T(8,128)} %copy-done, bf16[1,512,2560]{2,1,0:T(8,128)(2,1)} %param.17), kind=kLoop, calls=%fused_computation.2 | loop fusion | flops 3932160 | bytes 10485760 | tf_op jit(solution)/shard_map/convert_element_type | solution.py:187
  152.1 0.0 copy-start.1
  152.1 0.7 multiply_reduce_fusion.2
  153.6 0.0 copy-done.3
  153.6 0.0 copy-done.4
  153.7 14.0 %all-gather.1 = bf16[8,2,2560]{2,1,0:T(2,128)(2,1)S(1)} all-gather(bf16[1,2,2560]{2,1,0:T(2,128)(2,1)S(1)} %maximum_bitcast_fusion), channel_id=1, replica_groups=mesh['seq'=4,'vocab'=8] {'vocab'}, dimensions={0}, use_global_device_ids=true | all-gather | bytes 92160 | tf_op jit(solution)/shard_map/all_gather | solution.py:27
  167.7 9.2 %all_gather.17 = bf16[64,2560]{1,0:T(8,128)(2,1)S(1)} all-gather(bf16[16,2560]{1,0:T(8,128)(2,1)S(1)} %reshape.196), channel_id=1, replica_groups=mesh['seq'=4,'vocab'=8] {'seq'}, dimensions={0}, use_global_device_ids=true | all-gather | bytes 409600 | tf_op jit(solution)/shard_map/all_gather | solution.py:28
  176.9 0.1 reshape.190
  177.1 0.1 slice.57
  177.2 0.0 copy-done.1
  177.2 18.1 %fusion.38 = (f32[40]{0:T(128)S(1)}, f32[40,8000]{1,0:T(8,128)S(1)}) fusion(bf16[8000,2560]{1,0:T(8,128)(2,1)} %param.25, bf16[8,2560]{1,0:T(8,128)(2,1)S(1)} %bitcast.58, bf16[32,2560]{1,0:T(8,128)(2,1)S(1)} %bitcast.57), kind=kOutput, calls=%fused_computation.68 | convolution fusion | flops 1639129600 | bytes 42444960 | tf_op jit(solution)/shard_map/dot_general | solution.py:199
  195.3 0.4 exponential_reduce_fusion
  195.7 9.0 %all-gather.2 = f32[8,2,40]{2,1,0:T(2,128)S(1)} all-gather(f32[1,2,40]{2,1,0:T(2,128)S(1)} %maximum_bitcast_fusion.1), channel_id=2, replica_groups=mesh['seq'=4,'vocab'=8] {'vocab'}, dimensions={0}, use_global_device_ids=true | all-gather | bytes 2880 | tf_op jit(solution)/shard_map/all_gather | solution.py:27
  204.6 8.1 %all_gather.19 = f32[32,2,40]{2,1,0:T(2,128)S(1)} all-gather(f32[8,2,40]{2,1,0:T(2,128)S(1)} %all-gather.2), channel_id=1, replica_groups=mesh['seq'=4,'vocab'=8] {'seq'}, dimensions={0}, use_global_device_ids=true | all-gather | bytes 12800 | tf_op jit(solution)/shard_map/all_gather | solution.py:28
  212.8 0.1 subtract_convert_fusion
  213.0 0.7 slice.61
  213.7 0.8 slice.60
  (21 shorter events, 0.4 us)
Async XLA Ops:
  7.2 9.4 %copy-start.5 = (bf16[1,2560]{1,0:T(2,128)(2,1)S(1)}, bf16[1,2560]{1,0:T(2,128)(2,1)}, u32[]{:S(2)}) copy-start(bf16[1,2560]{1,0:T(2,128)(2,1)} %param.18) | copy-start | bytes 15364
  7.2 9.5 %copy-start.7 = (bf16[1,512]{1,0:T(2,128)(2,1)S(1)}, bf16[1,512]{1,0:T(2,128)(2,1)}, u32[]{:S(2)}) copy-start(bf16[1,512]{1,0:T(2,128)(2,1)} %param.19) | copy-start | bytes 3076
  7.2 9.6 %copy-start.2 = (bf16[1,2048,512]{2,1,0:T(8,128)(2,1)S(1)}, bf16[1,2048,512]{2,1,0:T(8,128)(2,1)}, u32[]{:S(2)}) copy-start(bf16[1,2048,512]{2,1,0:T(8,128)(2,1)} %param.20) | copy-start | bytes 6291460
  7.2 126.2 %all-gather.5.cloned.1.call-start = ((), (), s32[]{:S(2)}) async-start(), calls=%async_computation | async-start | bytes 14745600 | tf_op jit(solution)/shard_map/all_gather | solution.py:181
  10.0 17.0 %collective-permute-start.2 = (bf16[1,512,512]{2,1,0:T(8,128)(2,1)}, bf16[1,512,512]{2,1,0:T(8,128)(2,1)}, u32[]{:S(2)}, u32[]{:S(2)}) collective-permute-start(bf16[1,512,512]{2,1,0:T(8,128)(2,1)} %get-tuple-element.8), channel_id=1, source_target_pairs={{0,8},{8,16},{16,24},{24,0},{1,9},{9,17},{17,25},{25,1},{2,10},{10... | collective-permute-start | bytes 1572872 | tf_op jit(solution)/shard_map/ppermute | solution.py:23
  13.0 24.4 %collective-permute-start.1 = (bf16[1,512,512]{2,1,0:T(8,128)(2,1)S(1)}, bf16[1,512,512]{2,1,0:T(8,128)(2,1)}, u32[]{:S(2)}, u32[]{:S(2)}) collective-permute-start(bf16[1,512,512]{2,1,0:T(8,128)(2,1)S(1)} %get-tuple-element.9), channel_id=1, source_target_pairs={{0,16},{8,24},{16,0},{24,8},{1,17},{9,25},{17,1},{25,9},{2,18},{10... | collective-permute-start | bytes 1572872 | tf_op jit(solution)/shard_map/ppermute | solution.py:23
  14.5 23.2 %collective-permute-start = (bf16[1,512,512]{2,1,0:T(8,128)(2,1)S(1)}, bf16[1,512,512]{2,1,0:T(8,128)(2,1)}, u32[]{:S(2)}, u32[]{:S(2)}) collective-permute-start(bf16[1,512,512]{2,1,0:T(8,128)(2,1)S(1)} %get-tuple-element.10), channel_id=1, source_target_pairs={{0,24},{8,0},{16,8},{24,16},{1,25},{9,1},{17,9},{25,17},{2,26},{10... | collective-permute-start | bytes 1572872 | tf_op jit(solution)/shard_map/ppermute | solution.py:23
  133.4 13.2 %copy-start.6 = (bf16[1,2560]{1,0:T(2,128)(2,1)S(1)}, bf16[1,2560]{1,0:T(2,128)(2,1)}, u32[]{:S(2)}) copy-start(bf16[1,2560]{1,0:T(2,128)(2,1)} %param.22) | copy-start | bytes 15364
  144.3 2.3 %copy-start = (f32[513,2560]{1,0:T(8,128)}, f32[513,2560]{1,0:T(8,128)S(1)}, u32[]{:S(2)}) copy-start(f32[513,2560]{1,0:T(8,128)S(1)} %fusion.2) | copy-start | bytes 15759364
  147.3 6.3 %copy-start.4 = (bf16[1,2560]{1,0:T(2,128)(2,1)}, bf16[1,2560]{1,0:T(2,128)(2,1)S(1)}, u32[]{:S(2)}) copy-start(bf16[1,2560]{1,0:T(2,128)(2,1)S(1)} %get-tuple-element.5) | copy-start | bytes 15364
  148.0 5.6 %copy-start.3 = (f32[2560]{0:T(1024)S(1)}, f32[2560]{0:T(1024)}, u32[]{:S(2)}) copy-start(f32[2560]{0:T(1024)} %param.24) | copy-start | bytes 30724
  152.1 25.1 %copy-start.1 = (bf16[1,512,2560]{2,1,0:T(8,128)(2,1)}, bf16[1,512,2560]{2,1,0:T(8,128)(2,1)S(1)}, u32[]{:S(2)}) copy-start(bf16[1,512,2560]{2,1,0:T(8,128)(2,1)S(1)} %fusion.1) | copy-start | bytes 7864324
Sparse Core Ops, SparseCore 0:
  9.7 123.7 all-gather.4

commit v2 on v1

--- a/solution.py
+++ b/solution.py
@@ -132,9 +132,8 @@
         outgoing = jnp.where(seq_index + shift <= seq_count - 1, pre_fresh, pre_cache)
         kv_blocks[seq_count - shift] = from_behind(outgoing, "seq", shift)
     first_key = (WIN - seq_index * block_query - pre_start).astype(jnp.int32)
-    pre_mixed = prefill_attention(pre_query, kv_blocks, first_key).reshape(
-        local_pre * block_query, HQ * HEAD_SIZE
-    )
+    pre_mixed_3d = prefill_attention(pre_query, kv_blocks, first_key)
+    pre_mixed = pre_mixed_3d.reshape(local_pre * block_query, HQ * HEAD_SIZE)
     decode_token_rows = dec_query.reshape(-1, HQ, HEAD_SIZE)
     cache_scores = (
         jnp.einsum(
@@ -186,12 +185,22 @@
         pre_resid.astype(jnp.float32) + projected[:pre_rows].reshape(local_pre, block_query, D)
     ).astype(jnp.bfloat16)
     dec_out = (dec_resid.astype(jnp.float32) + projected[pre_rows:]).astype(jnp.bfloat16)
-    head_decode = normalize(dec_out, norm_gain)
-    head_prefill = normalize(pre_out[:, block_query - 1, :], norm_gain)
-    local_dec = head_decode.shape[0]
+    local_dec = dec_mixed.shape[0]
     vocab_count = lax.axis_size("vocab")
-    local_head = jnp.concatenate([head_decode, head_prefill], axis=0)
-    everyone = gather_all(local_head)
+    vocab_index = lax.axis_index("vocab")
+    weight_rows = out_weight.shape[0]
+    head_mixed = jnp.concatenate([dec_mixed, pre_mixed_3d[:, block_query - 1, :]], axis=0)
+    head_resid = jnp.concatenate([dec_resid, pre_resid[:, block_query - 1, :]], axis=0)
+    group_rows = lax.all_gather(
+        jnp.concatenate([head_mixed, head_resid], axis=1), "vocab", axis=0, tiled=True
+    )
+    own_columns = lax.dynamic_slice_in_dim(
+        group_rows, vocab_index * weight_rows, weight_rows, axis=1
+    )
+    partial = jnp.dot(own_columns, out_weight, preferred_element_type=jnp.float32)
+    head_proj = lax.psum(partial, "vocab")
+    head_in = (group_rows[:, D:].astype(jnp.float32) + head_proj).astype(jnp.bfloat16)
+    everyone = lax.all_gather(normalize(head_in, norm_gain), "seq", axis=0, tiled=True)
     layout = everyone.reshape(seq_count, vocab_count, local_dec + local_pre, D)
     decode_all = layout[:, :, :local_dec].reshape(-1, D)
     prefill_every_request = layout[seq_count - 1, :, local_dec:].reshape(-1, D)

time: 222 us -> 281 us (1.27)
  waiting for transfers between devices: 85.9 us -> 140 us
  blocking collectives: 40.3 us -> 46.3 us
    psum x0 -> x1, waiting for transfers between devices: none -> 50.7 us  [body(): head_proj = lax.psum(partial, 'vocab')]
    all_gather x0 -> x2, blocking collectives: none -> 23.5 us  [the longest x1 14.3 us: body(): lax.all_gather(jnp.concatenate([head_mixed, head_resid], axis=1), 'vocab'...]
    all_gather x2 -> x1, blocking collectives: 17.3 us -> 8.19 us  [gather_all(): return lax.all_gather(inner, 'seq', axis=0, tiled=True)]
    all_gather x2 -> x1, blocking collectives: 22.9 us -> 14.7 us  [gather_all(): inner = lax.all_gather(value, 'vocab', axis=0, tiled=True)]
  transfers between devices with their start and end apart: 4 -> 5, of which waited for: 4 -> 4; matrix products, arithmetic and copies ran while one was open for 2% -> 9% of each run, Pallas kernels for 13% -> 0%
where the time goes in v2:
time: 281 us
  waiting for transfers between devices  140 us (50%)
  blocking collectives  46.3 us (16%)
  matrix products  32.4 us (12%)
  Pallas kernels  29.6 us (11%)
  between operations  15.6 us (6%)
  other arithmetic  8.13 us (3%)
  starting transfers between devices  5.07 us (2%)
  local copies, waits for them, and re-layouts  3.47 us (1%)
    all_gather x1, waiting for transfers between devices, body(): lax.all_gather(out_weight, 'vocab', axis=0, tiled=True)  68.4 us
    psum x1, waiting for transfers between devices, body(): head_proj = lax.psum(partial, 'vocab')  50.7 us
    pallas_call x1, Pallas kernels, prefill_attention(): pl.pallas_call(kernel, out_shape=jax.ShapeDtypeStruct(pre_query.shape, jn...  29.6 us
    ppermute x3, waiting for transfers between devices, from_behind(): return lax.ppermute(value, axis, pairs)  20.2 us
    dot_general x1, matrix products, body(): lax.dot_general(head_rows, embedding, (((1,), (1,)), ((), ())), preferred...  19.4 us
    all_gather x1, blocking collectives, gather_all(): inner = lax.all_gather(value, 'vocab', axis=0, tiled=True)  14.7 us
    all_gather x1, blocking collectives, body(): lax.all_gather(jnp.concatenate([head_mixed, head_resid], axis=1), 'vocab'...  14.3 us
    dot_general x1, matrix products, body(): jnp.dot(mixed_rows, lax.all_gather(out_weight, 'vocab', axis=0, tiled=Tru...  11 us
  transfers between devices with their start and end apart: 5, of which 4 were waited for; matrix products, arithmetic and copies ran while one was open for 9% of the time, Pallas kernels for 0%

profile of v2, /device:TPU:0, one launch (start us, length us, event | category | flops | bytes accessed | tf_op | source)
XLA Modules:
  0.0 280.5 jit_solution(9415764951159991421)
XLA Ops:
  7.2 0.0 copy-start.5
  7.2 0.0 copy-start.6
  7.2 0.0 copy-start.2
  7.2 0.0 all-reduce.2.cloned.1.call-start
  7.3 2.2 broadcast_select_fusion
  9.5 3.9 %collective-permute-start = (bf16[1,512,512]{2,1,0:T(8,128)(2,1)}, bf16[1,512,512]{2,1,0:T(8,128)(2,1)}, u32[]{:S(2)}, u32[]{:S(2)}) collective-permute-start(bf16[1,512,512]{2,1,0:T(8,128)(2,1)} %get-tuple-element.8), channel_id=1, source_target_pairs={{0,24},{8,0},{16,8},{24,16},{1,25},{9,1},{17,9},{25,17},{2,26},{10... | collective-permute-start | bytes 1572872 | tf_op jit(solution)/shard_map/ppermute | solution.py:23
  13.4 0.5 collective-permute-start.1
  13.9 0.6 collective-permute-start.2
  15.1 0.0 copy-done.5
  15.2 0.0 copy-done.6
  15.2 0.1 fusion.9
  15.4 0.0 copy-done.2
  15.4 0.5 select_reduce_fusion
  15.9 0.2 fusion.21
  16.1 0.3 fusion.8
  17.1 0.8 slice_bitcast_fusion.2
  17.9 0.0 copy-start.3
  17.9 0.0 copy-start
  17.9 8.1 %collective-permute-done.refs_1_ = bf16[1,512,512]{2,1,0:T(8,128)(2,1)} collective-permute-done((bf16[1,512,512]{2,1,0:T(8,128)(2,1)}, bf16[1,512,512]{2,1,0:T(8,128)(2,1)}, u32[]{:S(2)}, u32[]{:S(2)}) %collective-permute-start) | collective-permute-done | bytes 524320 | tf_op jit(solution)/shard_map/ppermute | solution.py:23
  26.0 12.1 %collective-permute-done.1.refs_2_ = bf16[1,512,512]{2,1,0:T(8,128)(2,1)} collective-permute-done((bf16[1,512,512]{2,1,0:T(8,128)(2,1)S(1)}, bf16[1,512,512]{2,1,0:T(8,128)(2,1)}, u32[]{:S(2)}, u32[]{:S(2)}) %collective-permute-start.1) | collective-permute-done | bytes 524320 | tf_op jit(solution)/shard_map/ppermute | solution.py:23
  38.1 0.0 collective-permute-done.2.refs_3_
  38.1 29.6 %shard_map.156 = bf16[1,512,2560]{2,1,0:T(8,128)(2,1)} custom-call(s32[1]{0:T(128)S(6)} %sub.83.t0_ref, bf16[1,512,2560]{2,1,0:T(8,128)(2,1)} %q_ref.1, bf16[1,512,512]{2,1,0:T(8,128)(2,1)} %refs_0_.1, bf16[1,512,512]{2,1,0:T(8,128)(2,1)} %collective-permute-done.refs_1_, bf16[1,512,512]{2,1,0:T(8,128)(2,1)} %collective-permute-done.1.refs_2_, ...), custom_call_target="tpu_custom_call" | custom-call | flops 13421772800 | bytes 7864320 | tf_op jit(solution)/shard_map/pallas_call | solution.py:88
  67.7 0.0 copy-start.4
  67.7 0.8 slice_bitcast_fusion.1
  68.5 0.0 copy-done.3
  68.5 0.1 maximum_bitcast_fusion
  68.5 14.3 %all-gather.1 = bf16[8,2,5120]{2,1,0:T(2,128)(2,1)S(1)} all-gather(bf16[1,2,5120]{2,1,0:T(2,128)(2,1)S(1)} %maximum_bitcast_fusion), channel_id=1, replica_groups=mesh['seq'=4,'vocab'=8] {'vocab'}, dimensions={0}, use_global_device_ids=true | all-gather | bytes 184320 | tf_op jit(solution)/shard_map/all_gather | solution.py:194
  82.8 0.1 reshape.161
  82.9 0.0 copy-done
  82.9 1.1 fusion.27
  84.0 0.0 all-reduce.2.cloned.1.call-update
  84.0 0.0 all-gather.5.cloned.1.call-start
  84.0 0.7 all-gather.5.cloned.1.call-update
  84.7 50.7 %all-reduce.2.cloned.1.call-done = f32[16,2560]{1,0:T(8,128)} async-done(((f32[16,2560]{1,0:T(8,128)}), f32[16,2560]{1,0:T(8,128)}) %all-reduce.2.cloned.1.call-update) | async-done | bytes 163856 | tf_op jit(solution)/shard_map/psum | solution.py:201
  135.4 1.1 fusion.18
  136.5 0.0 copy-done.4
  136.5 1.0 fusion.20
  137.5 9.2 %all_gather.17 = bf16[64,2560]{1,0:T(8,128)(2,1)S(1)} all-gather(bf16[16,2560]{1,0:T(8,128)(2,1)S(1)} %fusion.20), channel_id=1, replica_groups=mesh['seq'=4,'vocab'=8] {'seq'}, dimensions={0}, use_global_device_ids=true | all-gather | bytes 409600 | tf_op jit(solution)/shard_map/all_gather | solution.py:203
  146.7 0.1 reshape.155
  146.8 0.1 slice.66
  147.0 19.4 %fusion.43 = (f32[40]{0:T(128)S(1)}, f32[40,8000]{1,0:T(8,128)S(1)}) fusion(bf16[8000,2560]{1,0:T(8,128)(2,1)} %param.25, bf16[8,2560]{1,0:T(8,128)(2,1)S(1)} %bitcast.63, bf16[32,2560]{1,0:T(8,128)(2,1)S(1)} %bitcast.62), kind=kOutput, calls=%fused_computation.74 | convolution fusion | flops 1639129600 | bytes 42444960 | tf_op jit(solution)/shard_map/dot_general | solution.py:208
  166.4 0.4 exponential_reduce_fusion
  166.8 14.7 %all-gather.2 = f32[8,2,40]{2,1,0:T(2,128)S(1)} all-gather(f32[1,2,40]{2,1,0:T(2,128)S(1)} %maximum_bitcast_fusion.1), channel_id=2, replica_groups=mesh['seq'=4,'vocab'=8] {'vocab'}, dimensions={0}, use_global_device_ids=true | all-gather | bytes 2880 | tf_op jit(solution)/shard_map/all_gather | solution.py:27
  181.5 8.2 %all_gather.19 = f32[32,2,40]{2,1,0:T(2,128)S(1)} all-gather(f32[8,2,40]{2,1,0:T(2,128)S(1)} %all-gather.2), channel_id=1, replica_groups=mesh['seq'=4,'vocab'=8] {'seq'}, dimensions={0}, use_global_device_ids=true | all-gather | bytes 12800 | tf_op jit(solution)/shard_map/all_gather | solution.py:28
  189.8 0.1 subtract_convert_fusion
  189.9 0.8 slice.69
  190.8 0.7 slice.70
  191.4 68.4 %all-gather.5.cloned.1.call-done = bf16[2560,2560]{1,0:T(8,128)(2,1)} async-done(((bf16[320,2560]{1,0:T(8,128)(2,1)}), bf16[2560,2560]{1,0:T(8,128)(2,1)}) %all-gather.5.cloned.1.call-update) | async-done | bytes 13107216 | tf_op jit(solution)/shard_map/all_gather | solution.py:180
  259.8 0.0 copy-start.1
  259.8 11.0 %fusion.2 = f32[513,2560]{1,0:T(8,128)S(1)} fusion(bf16[2560,2560]{1,0:T(8,128)(2,1)} %all-gather.5.cloned.1.call-done, bf16[1,2560]{1,0:T(2,128)(2,1)S(1)} %bitcast.68, bf16[512,2560]{1,0:T(8,128)(2,1)} %bitcast.72), kind=kOutput, calls=%fused_computation.3 | convolution fusion | flops 6729246720 | bytes 20986880 | tf_op jit(solution)/shard_map/dot_general | solution.py:178
  270.8 0.0 copy-done.1
  270.8 2.3 fusion.1
  273.1 0.6 fusion.29
  (16 shorter events, 0.3 us)
Async XLA Ops:
  7.2 8.0 %copy-start.5 = (bf16[1,2560]{1,0:T(2,128)(2,1)S(1)}, bf16[1,2560]{1,0:T(2,128)(2,1)}, u32[]{:S(2)}) copy-start(bf16[1,2560]{1,0:T(2,128)(2,1)} %param.18) | copy-start | bytes 15364
  7.2 8.0 %copy-start.6 = (bf16[1,512]{1,0:T(2,128)(2,1)S(1)}, bf16[1,512]{1,0:T(2,128)(2,1)}, u32[]{:S(2)}) copy-start(bf16[1,512]{1,0:T(2,128)(2,1)} %param.19) | copy-start | bytes 3076
  7.2 8.2 %copy-start.2 = (bf16[1,2048,512]{2,1,0:T(8,128)(2,1)S(1)}, bf16[1,2048,512]{2,1,0:T(8,128)(2,1)}, u32[]{:S(2)}) copy-start(bf16[1,2048,512]{2,1,0:T(8,128)(2,1)} %param.20) | copy-start | bytes 6291460
  7.2 128.2 %all-reduce.2.cloned.1.call-start = ((), (), s32[]{:S(2)}) async-start(), calls=%async_computation.1 | async-start | bytes 327680 | tf_op jit(solution)/shard_map/psum | solution.py:201
  9.5 16.5 %collective-permute-start = (bf16[1,512,512]{2,1,0:T(8,128)(2,1)}, bf16[1,512,512]{2,1,0:T(8,128)(2,1)}, u32[]{:S(2)}, u32[]{:S(2)}) collective-permute-start(bf16[1,512,512]{2,1,0:T(8,128)(2,1)} %get-tuple-element.8), channel_id=1, source_target_pairs={{0,24},{8,0},{16,8},{24,16},{1,25},{9,1},{17,9},{25,17},{2,26},{10... | collective-permute-start | bytes 1572872 | tf_op jit(solution)/shard_map/ppermute | solution.py:23
  13.4 24.7 %collective-permute-start.1 = (bf16[1,512,512]{2,1,0:T(8,128)(2,1)S(1)}, bf16[1,512,512]{2,1,0:T(8,128)(2,1)}, u32[]{:S(2)}, u32[]{:S(2)}) collective-permute-start(bf16[1,512,512]{2,1,0:T(8,128)(2,1)S(1)} %get-tuple-element.7), channel_id=1, source_target_pairs={{0,16},{8,24},{16,0},{24,8},{1,17},{9,25},{17,1},{25,9},{2,18},{10... | collective-permute-start | bytes 1572872 | tf_op jit(solution)/shard_map/ppermute | solution.py:23
  13.9 24.2 %collective-permute-start.2 = (bf16[1,512,512]{2,1,0:T(8,128)(2,1)S(1)}, bf16[1,512,512]{2,1,0:T(8,128)(2,1)}, u32[]{:S(2)}, u32[]{:S(2)}) collective-permute-start(bf16[1,512,512]{2,1,0:T(8,128)(2,1)S(1)} %get-tuple-element.6), channel_id=1, source_target_pairs={{0,8},{8,16},{16,24},{24,0},{1,9},{9,17},{17,25},{25,1},{2,10},{10... | collective-permute-start | bytes 1572872 | tf_op jit(solution)/shard_map/ppermute | solution.py:23
  17.9 50.6 %copy-start.3 = (bf16[1,2560]{1,0:T(2,128)(2,1)S(1)}, bf16[1,2560]{1,0:T(2,128)(2,1)}, u32[]{:S(2)}) copy-start(bf16[1,2560]{1,0:T(2,128)(2,1)} %param.22) | copy-start | bytes 15364
  17.9 65.0 %copy-start = (bf16[320,2560]{1,0:T(8,128)(2,1)S(1)}, bf16[320,2560]{1,0:T(8,128)(2,1)}, u32[]{:S(2)}) copy-start(bf16[320,2560]{1,0:T(8,128)(2,1)} %param.23) | copy-start | bytes 4915204
  67.7 68.8 %copy-start.4 = (f32[2560]{0:T(1024)S(1)}, f32[2560]{0:T(1024)}, u32[]{:S(2)}) copy-start(f32[2560]{0:T(1024)} %param.24) | copy-start | bytes 30724
  84.0 175.8 %all-gather.5.cloned.1.call-start = ((), (), s32[]{:S(2)}) async-start(), calls=%async_computation | async-start | bytes 14745600 | tf_op jit(solution)/shard_map/all_gather | solution.py:180
  259.8 11.0 %copy-start.1 = (bf16[1,512,2560]{2,1,0:T(8,128)(2,1)S(1)}, bf16[1,512,2560]{2,1,0:T(8,128)(2,1)}, u32[]{:S(2)}) copy-start(bf16[1,512,2560]{2,1,0:T(8,128)(2,1)} %param.17) | copy-start | bytes 7864324
Sparse Core Ops, SparseCore 0:
  84.1 51.2 all-reduce.1
  137.2 122.6 all-gather.4

commit v3 on v2

--- a/solution.py
+++ b/solution.py
@@ -189,19 +189,21 @@
     vocab_count = lax.axis_size("vocab")
     vocab_index = lax.axis_index("vocab")
     weight_rows = out_weight.shape[0]
+    head_count = local_dec + local_pre
     head_mixed = jnp.concatenate([dec_mixed, pre_mixed_3d[:, block_query - 1, :]], axis=0)
     head_resid = jnp.concatenate([dec_resid, pre_resid[:, block_query - 1, :]], axis=0)
-    group_rows = lax.all_gather(
-        jnp.concatenate([head_mixed, head_resid], axis=1), "vocab", axis=0, tiled=True
-    )
+    group_rows = lax.all_gather(head_mixed, "vocab", axis=0, tiled=True)
     own_columns = lax.dynamic_slice_in_dim(
         group_rows, vocab_index * weight_rows, weight_rows, axis=1
     )
     partial = jnp.dot(own_columns, out_weight, preferred_element_type=jnp.float32)
-    head_proj = lax.psum(partial, "vocab")
-    head_in = (group_rows[:, D:].astype(jnp.float32) + head_proj).astype(jnp.bfloat16)
-    everyone = lax.all_gather(normalize(head_in, norm_gain), "seq", axis=0, tiled=True)
-    layout = everyone.reshape(seq_count, vocab_count, local_dec + local_pre, D)
+    pieces = lax.all_to_all(
+        partial.reshape(vocab_count, head_count, D), "vocab", 0, 0, tiled=True
+    )
+    head_proj = jnp.sum(pieces, axis=0)
+    head_in = (head_resid.astype(jnp.float32) + head_proj).astype(jnp.bfloat16)
+    everyone = gather_all(normalize(head_in, norm_gain))
+    layout = everyone.reshape(seq_count, vocab_count, head_count, D)
     decode_all = layout[:, :, :local_dec].reshape(-1, D)
     prefill_every_request = layout[seq_count - 1, :, local_dec:].reshape(-1, D)
     head_rows = jnp.concatenate([decode_all, prefill_every_request], axis=0)

time: 281 us -> 191 us (0.68)
  waiting for transfers between devices: 140 us -> 35 us
  blocking collectives: 46.3 us -> 56.5 us
  starting transfers between devices: 5.07 us -> 12.4 us
    all_gather x1, waiting for transfers between devices: 68.4 us -> 0.01 us  [body(): lax.all_gather(out_weight, 'vocab', axis=0, tiled=True)]
    psum x1 -> x0, waiting for transfers between devices: 50.7 us -> none  [body(): head_proj = lax.psum(partial, 'vocab')]
    all_to_all x0 -> x1, waiting for transfers between devices: none -> 13.3 us  [body(): lax.all_to_all(partial.reshape(vocab_count, head_count, D), 'vocab', 0, 0...]
    all_gather x1 -> x2, blocking collectives: 14.7 us -> 25.6 us  [gather_all(): inner = lax.all_gather(value, 'vocab', axis=0, tiled=True)]
    all_gather x2 -> x1, blocking collectives: 23.5 us -> 14.4 us  [body(): group_rows = lax.all_gather(head_mixed, 'vocab', axis=0, tiled=True)]
    all_gather x1 -> x2, blocking collectives: 8.19 us -> 16.5 us  [gather_all(): return lax.all_gather(inner, 'seq', axis=0, tiled=True)]
    all_to_all x0 -> x1, starting transfers between devices: none -> 7.36 us  [body(): lax.all_to_all(partial.reshape(vocab_count, head_count, D), 'vocab', 0, 0...]
  transfers between devices with their start and end apart: 5 -> 5, of which waited for: 4 -> 3; matrix products, arithmetic and copies ran while one was open for 9% -> 14% of each run, Pallas kernels for 0% -> 16%
where the time goes in v3:
time: 191 us; the launch traced here: 190 us
  blocking collectives  56.5 us (30%)
  waiting for transfers between devices  35 us (18%)
  matrix products  30.5 us (16%)
  Pallas kernels  29.6 us (15%)
  between operations  15.6 us (8%)
  starting transfers between devices  12.4 us (6%)
  other arithmetic  6.23 us (3%)
  local copies, waits for them, and re-layouts  4.25 us (2%)
    pallas_call x1, Pallas kernels, prefill_attention(): pl.pallas_call(kernel, out_shape=jax.ShapeDtypeStruct(pre_query.shape, jn...  29.6 us
    all_gather x2, blocking collectives, gather_all(): inner = lax.all_gather(value, 'vocab', axis=0, tiled=True)  25.6 us
    ppermute x3, waiting for transfers between devices, from_behind(): return lax.ppermute(value, axis, pairs)  21 us
    dot_general x1, matrix products, body(): lax.dot_general(head_rows, embedding, (((1,), (1,)), ((), ())), preferred...  18.2 us
    all_gather x2, blocking collectives, gather_all(): return lax.all_gather(inner, 'seq', axis=0, tiled=True)  16.5 us
    all_gather x1, blocking collectives, body(): group_rows = lax.all_gather(head_mixed, 'vocab', axis=0, tiled=True)  14.4 us
    all_to_all x1, waiting for transfers between devices, body(): lax.all_to_all(partial.reshape(vocab_count, head_count, D), 'vocab', 0, 0...  13.3 us
    dot_general x1, matrix products, body(): jnp.dot(mixed_rows, lax.all_gather(out_weight, 'vocab', axis=0, tiled=Tru...  11 us
  transfers between devices with their start and end apart: 5, of which 3 were waited for; matrix products, arithmetic and copies ran while one was open for 14% of the time, Pallas kernels for 16%

profile of v3, /device:TPU:0, one launch (start us, length us, event | category | flops | bytes accessed | tf_op | source)
XLA Modules:
  0.0 190.1 jit_solution(2685568171718785807)
XLA Ops:
  7.2 0.0 copy-start.5
  7.2 0.0 copy-start.6
  7.2 0.0 copy-start.2
  7.2 0.0 all-gather.6.cloned.1.call-start
  7.2 0.7 all-gather.6.cloned.1.call-update
  7.9 2.1 %broadcast_select_fusion = (bf16[1,512,512]{2,1,0:T(8,128)(2,1)S(1)}, bf16[1,512,512]{2,1,0:T(8,128)(2,1)S(1)}, bf16[1,512,512]{2,1,0:T(8,128)(2,1)}) fusion(bf16[1,512,512]{2,1,0:T(8,128)(2,1)} %refs_4_.1, bf16[1,512,512]{2,1,0:T(8,128)(2,1)} %refs_0_.1, pred[]{:T(512)S(6)} %le.11, pred[]{:T(512)S(6)} %le.10, pred[]{:T(512)S(6)} %le.9), kind=kLoop, calls=%fused_computation.20 | loop fusion | flops 786432 | bytes 2621443 | tf_op jit(solution)/shard_map/jit(_where)/select_n | solution.py:132
  10.0 3.9 %collective-permute-start = (bf16[1,512,512]{2,1,0:T(8,128)(2,1)}, bf16[1,512,512]{2,1,0:T(8,128)(2,1)}, u32[]{:S(2)}, u32[]{:S(2)}) collective-permute-start(bf16[1,512,512]{2,1,0:T(8,128)(2,1)} %get-tuple-element.10), channel_id=1, source_target_pairs={{0,24},{8,0},{16,8},{24,16},{1,25},{9,1},{17,9},{25,17},{2,26},{10... | collective-permute-start | bytes 1572872 | tf_op jit(solution)/shard_map/ppermute | solution.py:23
  13.9 0.5 collective-permute-start.1
  14.4 0.6 collective-permute-start.2
  15.7 0.0 copy-done.5
  15.8 0.0 copy-done.6
  15.8 0.1 fusion.9
  15.9 0.0 copy-done.2
  15.9 0.5 select_reduce_fusion
  16.4 0.2 fusion.18
  16.7 0.3 fusion.8
  17.6 0.0 copy-start
  17.7 8.9 %collective-permute-done.refs_1_ = bf16[1,512,512]{2,1,0:T(8,128)(2,1)} collective-permute-done((bf16[1,512,512]{2,1,0:T(8,128)(2,1)}, bf16[1,512,512]{2,1,0:T(8,128)(2,1)}, u32[]{:S(2)}, u32[]{:S(2)}) %collective-permute-start) | collective-permute-done | bytes 524320 | tf_op jit(solution)/shard_map/ppermute | solution.py:23
  26.6 12.1 %collective-permute-done.1.refs_2_ = bf16[1,512,512]{2,1,0:T(8,128)(2,1)} collective-permute-done((bf16[1,512,512]{2,1,0:T(8,128)(2,1)S(1)}, bf16[1,512,512]{2,1,0:T(8,128)(2,1)}, u32[]{:S(2)}, u32[]{:S(2)}) %collective-permute-start.1) | collective-permute-done | bytes 524320 | tf_op jit(solution)/shard_map/ppermute | solution.py:23
  38.7 0.0 collective-permute-done.2.refs_3_
  38.7 29.6 %shard_map.156 = bf16[1,512,2560]{2,1,0:T(8,128)(2,1)} custom-call(s32[1]{0:T(128)S(6)} %sub.83.t0_ref, bf16[1,512,2560]{2,1,0:T(8,128)(2,1)} %q_ref.1, bf16[1,512,512]{2,1,0:T(8,128)(2,1)} %refs_0_.1, bf16[1,512,512]{2,1,0:T(8,128)(2,1)} %collective-permute-done.refs_1_, bf16[1,512,512]{2,1,0:T(8,128)(2,1)} %collective-permute-done.1.refs_2_, ...), custom_call_target="tpu_custom_call" | custom-call | flops 13421772800 | bytes 7864320 | tf_op jit(solution)/shard_map/pallas_call | solution.py:88
  68.2 0.0 copy-start.3
  68.2 0.0 copy-start.4
  68.3 0.8 slice_bitcast_fusion.1
  69.1 14.4 %all-gather.1 = bf16[8,2,2560]{2,1,0:T(2,128)(2,1)S(1)} all-gather(bf16[1,2,2560]{2,1,0:T(2,128)(2,1)S(1)} %maximum_bitcast_fusion), channel_id=1, replica_groups=mesh['seq'=4,'vocab'=8] {'vocab'}, dimensions={0}, use_global_device_ids=true | all-gather | bytes 92160 | tf_op jit(solution)/shard_map/all_gather | solution.py:195
  83.6 0.0 copy-done
  83.6 0.4 fusion.27
  84.0 0.8 reshape.158
  84.7 7.4 %all-to-all-start = ((f32[8,2,2560]{2,1,0:T(2,128)}), f32[8,2,2560]{2,1,0:T(2,128)S(1)}, u32[]{:S(2)}, u32[]{:S(2)}) async-start(f32[8,2,2560]{2,1,0:T(2,128)} %reshape.158), calls=%async_computation | async-start | bytes 327680 | tf_op jit(solution)/shard_map/all_to_all | solution.py:200
  92.1 0.8 slice_bitcast_fusion.2
  92.9 13.3 %all-to-all-done = f32[8,2,2560]{2,1,0:T(2,128)S(1)} async-done(((f32[8,2,2560]{2,1,0:T(2,128)}), f32[8,2,2560]{2,1,0:T(2,128)S(1)}, u32[]{:S(2)}, u32[]{:S(2)}) %all-to-all-start) | async-done | bytes 163872 | tf_op jit(solution)/shard_map/all_to_all | solution.py:200
  106.2 0.1 reduce_sum.46
  106.3 0.0 copy-done.3
  106.3 0.2 fusion.24
  106.5 0.0 copy-done.4
  106.5 0.1 fusion.30
  106.6 14.3 %all-gather.2 = bf16[8,2,2560]{2,1,0:T(2,128)(2,1)S(1)} all-gather(bf16[1,2,2560]{2,1,0:T(2,128)(2,1)S(1)} %fusion.30), channel_id=1, replica_groups=mesh['seq'=4,'vocab'=8] {'vocab'}, dimensions={0}, use_global_device_ids=true | all-gather | bytes 92160 | tf_op jit(solution)/shard_map/all_gather | solution.py:27
  120.9 9.3 %all_gather.21 = bf16[64,2560]{1,0:T(8,128)(2,1)S(1)} all-gather(bf16[16,2560]{1,0:T(8,128)(2,1)S(1)} %reshape.167), channel_id=1, replica_groups=mesh['seq'=4,'vocab'=8] {'seq'}, dimensions={0}, use_global_device_ids=true | all-gather | bytes 409600 | tf_op jit(solution)/shard_map/all_gather | solution.py:28
  130.2 0.1 reshape.159
  130.3 0.1 slice.61
  130.5 18.2 %fusion.44 = (f32[40]{0:T(128)S(1)}, f32[40,8000]{1,0:T(8,128)S(1)}) fusion(bf16[8000,2560]{1,0:T(8,128)(2,1)} %param.25, bf16[8,2560]{1,0:T(8,128)(2,1)S(1)} %bitcast.65, bf16[32,2560]{1,0:T(8,128)(2,1)S(1)} %bitcast.64), kind=kOutput, calls=%fused_computation.75 | convolution fusion | flops 1639129600 | bytes 42444960 | tf_op jit(solution)/shard_map/dot_general | solution.py:210
  148.7 0.4 exponential_reduce_fusion
  149.1 11.4 %all-gather.3 = f32[8,2,40]{2,1,0:T(2,128)S(1)} all-gather(f32[1,2,40]{2,1,0:T(2,128)S(1)} %maximum_bitcast_fusion.1), channel_id=2, replica_groups=mesh['seq'=4,'vocab'=8] {'vocab'}, dimensions={0}, use_global_device_ids=true | all-gather | bytes 2880 | tf_op jit(solution)/shard_map/all_gather | solution.py:27
  160.4 7.1 %all_gather.23 = f32[32,2,40]{2,1,0:T(2,128)S(1)} all-gather(f32[8,2,40]{2,1,0:T(2,128)S(1)} %all-gather.3), channel_id=1, replica_groups=mesh['seq'=4,'vocab'=8] {'seq'}, dimensions={0}, use_global_device_ids=true | all-gather | bytes 12800 | tf_op jit(solution)/shard_map/all_gather | solution.py:28
  167.7 0.1 subtract_convert_fusion
  167.8 0.8 slice.64
  168.7 0.7 slice.65
  169.3 0.0 all-gather.6.cloned.1.call-done
  169.3 0.0 copy-start.1
  169.3 11.0 %fusion.2 = f32[513,2560]{1,0:T(8,128)S(1)} fusion(bf16[2560,2560]{1,0:T(8,128)(2,1)} %all-gather.6.cloned.1.call-done, bf16[1,2560]{1,0:T(2,128)(2,1)S(1)} %bitcast.70, bf16[512,2560]{1,0:T(8,128)(2,1)} %bitcast.74), kind=kOutput, calls=%fused_computation.3 | convolution fusion | flops 6729246720 | bytes 20986880 | tf_op jit(solution)/shard_map/dot_general | solution.py:178
  180.3 0.0 copy-done.1
  180.3 2.3 %fusion.1 = bf16[1,512,2560]{2,1,0:T(8,128)(2,1)} fusion(f32[513,2560]{1,0:T(8,128)S(1)} %fusion.2, bf16[1,512,2560]{2,1,0:T(8,128)(2,1)S(1)} %copy-done.1), kind=kLoop, calls=%fused_computation.2 | loop fusion | flops 3932160 | bytes 10485760 | tf_op jit(solution)/shard_map/convert_element_type | solution.py:186
  182.6 0.6 fusion.29
  (19 shorter events, 0.4 us)
Async XLA Ops:
  7.2 8.5 %copy-start.5 = (bf16[1,2560]{1,0:T(2,128)(2,1)S(1)}, bf16[1,2560]{1,0:T(2,128)(2,1)}, u32[]{:S(2)}) copy-start(bf16[1,2560]{1,0:T(2,128)(2,1)} %param.18) | copy-start | bytes 15364
  7.2 8.6 %copy-start.6 = (bf16[1,512]{1,0:T(2,128)(2,1)S(1)}, bf16[1,512]{1,0:T(2,128)(2,1)}, u32[]{:S(2)}) copy-start(bf16[1,512]{1,0:T(2,128)(2,1)} %param.19) | copy-start | bytes 3076
  7.2 8.7 %copy-start.2 = (bf16[1,2048,512]{2,1,0:T(8,128)(2,1)S(1)}, bf16[1,2048,512]{2,1,0:T(8,128)(2,1)}, u32[]{:S(2)}) copy-start(bf16[1,2048,512]{2,1,0:T(8,128)(2,1)} %param.20) | copy-start | bytes 6291460
  7.2 162.1 %all-gather.6.cloned.1.call-start = ((), (), s32[]{:S(2)}) async-start(), calls=%async_computation.1 | async-start | bytes 14745600 | tf_op jit(solution)/shard_map/all_gather | solution.py:180
  10.0 16.5 %collective-permute-start = (bf16[1,512,512]{2,1,0:T(8,128)(2,1)}, bf16[1,512,512]{2,1,0:T(8,128)(2,1)}, u32[]{:S(2)}, u32[]{:S(2)}) collective-permute-start(bf16[1,512,512]{2,1,0:T(8,128)(2,1)} %get-tuple-element.10), channel_id=1, source_target_pairs={{0,24},{8,0},{16,8},{24,16},{1,25},{9,1},{17,9},{25,17},{2,26},{10... | collective-permute-start | bytes 1572872 | tf_op jit(solution)/shard_map/ppermute | solution.py:23
  13.9 24.7 %collective-permute-start.1 = (bf16[1,512,512]{2,1,0:T(8,128)(2,1)S(1)}, bf16[1,512,512]{2,1,0:T(8,128)(2,1)}, u32[]{:S(2)}, u32[]{:S(2)}) collective-permute-start(bf16[1,512,512]{2,1,0:T(8,128)(2,1)S(1)} %get-tuple-element.9), channel_id=1, source_target_pairs={{0,16},{8,24},{16,0},{24,8},{1,17},{9,25},{17,1},{25,9},{2,18},{10... | collective-permute-start | bytes 1572872 | tf_op jit(solution)/shard_map/ppermute | solution.py:23
  14.4 24.2 %collective-permute-start.2 = (bf16[1,512,512]{2,1,0:T(8,128)(2,1)S(1)}, bf16[1,512,512]{2,1,0:T(8,128)(2,1)}, u32[]{:S(2)}, u32[]{:S(2)}) collective-permute-start(bf16[1,512,512]{2,1,0:T(8,128)(2,1)S(1)} %get-tuple-element.8), channel_id=1, source_target_pairs={{0,8},{8,16},{16,24},{24,0},{1,9},{9,17},{17,25},{25,1},{2,10},{10... | collective-permute-start | bytes 1572872 | tf_op jit(solution)/shard_map/ppermute | solution.py:23
  17.6 65.9 %copy-start = (bf16[320,2560]{1,0:T(8,128)(2,1)S(1)}, bf16[320,2560]{1,0:T(8,128)(2,1)}, u32[]{:S(2)}) copy-start(bf16[320,2560]{1,0:T(8,128)(2,1)} %param.23) | copy-start | bytes 4915204
  68.2 38.1 %copy-start.3 = (bf16[1,2560]{1,0:T(2,128)(2,1)S(1)}, bf16[1,2560]{1,0:T(2,128)(2,1)}, u32[]{:S(2)}) copy-start(bf16[1,2560]{1,0:T(2,128)(2,1)} %param.22) | copy-start | bytes 15364
  68.2 38.2 %copy-start.4 = (f32[2560]{0:T(1024)S(1)}, f32[2560]{0:T(1024)}, u32[]{:S(2)}) copy-start(f32[2560]{0:T(1024)} %param.24) | copy-start | bytes 30724
  84.7 21.5 %all-to-all-start = ((f32[8,2,2560]{2,1,0:T(2,128)}), f32[8,2,2560]{2,1,0:T(2,128)S(1)}, u32[]{:S(2)}, u32[]{:S(2)}) async-start(f32[8,2,2560]{2,1,0:T(2,128)} %reshape.158), calls=%async_computation | async-start | bytes 327680 | tf_op jit(solution)/shard_map/all_to_all | solution.py:200
  169.3 11.0 %copy-start.1 = (bf16[1,512,2560]{2,1,0:T(8,128)(2,1)S(1)}, bf16[1,512,2560]{2,1,0:T(8,128)(2,1)}, u32[]{:S(2)}) copy-start(bf16[1,512,2560]{2,1,0:T(8,128)(2,1)} %param.17) | copy-start | bytes 7864324
Sparse Core Ops, SparseCore 0:
  9.7 128.3 all-gather.5

commit v4 on v2

--- a/solution.py
+++ b/solution.py
@@ -26,6 +26,18 @@
 def gather_all(value):
     inner = lax.all_gather(value, "vocab", axis=0, tiled=True)
     return lax.all_gather(inner, "seq", axis=0, tiled=True)
+
+
+def pairwise_sum(value, axis):
+    count = lax.axis_size(axis)
+    if count & (count - 1):
+        return lax.psum(value, axis)
+    step = 1
+    while step < count:
+        pairs = [(source, source ^ step) for source in range(count)]
+        value = value + lax.ppermute(value, axis, pairs)
+        step *= 2
+    return value
 
 
 def normalize(rows_in, gain):
@@ -189,6 +201,7 @@
     vocab_count = lax.axis_size("vocab")
     vocab_index = lax.axis_index("vocab")
     weight_rows = out_weight.shape[0]
+    head_count = local_dec + local_pre
     head_mixed = jnp.concatenate([dec_mixed, pre_mixed_3d[:, block_query - 1, :]], axis=0)
     head_resid = jnp.concatenate([dec_resid, pre_resid[:, block_query - 1, :]], axis=0)
     group_rows = lax.all_gather(
@@ -198,10 +211,10 @@
         group_rows, vocab_index * weight_rows, weight_rows, axis=1
     )
     partial = jnp.dot(own_columns, out_weight, preferred_element_type=jnp.float32)
-    head_proj = lax.psum(partial, "vocab")
+    head_proj = pairwise_sum(partial, "vocab")
     head_in = (group_rows[:, D:].astype(jnp.float32) + head_proj).astype(jnp.bfloat16)
     everyone = lax.all_gather(normalize(head_in, norm_gain), "seq", axis=0, tiled=True)
-    layout = everyone.reshape(seq_count, vocab_count, local_dec + local_pre, D)
+    layout = everyone.reshape(seq_count, vocab_count, head_count, D)
     decode_all = layout[:, :, :local_dec].reshape(-1, D)
     prefill_every_request = layout[seq_count - 1, :, local_dec:].reshape(-1, D)
     head_rows = jnp.concatenate([decode_all, prefill_every_request], axis=0)

time: 281 us -> 203 us (0.72)
  waiting for transfers between devices: 140 us -> 63 us
    all_gather x1, waiting for transfers between devices: 68.4 us -> 0.01 us  [body(): lax.all_gather(out_weight, 'vocab', axis=0, tiled=True)]
    psum x1 -> x0, waiting for transfers between devices: 50.7 us -> none  [body(): head_proj = lax.psum(partial, 'vocab')]
    ppermute x0 -> x3, waiting for transfers between devices: none -> 41.9 us  [pairwise_sum(): value = value + lax.ppermute(value, axis, pairs)]
    all_gather x1, blocking collectives: 14.3 us -> 17.9 us  [body(): lax.all_gather(jnp.concatenate([head_mixed, head_resid], axis=1), 'vocab'...]
  transfers between devices with their start and end apart: 5 -> 7, of which waited for: 4 -> 5; matrix products, arithmetic and copies ran while one was open for 9% -> 13% of each run, Pallas kernels for 0% -> 15%
where the time goes in v4:
time: 203 us
  waiting for transfers between devices  63 us (31%)
  blocking collectives  48.6 us (24%)
  matrix products  30.5 us (15%)
  Pallas kernels  29.6 us (15%)
  between operations  15.6 us (8%)
  other arithmetic  6.41 us (3%)
  starting transfers between devices  5.51 us (3%)
  local copies, waits for them, and re-layouts  3.48 us (2%)
    ppermute x3, waiting for transfers between devices, pairwise_sum(): value = value + lax.ppermute(value, axis, pairs)  41.9 us
    pallas_call x1, Pallas kernels, prefill_attention(): pl.pallas_call(kernel, out_shape=jax.ShapeDtypeStruct(pre_query.shape, jn...  29.6 us
    ppermute x3, waiting for transfers between devices, from_behind(): return lax.ppermute(value, axis, pairs)  20.4 us
    dot_general x1, matrix products, body(): lax.dot_general(head_rows, embedding, (((1,), (1,)), ((), ())), preferred...  18.1 us
    all_gather x1, blocking collectives, body(): lax.all_gather(jnp.concatenate([head_mixed, head_resid], axis=1), 'vocab'...  17.9 us
    all_gather x1, blocking collectives, gather_all(): inner = lax.all_gather(value, 'vocab', axis=0, tiled=True)  14.9 us
    dot_general x1, matrix products, body(): jnp.dot(mixed_rows, lax.all_gather(out_weight, 'vocab', axis=0, tiled=Tru...  11 us
    all_gather x1, blocking collectives, body(): lax.all_gather(normalize(head_in, norm_gain), 'seq', axis=0, tiled=True)  8.44 us
  transfers between devices with their start and end apart: 7, of which 5 were waited for; matrix products, arithmetic and copies ran while one was open for 13% of the time, Pallas kernels for 15%

profile of v4, /device:TPU:0, one launch (start us, length us, event | category | flops | bytes accessed | tf_op | source)
XLA Modules:
  0.0 202.6 jit_solution(10645316477346951010)
XLA Ops:
  7.2 0.0 copy-start.5
  7.2 0.0 copy-start.6
  7.2 0.0 copy-start.2
  7.2 0.0 all-gather.5.cloned.1.call-start
  7.2 0.7 all-gather.5.cloned.1.call-update
  7.9 2.3 %broadcast_select_fusion = (bf16[1,512,512]{2,1,0:T(8,128)(2,1)S(1)}, bf16[1,512,512]{2,1,0:T(8,128)(2,1)}, bf16[1,512,512]{2,1,0:T(8,128)(2,1)}) fusion(bf16[1,512,512]{2,1,0:T(8,128)(2,1)} %refs_4_.1, bf16[1,512,512]{2,1,0:T(8,128)(2,1)} %refs_0_.1, pred[]{:T(512)S(6)} %le.11, pred[]{:T(512)S(6)} %le.10, pred[]{:T(512)S(6)} %le.9), kind=kLoop, calls=%fused_computation.20 | loop fusion | flops 786432 | bytes 2621443 | tf_op jit(solution)/shard_map/jit(_where)/select_n | solution.py:144
  10.2 3.9 %collective-permute-start = (bf16[1,512,512]{2,1,0:T(8,128)(2,1)}, bf16[1,512,512]{2,1,0:T(8,128)(2,1)S(1)}, u32[]{:S(2)}, u32[]{:S(2)}) collective-permute-start(bf16[1,512,512]{2,1,0:T(8,128)(2,1)} %get-tuple-element.10), channel_id=1, source_target_pairs={{0,24},{8,0},{16,8},{24,16},{1,25},{9,1},{17,9},{25,17},{2,26},{10... | collective-permute-start | bytes 1572872 | tf_op jit(solution)/shard_map/ppermute | solution.py:23
  14.1 0.5 collective-permute-start.1
  14.6 0.6 collective-permute-start.2
  15.9 0.0 copy-done.5
  16.0 0.0 copy-done.6
  16.0 0.1 fusion.9
  16.1 0.0 copy-done.2
  16.1 0.5 select_reduce_fusion
  16.6 0.2 fusion.21
  16.8 0.3 fusion.8
  17.8 0.8 slice_bitcast_fusion.2
  18.6 0.0 copy-start.3
  18.6 0.0 copy-start
  18.7 8.1 %collective-permute-done.refs_1_ = bf16[1,512,512]{2,1,0:T(8,128)(2,1)S(1)} collective-permute-done((bf16[1,512,512]{2,1,0:T(8,128)(2,1)}, bf16[1,512,512]{2,1,0:T(8,128)(2,1)S(1)}, u32[]{:S(2)}, u32[]{:S(2)}) %collective-permute-start) | collective-permute-done | bytes 524320 | tf_op jit(solution)/shard_map/ppermute | solution.py:23
  26.8 0.0 copy-start.7
  26.8 12.3 %collective-permute-done.1.refs_2_ = bf16[1,512,512]{2,1,0:T(8,128)(2,1)} collective-permute-done((bf16[1,512,512]{2,1,0:T(8,128)(2,1)}, bf16[1,512,512]{2,1,0:T(8,128)(2,1)}, u32[]{:S(2)}, u32[]{:S(2)}) %collective-permute-start.1) | collective-permute-done | bytes 524320 | tf_op jit(solution)/shard_map/ppermute | solution.py:23
  39.0 0.0 collective-permute-done.2.refs_3_
  39.1 0.0 copy-done.7
  39.1 29.6 %shard_map.156 = bf16[1,512,2560]{2,1,0:T(8,128)(2,1)} custom-call(s32[1]{0:T(128)S(6)} %sub.83.t0_ref, bf16[1,512,2560]{2,1,0:T(8,128)(2,1)} %q_ref.1, bf16[1,512,512]{2,1,0:T(8,128)(2,1)} %refs_0_.1, bf16[1,512,512]{2,1,0:T(8,128)(2,1)} %copy-done.7, bf16[1,512,512]{2,1,0:T(8,128)(2,1)} %collective-permute-done.1.refs_2_, ...), custom_call_target="tpu_custom_call" | custom-call | flops 13421772800 | bytes 7864320 | tf_op jit(solution)/shard_map/pallas_call | solution.py:100
  68.7 0.0 copy-start.4
  68.7 0.8 slice_bitcast_fusion.1
  69.5 0.0 copy-done.3
  69.5 0.1 maximum_bitcast_fusion
  69.5 17.9 %all-gather.1 = bf16[8,2,5120]{2,1,0:T(2,128)(2,1)S(1)} all-gather(bf16[1,2,5120]{2,1,0:T(2,128)(2,1)S(1)} %maximum_bitcast_fusion), channel_id=1, replica_groups=mesh['seq'=4,'vocab'=8] {'vocab'}, dimensions={0}, use_global_device_ids=true | all-gather | bytes 184320 | tf_op jit(solution)/shard_map/all_gather | solution.py:207
  87.4 0.1 reshape.161
  87.5 0.0 copy-done
  87.5 0.4 fusion.27
  87.9 0.3 collective-permute-start.3
  88.2 1.1 collective-permute-done.3
  89.3 0.1 collective-permute-start.4
  89.4 22.6 %collective-permute-done.4 = f32[16,2560]{1,0:T(8,128)S(1)} collective-permute-done((f32[16,2560]{1,0:T(8,128)S(1)}, f32[16,2560]{1,0:T(8,128)S(1)}, u32[]{:S(2)}, u32[]{:S(2)}) %collective-permute-start.4) | collective-permute-done | bytes 163872 | tf_op jit(solution)/shard_map/ppermute | solution.py:38
  112.0 0.1 collective-permute-start.5
  112.1 18.2 %collective-permute-done.5 = f32[16,2560]{1,0:T(8,128)S(1)} collective-permute-done((f32[16,2560]{1,0:T(8,128)S(1)}, f32[16,2560]{1,0:T(8,128)S(1)}, u32[]{:S(2)}, u32[]{:S(2)}) %collective-permute-start.5) | collective-permute-done | bytes 163872 | tf_op jit(solution)/shard_map/ppermute | solution.py:38
  130.3 0.1 fusion.18
  130.5 0.0 copy-done.4
  130.5 0.1 fusion.20
  130.6 8.4 %all_gather.17 = bf16[64,2560]{1,0:T(8,128)(2,1)S(1)} all-gather(bf16[16,2560]{1,0:T(8,128)(2,1)S(1)} %fusion.20), channel_id=1, replica_groups=mesh['seq'=4,'vocab'=8] {'seq'}, dimensions={0}, use_global_device_ids=true | all-gather | bytes 409600 | tf_op jit(solution)/shard_map/all_gather | solution.py:216
  139.0 0.1 reshape.155
  139.1 0.1 slice.66
  139.3 18.1 %fusion.43 = (f32[40]{0:T(128)S(1)}, f32[40,8000]{1,0:T(8,128)S(1)}) fusion(bf16[8000,2560]{1,0:T(8,128)(2,1)} %param.25, bf16[8,2560]{1,0:T(8,128)(2,1)S(1)} %bitcast.63, bf16[32,2560]{1,0:T(8,128)(2,1)S(1)} %bitcast.62), kind=kOutput, calls=%fused_computation.74 | convolution fusion | flops 1639129600 | bytes 42444960 | tf_op jit(solution)/shard_map/dot_general | solution.py:221
  157.4 0.4 exponential_reduce_fusion
  157.8 14.9 %all-gather.2 = f32[8,2,40]{2,1,0:T(2,128)S(1)} all-gather(f32[1,2,40]{2,1,0:T(2,128)S(1)} %maximum_bitcast_fusion.1), channel_id=2, replica_groups=mesh['seq'=4,'vocab'=8] {'vocab'}, dimensions={0}, use_global_device_ids=true | all-gather | bytes 2880 | tf_op jit(solution)/shard_map/all_gather | solution.py:27
  172.7 7.4 %all_gather.19 = f32[32,2,40]{2,1,0:T(2,128)S(1)} all-gather(f32[8,2,40]{2,1,0:T(2,128)S(1)} %all-gather.2), channel_id=1, replica_groups=mesh['seq'=4,'vocab'=8] {'seq'}, dimensions={0}, use_global_device_ids=true | all-gather | bytes 12800 | tf_op jit(solution)/shard_map/all_gather | solution.py:28
  180.2 0.1 subtract_convert_fusion
  180.3 0.8 slice.69
  181.2 0.7 slice.70
  181.8 0.0 all-gather.5.cloned.1.call-done
  181.8 0.0 copy-start.1
  181.8 11.0 %fusion.2 = f32[513,2560]{1,0:T(8,128)S(1)} fusion(bf16[2560,2560]{1,0:T(8,128)(2,1)} %all-gather.5.cloned.1.call-done, bf16[1,2560]{1,0:T(2,128)(2,1)S(1)} %bitcast.68, bf16[512,2560]{1,0:T(8,128)(2,1)} %bitcast.72), kind=kOutput, calls=%fused_computation.3 | convolution fusion | flops 6729246720 | bytes 20986880 | tf_op jit(solution)/shard_map/dot_general | solution.py:190
  192.8 0.0 copy-done.1
  192.9 2.3 %fusion.1 = bf16[1,512,2560]{2,1,0:T(8,128)(2,1)} fusion(f32[513,2560]{1,0:T(8,128)S(1)} %fusion.2, bf16[1,512,2560]{2,1,0:T(8,128)(2,1)S(1)} %copy-done.1), kind=kLoop, calls=%fused_computation.2 | loop fusion | flops 3932160 | bytes 10485760 | tf_op jit(solution)/shard_map/convert_element_type | solution.py:198
  195.1 0.6 fusion.29
  (18 shorter events, 0.3 us)
Async XLA Ops:
  7.2 8.7 %copy-start.5 = (bf16[1,2560]{1,0:T(2,128)(2,1)S(1)}, bf16[1,2560]{1,0:T(2,128)(2,1)}, u32[]{:S(2)}) copy-start(bf16[1,2560]{1,0:T(2,128)(2,1)} %param.18) | copy-start | bytes 15364
  7.2 8.8 %copy-start.6 = (bf16[1,512]{1,0:T(2,128)(2,1)S(1)}, bf16[1,512]{1,0:T(2,128)(2,1)}, u32[]{:S(2)}) copy-start(bf16[1,512]{1,0:T(2,128)(2,1)} %param.19) | copy-start | bytes 3076
  7.2 8.9 %copy-start.2 = (bf16[1,2048,512]{2,1,0:T(8,128)(2,1)S(1)}, bf16[1,2048,512]{2,1,0:T(8,128)(2,1)}, u32[]{:S(2)}) copy-start(bf16[1,2048,512]{2,1,0:T(8,128)(2,1)} %param.20) | copy-start | bytes 6291460
  7.2 174.6 %all-gather.5.cloned.1.call-start = ((), (), s32[]{:S(2)}) async-start(), calls=%async_computation | async-start | bytes 14745600 | tf_op jit(solution)/shard_map/all_gather | solution.py:192
  10.2 16.5 %collective-permute-start = (bf16[1,512,512]{2,1,0:T(8,128)(2,1)}, bf16[1,512,512]{2,1,0:T(8,128)(2,1)S(1)}, u32[]{:S(2)}, u32[]{:S(2)}) collective-permute-start(bf16[1,512,512]{2,1,0:T(8,128)(2,1)} %get-tuple-element.10), channel_id=1, source_target_pairs={{0,24},{8,0},{16,8},{24,16},{1,25},{9,1},{17,9},{25,17},{2,26},{10... | collective-permute-start | bytes 1572872 | tf_op jit(solution)/shard_map/ppermute | solution.py:23
  14.1 24.9 %collective-permute-start.1 = (bf16[1,512,512]{2,1,0:T(8,128)(2,1)}, bf16[1,512,512]{2,1,0:T(8,128)(2,1)}, u32[]{:S(2)}, u32[]{:S(2)}) collective-permute-start(bf16[1,512,512]{2,1,0:T(8,128)(2,1)} %get-tuple-element.9), channel_id=1, source_target_pairs={{0,16},{8,24},{16,0},{24,8},{1,17},{9,25},{17,1},{25,9},{2,18},{10... | collective-permute-start | bytes 1572872 | tf_op jit(solution)/shard_map/ppermute | solution.py:23
  14.6 24.4 %collective-permute-start.2 = (bf16[1,512,512]{2,1,0:T(8,128)(2,1)S(1)}, bf16[1,512,512]{2,1,0:T(8,128)(2,1)}, u32[]{:S(2)}, u32[]{:S(2)}) collective-permute-start(bf16[1,512,512]{2,1,0:T(8,128)(2,1)S(1)} %get-tuple-element.8), channel_id=1, source_target_pairs={{0,8},{8,16},{16,24},{24,0},{1,9},{9,17},{17,25},{25,1},{2,10},{10... | collective-permute-start | bytes 1572872 | tf_op jit(solution)/shard_map/ppermute | solution.py:23
  18.6 50.8 %copy-start.3 = (bf16[1,2560]{1,0:T(2,128)(2,1)S(1)}, bf16[1,2560]{1,0:T(2,128)(2,1)}, u32[]{:S(2)}) copy-start(bf16[1,2560]{1,0:T(2,128)(2,1)} %param.22) | copy-start | bytes 15364
  18.6 68.8 %copy-start = (bf16[320,2560]{1,0:T(8,128)(2,1)S(1)}, bf16[320,2560]{1,0:T(8,128)(2,1)}, u32[]{:S(2)}) copy-start(bf16[320,2560]{1,0:T(8,128)(2,1)} %param.23) | copy-start | bytes 4915204
  26.8 12.3 %copy-start.7 = (bf16[1,512,512]{2,1,0:T(8,128)(2,1)}, bf16[1,512,512]{2,1,0:T(8,128)(2,1)S(1)}, u32[]{:S(2)}) copy-start(bf16[1,512,512]{2,1,0:T(8,128)(2,1)S(1)} %collective-permute-done.refs_1_) | copy-start | bytes 1572868
  68.7 61.8 %copy-start.4 = (f32[2560]{0:T(1024)S(1)}, f32[2560]{0:T(1024)}, u32[]{:S(2)}) copy-start(f32[2560]{0:T(1024)} %param.24) | copy-start | bytes 30724
  87.9 1.4 collective-permute-start.3
  89.3 22.7 %collective-permute-start.4 = (f32[16,2560]{1,0:T(8,128)S(1)}, f32[16,2560]{1,0:T(8,128)S(1)}, u32[]{:S(2)}, u32[]{:S(2)}) collective-permute-start(f32[16,2560]{1,0:T(8,128)S(1)} %add.78), channel_id=1, source_target_pairs={{0,2},{1,3},{2,0},{3,1},{4,6},{5,7},{6,4},{7,5},{8,10},{9,11},{10,... | collective-permute-start | bytes 491528 | tf_op jit(solution)/shard_map/ppermute | solution.py:38
  112.0 18.3 %collective-permute-start.5 = (f32[16,2560]{1,0:T(8,128)S(1)}, f32[16,2560]{1,0:T(8,128)S(1)}, u32[]{:S(2)}, u32[]{:S(2)}) collective-permute-start(f32[16,2560]{1,0:T(8,128)S(1)} %add.79), channel_id=1, source_target_pairs={{0,4},{1,5},{2,6},{3,7},{4,0},{5,1},{6,2},{7,3},{8,12},{9,13},{10,... | collective-permute-start | bytes 491528 | tf_op jit(solution)/shard_map/ppermute | solution.py:38
  181.8 11.0 %copy-start.1 = (bf16[1,512,2560]{2,1,0:T(8,128)(2,1)S(1)}, bf16[1,512,2560]{2,1,0:T(8,128)(2,1)}, u32[]{:S(2)}) copy-start(bf16[1,512,2560]{2,1,0:T(8,128)(2,1)} %param.17) | copy-start | bytes 7864324
Sparse Core Ops, SparseCore 0:
  9.7 131.8 all-gather.4

commit v5 on v3

--- a/solution.py
+++ b/solution.py
@@ -34,75 +34,137 @@
     return (values * lax.rsqrt(square_mean + STABILITY_FLOOR) * gain).astype(jnp.bfloat16)
 
 
-def prefill_kernel(t0_ref, q_ref, *refs, n_blocks, block, tq):
-    kv_refs = refs[:n_blocks]
-    o_ref = refs[n_blocks]
+def prefill_kernel(t0_ref, q_ref, *refs, positions, n_blocks, block, tq, carry_in, final):
+    n_in = len(positions)
+    if carry_in:
+        peak_ref, denom_ref, accum_ref = refs[:3]
+        refs = refs[3:]
+    kv_refs = refs[:n_in]
+    out_refs = refs[n_in:]
     r = pl.program_id(0)
     qi = pl.program_id(2)
     t0 = t0_ref[r]
     q = q_ref[0]
     row = qi * tq + lax.broadcasted_iota(jnp.int32, (tq, block), 0)
     col = lax.broadcasted_iota(jnp.int32, (tq, block), 1)
-    peak = jnp.full((tq, 1), NEG_BIG, jnp.float32)
-    denom = jnp.zeros((tq, 1), jnp.float32)
-    accum = jnp.zeros((tq, HEAD_SIZE), jnp.float32)
+    if carry_in:
+        state = (peak_ref[0, 0], denom_ref[0, 0], accum_ref[0])
+    else:
+        state = (
+            jnp.full((tq, 1), NEG_BIG, jnp.float32),
+            jnp.zeros((tq, 1), jnp.float32),
+            jnp.zeros((tq, HEAD_SIZE), jnp.float32),
+        )
     scale = HEAD_SIZE ** (-0.5)
-    for j in range(n_blocks):
-        kv = kv_refs[j]
+    for kv, j in zip(kv_refs, positions):
         keys = kv[0, :, :HEAD_SIZE]
         values = kv[0, :, HEAD_SIZE:]
-        scores = (
-            lax.dot_general(
-                q, keys, (((1,), (1,)), ((), ())), preferred_element_type=jnp.float32
+
+        def absorb(state, valid):
+            peak, denom, accum = state
+            scores = (
+                lax.dot_general(
+                    q, keys, (((1,), (1,)), ((), ())), preferred_element_type=jnp.float32
+                )
+                * scale
             )
-            * scale
-        )
-        t = j * block + col
-        valid = t >= t0
-        if j == 0:
-            valid = valid & (t > row)
-        if j == n_blocks - 1:
-            valid = valid & (t <= row + WIN)
-        peak_new = jnp.maximum(
-            peak, jnp.max(jnp.where(valid, scores, NEG_BIG), axis=1, keepdims=True)
-        )
-        weights = jnp.where(valid, jnp.exp(scores - peak_new), 0.0)
-        decay = jnp.exp(peak - peak_new)
-        denom = denom * decay + jnp.sum(weights, axis=1, keepdims=True)
-        accum = accum * decay + jnp.dot(
-            weights.astype(jnp.bfloat16), values, preferred_element_type=jnp.float32
-        )
-        peak = peak_new
-    o_ref[0] = (accum / denom).astype(o_ref.dtype)
-
-
-def prefill_attention(pre_query, kv_blocks, first_key):
+            if valid is None:
+                peak_new = jnp.maximum(peak, jnp.max(scores, axis=1, keepdims=True))
+                weights = jnp.exp(scores - peak_new)
+            else:
+                peak_new = jnp.maximum(
+                    peak, jnp.max(jnp.where(valid, scores, NEG_BIG), axis=1, keepdims=True)
+                )
+                weights = jnp.where(valid, jnp.exp(scores - peak_new), 0.0)
+            decay = jnp.exp(peak - peak_new)
+            denom = denom * decay + jnp.sum(weights, axis=1, keepdims=True)
+            accum = accum * decay + jnp.dot(
+                weights.astype(jnp.bfloat16), values, preferred_element_type=jnp.float32
+            )
+            return (peak_new, denom, accum)
+
+        def masked(state):
+            t = j * block + col
+            valid = t >= t0
+            if j == 0:
+                valid = valid & (t > row)
+            if j == n_blocks - 1:
+                valid = valid & (t <= row + WIN)
+            return absorb(state, valid)
+
+        if j == 0 or j == n_blocks - 1:
+            state = masked(state)
+        else:
+            state = lax.cond(
+                t0 <= j * block, lambda st: absorb(st, None), masked, state
+            )
+    peak, denom, accum = state
+    if final:
+        out_refs[0][0] = (accum / denom).astype(out_refs[0].dtype)
+    else:
+        out_refs[0][0, 0] = peak
+        out_refs[1][0, 0] = denom
+        out_refs[2][0] = accum
+
+
+def prefill_pass(pre_query, kv_blocks, positions, n_blocks, first_key, carry, final):
     local_pre, block_query, _ = pre_query.shape
     block = kv_blocks[0].shape[1]
-    n_blocks = len(kv_blocks)
     tq = min(block_query, 512)
-    kernel = functools.partial(prefill_kernel, n_blocks=n_blocks, block=block, tq=tq)
+    kernel = functools.partial(
+        prefill_kernel,
+        positions=tuple(positions),
+        n_blocks=n_blocks,
+        block=block,
+        tq=tq,
+        carry_in=carry is not None,
+        final=final,
+    )
     kv_spec = pl.BlockSpec((1, block, 2 * HEAD_SIZE), lambda r, h, qi, t0: (r, 0, 0))
     q_spec = pl.BlockSpec((1, tq, HEAD_SIZE), lambda r, h, qi, t0: (r, qi, h))
-    flops = 4 * local_pre * HQ * block_query * block * n_blocks * HEAD_SIZE
+    stat_spec = pl.BlockSpec((1, 1, tq, 1), lambda r, h, qi, t0: (r, h, qi, 0))
+    stat_shape = jax.ShapeDtypeStruct((local_pre, HQ, block_query, 1), jnp.float32)
+    accum_shape = jax.ShapeDtypeStruct(pre_query.shape, jnp.float32)
+    carry_specs = [] if carry is None else [stat_spec, stat_spec, q_spec]
+    carry_args = [] if carry is None else list(carry)
+    if final:
+        out_shape = jax.ShapeDtypeStruct(pre_query.shape, jnp.bfloat16)
+        out_specs = q_spec
+    else:
+        out_shape = (stat_shape, stat_shape, accum_shape)
+        out_specs = (stat_spec, stat_spec, q_spec)
+    n_in = len(kv_blocks)
+    flops = 4 * local_pre * HQ * block_query * block * n_in * HEAD_SIZE
     return pl.pallas_call(
         kernel,
-        out_shape=jax.ShapeDtypeStruct(pre_query.shape, jnp.bfloat16),
+        out_shape=out_shape,
         grid_spec=pltpu.PrefetchScalarGridSpec(
             num_scalar_prefetch=1,
             grid=(local_pre, HQ, block_query // tq),
-            in_specs=[q_spec] + [kv_spec] * n_blocks,
-            out_specs=q_spec,
+            in_specs=[q_spec] + carry_specs + [kv_spec] * n_in,
+            out_specs=out_specs,
         ),
         compiler_params=pltpu.CompilerParams(
             dimension_semantics=("arbitrary", "arbitrary", "arbitrary")
         ),
         cost_estimate=pl.CostEstimate(
             flops=flops,
-            transcendentals=local_pre * HQ * block_query * block * n_blocks,
+            transcendentals=local_pre * HQ * block_query * block * n_in,
             bytes_accessed=2 * pre_query.size * 2 + sum(b.size for b in kv_blocks) * 2,
         ),
-    )(first_key, pre_query, *kv_blocks)
+    )(first_key, pre_query, *carry_args, *kv_blocks)
+
+
+def prefill_attention(pre_query, kv_blocks, first_key):
+    n_blocks = len(kv_blocks)
+    carry = prefill_pass(
+        pre_query, [kv_blocks[0], kv_blocks[-1]], [0, n_blocks - 1], n_blocks,
+        first_key, None, False,
+    )
+    middle = list(range(1, n_blocks - 1))
+    return prefill_pass(
+        pre_query, [kv_blocks[j] for j in middle], middle, n_blocks, first_key, carry, True
+    )
 
 
 def body(

time: 191 us -> 212 us (1.11); the launches traced: 190 us -> 214 us
  Pallas kernels: 29.6 us -> 69.2 us
  waiting for transfers between devices: 35 us -> 20 us
    pallas_call x1 -> x2, Pallas kernels: 29.6 us -> 69.2 us  [prefill_pass(): pl.pallas_call(kernel, out_shape=out_shape, grid_spec=pltpu.PrefetchScala...]
    ppermute x3, waiting for transfers between devices: 21 us -> 6.06 us  [from_behind(): return lax.ppermute(value, axis, pairs)]
    all_gather x2, blocking collectives: 25.6 us -> 23.5 us  [gather_all(): inner = lax.all_gather(value, 'vocab', axis=0, tiled=True)]
  transfers between devices with their start and end apart: 5 -> 5, of which waited for: 3 -> 2; matrix products, arithmetic and copies ran while one was open for 14% -> 13% of each run, Pallas kernels for 16% -> 32%
where the time goes in v5:
time: 212 us; the launch traced here: 214 us
  Pallas kernels  69.2 us (33%)
  blocking collectives  55.6 us (26%)
  matrix products  30.4 us (14%)
  waiting for transfers between devices  20 us (9%)
  between operations  15.6 us (7%)
  starting transfers between devices  12.9 us (6%)
  other arithmetic  6.23 us (3%)
  local copies, waits for them, and re-layouts  4.24 us (2%)
    pallas_call x2, Pallas kernels, prefill_pass(): pl.pallas_call(kernel, out_shape=out_shape, grid_spec=pltpu.PrefetchScala...  69.2 us
    all_gather x2, blocking collectives, gather_all(): inner = lax.all_gather(value, 'vocab', axis=0, tiled=True)  23.5 us
    dot_general x1, matrix products, body(): lax.dot_general(head_rows, embedding, (((1,), (1,)), ((), ())), preferred...  18.1 us
    all_gather x2, blocking collectives, gather_all(): return lax.all_gather(inner, 'seq', axis=0, tiled=True)  16.4 us
    all_gather x1, blocking collectives, body(): group_rows = lax.all_gather(head_mixed, 'vocab', axis=0, tiled=True)  15.7 us
    all_to_all x1, waiting for transfers between devices, body(): lax.all_to_all(partial.reshape(vocab_count, head_count, D), 'vocab', 0, 0...  13.3 us
    dot_general x1, matrix products, body(): jnp.dot(mixed_rows, lax.all_gather(out_weight, 'vocab', axis=0, tiled=Tru...  11 us
    all_to_all x1, starting transfers between devices, body(): lax.all_to_all(partial.reshape(vocab_count, head_count, D), 'vocab', 0, 0...  7.87 us
  transfers between devices with their start and end apart: 5, of which 2 were waited for; matrix products, arithmetic and copies ran while one was open for 13% of the time, Pallas kernels for 32%

profile of v5, /device:TPU:0, one launch (start us, length us, event | category | flops | bytes accessed | tf_op | source)
XLA Modules:
  0.0 214.1 jit_solution(16132646600009351971)
XLA Ops:
  7.2 0.0 copy-start.5
  7.2 0.0 copy-start.6
  7.2 0.0 copy-start.2
  7.2 0.0 all-gather.6.cloned.1.call-start
  7.2 0.7 all-gather.6.cloned.1.call-update
  7.9 2.1 broadcast_select_fusion
  10.0 3.9 %collective-permute-start = (bf16[1,512,512]{2,1,0:T(8,128)(2,1)}, bf16[1,512,512]{2,1,0:T(8,128)(2,1)}, u32[]{:S(2)}, u32[]{:S(2)}) collective-permute-start(bf16[1,512,512]{2,1,0:T(8,128)(2,1)} %get-tuple-element.15), channel_id=1, source_target_pairs={{0,24},{8,0},{16,8},{24,16},{1,25},{9,1},{17,9},{25,17},{2,26},{10... | collective-permute-start | bytes 1572872 | tf_op jit(solution)/shard_map/ppermute | solution.py:23
  13.9 0.5 collective-permute-start.1
  14.4 0.6 collective-permute-start.2
  15.7 0.0 copy-done.5
  15.8 0.0 copy-done.6
  15.8 0.1 fusion.9
  15.9 0.0 copy-done.2
  15.9 0.5 select_reduce_fusion
  16.4 0.2 fusion.18
  16.7 0.3 fusion.8
  17.7 14.9 %shard_map.156 = (f32[1,10,512,1]{3,2,1,0:T(8,128)}, f32[1,10,512,1]{3,2,1,0:T(8,128)}, f32[1,512,2560]{2,1,0:T(8,128)}) custom-call(s32[1]{0:T(128)S(6)} %sub.83.t0_ref, bf16[1,512,2560]{2,1,0:T(8,128)(2,1)} %q_ref.3, bf16[1,512,512]{2,1,0:T(8,128)(2,1)} %refs_0_.1, bf16[1,512,512]{2,1,0:T(8,128)(2,1)} %refs_1_.1), custom_call_target="tpu_custom_call" | custom-call | flops 5368709120 | bytes 6291456 | tf_op jit(solution)/shard_map/pallas_call | solution.py:138
  32.6 0.0 collective-permute-done.refs_3_
  32.6 6.1 %collective-permute-done.1.refs_4_ = bf16[1,512,512]{2,1,0:T(8,128)(2,1)} collective-permute-done((bf16[1,512,512]{2,1,0:T(8,128)(2,1)S(1)}, bf16[1,512,512]{2,1,0:T(8,128)(2,1)}, u32[]{:S(2)}, u32[]{:S(2)}) %collective-permute-start.1) | collective-permute-done | bytes 524320 | tf_op jit(solution)/shard_map/ppermute | solution.py:23
  38.7 0.0 collective-permute-done.2.refs_5_
  38.7 0.0 copy-start
  38.7 54.2 %shard_map.157 = bf16[1,512,2560]{2,1,0:T(8,128)(2,1)} custom-call(s32[1]{0:T(128)S(6)} %sub.83.t0_ref, bf16[1,512,2560]{2,1,0:T(8,128)(2,1)} %q_ref.3, f32[1,10,512,1]{3,2,1,0:T(8,128)} %get-tuple-element.7.refs_0_, f32[1,10,512,1]{3,2,1,0:T(8,128)} %get-tuple-element.8.refs_1_, f32[1,512,2560]{2,1,0:T(8,128)} %get-tuple-element.9.refs_2_, ...), custom_call_target="tpu_custom_call" | custom-call | flops 8053063680 | bytes 6815744 | tf_op jit(solution)/shard_map/pallas_call | solution.py:138
  92.9 0.0 copy-start.3
  92.9 0.0 copy-start.4
  92.9 0.8 slice_bitcast_fusion.1
  93.8 15.7 %all-gather.1 = bf16[8,2,2560]{2,1,0:T(2,128)(2,1)S(1)} all-gather(bf16[1,2,2560]{2,1,0:T(2,128)(2,1)S(1)} %maximum_bitcast_fusion), channel_id=1, replica_groups=mesh['seq'=4,'vocab'=8] {'vocab'}, dimensions={0}, use_global_device_ids=true | all-gather | bytes 92160 | tf_op jit(solution)/shard_map/all_gather | solution.py:257
  109.5 0.0 copy-done
  109.5 0.4 fusion.27
  109.9 0.8 reshape.158
  110.7 7.9 %all-to-all-start = ((f32[8,2,2560]{2,1,0:T(2,128)}), f32[8,2,2560]{2,1,0:T(2,128)S(1)}, u32[]{:S(2)}, u32[]{:S(2)}) async-start(f32[8,2,2560]{2,1,0:T(2,128)} %reshape.158), calls=%async_computation | async-start | bytes 327680 | tf_op jit(solution)/shard_map/all_to_all | solution.py:262
  118.5 0.8 slice_bitcast_fusion.2
  119.3 13.3 %all-to-all-done = f32[8,2,2560]{2,1,0:T(2,128)S(1)} async-done(((f32[8,2,2560]{2,1,0:T(2,128)}), f32[8,2,2560]{2,1,0:T(2,128)S(1)}, u32[]{:S(2)}, u32[]{:S(2)}) %all-to-all-start) | async-done | bytes 163872 | tf_op jit(solution)/shard_map/all_to_all | solution.py:262
  132.6 0.1 reduce_sum.46
  132.7 0.0 copy-done.3
  132.7 0.2 fusion.24
  132.9 0.0 copy-done.4
  132.9 0.1 fusion.30
  133.0 14.1 %all-gather.2 = bf16[8,2,2560]{2,1,0:T(2,128)(2,1)S(1)} all-gather(bf16[1,2,2560]{2,1,0:T(2,128)(2,1)S(1)} %fusion.30), channel_id=1, replica_groups=mesh['seq'=4,'vocab'=8] {'vocab'}, dimensions={0}, use_global_device_ids=true | all-gather | bytes 92160 | tf_op jit(solution)/shard_map/all_gather | solution.py:27
  147.1 7.8 %all_gather.21 = bf16[64,2560]{1,0:T(8,128)(2,1)S(1)} all-gather(bf16[16,2560]{1,0:T(8,128)(2,1)S(1)} %reshape.167), channel_id=1, replica_groups=mesh['seq'=4,'vocab'=8] {'seq'}, dimensions={0}, use_global_device_ids=true | all-gather | bytes 409600 | tf_op jit(solution)/shard_map/all_gather | solution.py:28
  155.0 0.1 reshape.159
  155.1 0.1 slice.61
  155.2 18.1 %fusion.44 = (f32[40]{0:T(128)S(1)}, f32[40,8000]{1,0:T(8,128)S(1)}) fusion(bf16[8000,2560]{1,0:T(8,128)(2,1)} %param.25, bf16[8,2560]{1,0:T(8,128)(2,1)S(1)} %bitcast.65, bf16[32,2560]{1,0:T(8,128)(2,1)S(1)} %bitcast.64), kind=kOutput, calls=%fused_computation.75 | convolution fusion | flops 1639129600 | bytes 42444960 | tf_op jit(solution)/shard_map/dot_general | solution.py:272
  173.3 0.4 exponential_reduce_fusion
  173.7 9.3 %all-gather.3 = f32[8,2,40]{2,1,0:T(2,128)S(1)} all-gather(f32[1,2,40]{2,1,0:T(2,128)S(1)} %maximum_bitcast_fusion.1), channel_id=2, replica_groups=mesh['seq'=4,'vocab'=8] {'vocab'}, dimensions={0}, use_global_device_ids=true | all-gather | bytes 2880 | tf_op jit(solution)/shard_map/all_gather | solution.py:27
  183.0 8.6 %all_gather.23 = f32[32,2,40]{2,1,0:T(2,128)S(1)} all-gather(f32[8,2,40]{2,1,0:T(2,128)S(1)} %all-gather.3), channel_id=1, replica_groups=mesh['seq'=4,'vocab'=8] {'seq'}, dimensions={0}, use_global_device_ids=true | all-gather | bytes 12800 | tf_op jit(solution)/shard_map/all_gather | solution.py:28
  191.7 0.1 subtract_convert_fusion
  191.9 0.8 slice.64
  192.7 0.7 slice.65
  193.3 0.0 all-gather.6.cloned.1.call-done
  193.3 0.0 copy-start.1
  193.3 11.0 %fusion.2 = f32[513,2560]{1,0:T(8,128)S(1)} fusion(bf16[2560,2560]{1,0:T(8,128)(2,1)} %all-gather.6.cloned.1.call-done, bf16[1,2560]{1,0:T(2,128)(2,1)S(1)} %bitcast.70, bf16[512,2560]{1,0:T(8,128)(2,1)} %bitcast.74), kind=kOutput, calls=%fused_computation.3 | convolution fusion | flops 6729246720 | bytes 20986880 | tf_op jit(solution)/shard_map/dot_general | solution.py:240
  204.4 0.0 copy-done.1
  204.4 2.3 %fusion.1 = bf16[1,512,2560]{2,1,0:T(8,128)(2,1)} fusion(f32[513,2560]{1,0:T(8,128)S(1)} %fusion.2, bf16[1,512,2560]{2,1,0:T(8,128)(2,1)S(1)} %copy-done.1), kind=kLoop, calls=%fused_computation.2 | loop fusion | flops 3932160 | bytes 10485760 | tf_op jit(solution)/shard_map/convert_element_type | solution.py:248
  206.7 0.6 fusion.29
  (19 shorter events, 0.4 us)
Async XLA Ops:
  7.2 8.5 %copy-start.5 = (bf16[1,2560]{1,0:T(2,128)(2,1)S(1)}, bf16[1,2560]{1,0:T(2,128)(2,1)}, u32[]{:S(2)}) copy-start(bf16[1,2560]{1,0:T(2,128)(2,1)} %param.18) | copy-start | bytes 15364
  7.2 8.6 %copy-start.6 = (bf16[1,512]{1,0:T(2,128)(2,1)S(1)}, bf16[1,512]{1,0:T(2,128)(2,1)}, u32[]{:S(2)}) copy-start(bf16[1,512]{1,0:T(2,128)(2,1)} %param.19) | copy-start | bytes 3076
  7.2 8.7 %copy-start.2 = (bf16[1,2048,512]{2,1,0:T(8,128)(2,1)S(1)}, bf16[1,2048,512]{2,1,0:T(8,128)(2,1)}, u32[]{:S(2)}) copy-start(bf16[1,2048,512]{2,1,0:T(8,128)(2,1)} %param.20) | copy-start | bytes 6291460
  7.2 186.2 %all-gather.6.cloned.1.call-start = ((), (), s32[]{:S(2)}) async-start(), calls=%async_computation.1 | async-start | bytes 14745600 | tf_op jit(solution)/shard_map/all_gather | solution.py:242
  10.0 22.6 %collective-permute-start = (bf16[1,512,512]{2,1,0:T(8,128)(2,1)}, bf16[1,512,512]{2,1,0:T(8,128)(2,1)}, u32[]{:S(2)}, u32[]{:S(2)}) collective-permute-start(bf16[1,512,512]{2,1,0:T(8,128)(2,1)} %get-tuple-element.15), channel_id=1, source_target_pairs={{0,24},{8,0},{16,8},{24,16},{1,25},{9,1},{17,9},{25,17},{2,26},{10... | collective-permute-start | bytes 1572872 | tf_op jit(solution)/shard_map/ppermute | solution.py:23
  13.9 24.7 %collective-permute-start.1 = (bf16[1,512,512]{2,1,0:T(8,128)(2,1)S(1)}, bf16[1,512,512]{2,1,0:T(8,128)(2,1)}, u32[]{:S(2)}, u32[]{:S(2)}) collective-permute-start(bf16[1,512,512]{2,1,0:T(8,128)(2,1)S(1)} %get-tuple-element.16), channel_id=1, source_target_pairs={{0,16},{8,24},{16,0},{24,8},{1,17},{9,25},{17,1},{25,9},{2,18},{10... | collective-permute-start | bytes 1572872 | tf_op jit(solution)/shard_map/ppermute | solution.py:23
  14.4 24.2 %collective-permute-start.2 = (bf16[1,512,512]{2,1,0:T(8,128)(2,1)S(1)}, bf16[1,512,512]{2,1,0:T(8,128)(2,1)}, u32[]{:S(2)}, u32[]{:S(2)}) collective-permute-start(bf16[1,512,512]{2,1,0:T(8,128)(2,1)S(1)} %get-tuple-element.14), channel_id=1, source_target_pairs={{0,8},{8,16},{16,24},{24,0},{1,9},{9,17},{17,25},{25,1},{2,10},{10... | collective-permute-start | bytes 1572872 | tf_op jit(solution)/shard_map/ppermute | solution.py:23
  38.7 70.8 %copy-start = (bf16[320,2560]{1,0:T(8,128)(2,1)S(1)}, bf16[320,2560]{1,0:T(8,128)(2,1)}, u32[]{:S(2)}) copy-start(bf16[320,2560]{1,0:T(8,128)(2,1)} %param.23) | copy-start | bytes 4915204
  92.9 39.8 %copy-start.3 = (bf16[1,2560]{1,0:T(2,128)(2,1)S(1)}, bf16[1,2560]{1,0:T(2,128)(2,1)}, u32[]{:S(2)}) copy-start(bf16[1,2560]{1,0:T(2,128)(2,1)} %param.22) | copy-start | bytes 15364
  92.9 40.0 %copy-start.4 = (f32[2560]{0:T(1024)S(1)}, f32[2560]{0:T(1024)}, u32[]{:S(2)}) copy-start(f32[2560]{0:T(1024)} %param.24) | copy-start | bytes 30724
  110.7 22.0 %all-to-all-start = ((f32[8,2,2560]{2,1,0:T(2,128)}), f32[8,2,2560]{2,1,0:T(2,128)S(1)}, u32[]{:S(2)}, u32[]{:S(2)}) async-start(f32[8,2,2560]{2,1,0:T(2,128)} %reshape.158), calls=%async_computation | async-start | bytes 327680 | tf_op jit(solution)/shard_map/all_to_all | solution.py:262
  193.3 11.0 %copy-start.1 = (bf16[1,512,2560]{2,1,0:T(8,128)(2,1)S(1)}, bf16[1,512,2560]{2,1,0:T(8,128)(2,1)}, u32[]{:S(2)}) copy-start(bf16[1,512,2560]{2,1,0:T(8,128)(2,1)} %param.17) | copy-start | bytes 7864324
Sparse Core Ops, SparseCore 0:
  9.7 127.8 all-gather.5

commit v6 on v5

--- a/solution.py
+++ b/solution.py
@@ -92,12 +92,7 @@
                 valid = valid & (t <= row + WIN)
             return absorb(state, valid)
 
-        if j == 0 or j == n_blocks - 1:
-            state = masked(state)
-        else:
-            state = lax.cond(
-                t0 <= j * block, lambda st: absorb(st, None), masked, state
-            )
+        state = masked(state)
     peak, denom, accum = state
     if final:
         out_refs[0][0] = (accum / denom).astype(out_refs[0].dtype)

time: 212 us -> 200 us (0.943); the launches traced: 214 us -> 200 us
  Pallas kernels: 69.2 us -> 56.1 us
  blocking collectives: 55.6 us -> 62 us
  starting transfers between devices: 12.9 us -> 8.41 us
  waiting for transfers between devices: 20 us -> 17 us
    pallas_call x2, Pallas kernels: 69.2 us -> 56.1 us  [prefill_pass(): pl.pallas_call(kernel, out_shape=out_shape, grid_spec=pltpu.PrefetchScala...]
    all_to_all x1, starting transfers between devices: 7.87 us -> 3.38 us  [body(): lax.all_to_all(partial.reshape(vocab_count, head_count, D), 'vocab', 0, 0...]
    all_gather x1, blocking collectives: 15.7 us -> 19.4 us  [body(): group_rows = lax.all_gather(head_mixed, 'vocab', axis=0, tiled=True)]
    all_to_all x1, waiting for transfers between devices: 13.3 us -> 10.3 us  [body(): lax.all_to_all(partial.reshape(vocab_count, head_count, D), 'vocab', 0, 0...]
  transfers between devices with their start and end apart: 5 -> 5, of which waited for: 2 -> 2; matrix products, arithmetic and copies ran while one was open for 13% -> 13% of each run, Pallas kernels for 32% -> 28%
where the time goes in v6:
time: 200 us
  blocking collectives  62 us (31%)
  Pallas kernels  56.1 us (28%)
  matrix products  30.4 us (15%)
  waiting for transfers between devices  17 us (8%)
  between operations  15.6 us (8%)
  starting transfers between devices  8.41 us (4%)
  other arithmetic  6.23 us (3%)
  local copies, waits for them, and re-layouts  4.25 us (2%)
    pallas_call x2, Pallas kernels, prefill_pass(): pl.pallas_call(kernel, out_shape=out_shape, grid_spec=pltpu.PrefetchScala...  56.1 us
    all_gather x2, blocking collectives, gather_all(): inner = lax.all_gather(value, 'vocab', axis=0, tiled=True)  25.2 us
    all_gather x1, blocking collectives, body(): group_rows = lax.all_gather(head_mixed, 'vocab', axis=0, tiled=True)  19.4 us
    dot_general x1, matrix products, body(): lax.dot_general(head_rows, embedding, (((1,), (1,)), ((), ())), preferred...  18.1 us
    all_gather x2, blocking collectives, gather_all(): return lax.all_gather(inner, 'seq', axis=0, tiled=True)  17.4 us
    dot_general x1, matrix products, body(): jnp.dot(mixed_rows, lax.all_gather(out_weight, 'vocab', axis=0, tiled=Tru...  11 us
    all_to_all x1, waiting for transfers between devices, body(): lax.all_to_all(partial.reshape(vocab_count, head_count, D), 'vocab', 0, 0...  10.3 us
    ppermute x3, waiting for transfers between devices, from_behind(): return lax.ppermute(value, axis, pairs)  6.06 us
  transfers between devices with their start and end apart: 5, of which 2 were waited for; matrix products, arithmetic and copies ran while one was open for 13% of the time, Pallas kernels for 28%

profile of v6, /device:TPU:0, one launch (start us, length us, event | category | flops | bytes accessed | tf_op | source)
XLA Modules:
  0.0 200.0 jit_solution(7104040618849468083)
XLA Ops:
  7.2 0.0 copy-start.5
  7.2 0.0 copy-start.6
  7.2 0.0 copy-start.2
  7.2 0.0 all-gather.6.cloned.1.call-start
  7.2 0.7 all-gather.6.cloned.1.call-update
  7.9 2.1 %broadcast_select_fusion = (bf16[1,512,512]{2,1,0:T(8,128)(2,1)S(1)}, bf16[1,512,512]{2,1,0:T(8,128)(2,1)}, bf16[1,512,512]{2,1,0:T(8,128)(2,1)S(1)}) fusion(bf16[1,512,512]{2,1,0:T(8,128)(2,1)} %refs_1_.1, bf16[1,512,512]{2,1,0:T(8,128)(2,1)} %refs_0_.1, pred[]{:T(512)S(6)} %le.11, pred[]{:T(512)S(6)} %le.9, pred[]{:T(512)S(6)} %le.10), kind=kLoop, calls=%fused_computation.20 | loop fusion | flops 786432 | bytes 2621443 | tf_op jit(solution)/shard_map/jit(_where)/select_n | solution.py:189
  10.0 3.9 %collective-permute-start = (bf16[1,512,512]{2,1,0:T(8,128)(2,1)}, bf16[1,512,512]{2,1,0:T(8,128)(2,1)}, u32[]{:S(2)}, u32[]{:S(2)}) collective-permute-start(bf16[1,512,512]{2,1,0:T(8,128)(2,1)} %get-tuple-element.15), channel_id=1, source_target_pairs={{0,24},{8,0},{16,8},{24,16},{1,25},{9,1},{17,9},{25,17},{2,26},{10... | collective-permute-start | bytes 1572872 | tf_op jit(solution)/shard_map/ppermute | solution.py:23
  13.9 0.5 collective-permute-start.1
  14.4 0.6 collective-permute-start.2
  15.7 0.0 copy-done.5
  15.8 0.0 copy-done.6
  15.8 0.1 fusion.9
  15.9 0.0 copy-done.2
  15.9 0.5 select_reduce_fusion
  16.4 0.2 fusion.18
  16.7 0.3 fusion.8
  17.7 14.9 %shard_map.156 = (f32[1,10,512,1]{3,2,1,0:T(8,128)}, f32[1,10,512,1]{3,2,1,0:T(8,128)}, f32[1,512,2560]{2,1,0:T(8,128)}) custom-call(s32[1]{0:T(128)S(6)} %sub.83.t0_ref, bf16[1,512,2560]{2,1,0:T(8,128)(2,1)} %q_ref.3, bf16[1,512,512]{2,1,0:T(8,128)(2,1)} %refs_0_.1, bf16[1,512,512]{2,1,0:T(8,128)(2,1)} %refs_1_.1), custom_call_target="tpu_custom_call" | custom-call | flops 5368709120 | bytes 6291456 | tf_op jit(solution)/shard_map/pallas_call | solution.py:133
  32.6 0.0 collective-permute-done.refs_3_
  32.6 6.1 %collective-permute-done.1.refs_4_ = bf16[1,512,512]{2,1,0:T(8,128)(2,1)} collective-permute-done((bf16[1,512,512]{2,1,0:T(8,128)(2,1)S(1)}, bf16[1,512,512]{2,1,0:T(8,128)(2,1)}, u32[]{:S(2)}, u32[]{:S(2)}) %collective-permute-start.1) | collective-permute-done | bytes 524320 | tf_op jit(solution)/shard_map/ppermute | solution.py:23
  38.7 0.0 collective-permute-done.2.refs_5_
  38.7 0.0 copy-start
  38.7 41.2 %shard_map.157 = bf16[1,512,2560]{2,1,0:T(8,128)(2,1)} custom-call(s32[1]{0:T(128)S(6)} %sub.83.t0_ref, bf16[1,512,2560]{2,1,0:T(8,128)(2,1)} %q_ref.3, f32[1,10,512,1]{3,2,1,0:T(8,128)} %get-tuple-element.7.refs_0_, f32[1,10,512,1]{3,2,1,0:T(8,128)} %get-tuple-element.8.refs_1_, f32[1,512,2560]{2,1,0:T(8,128)} %get-tuple-element.9.refs_2_, ...), custom_call_target="tpu_custom_call" | custom-call | flops 8053063680 | bytes 6815744 | tf_op jit(solution)/shard_map/pallas_call | solution.py:133
  79.8 0.0 copy-start.3
  79.8 0.0 copy-start.4
  79.8 0.8 slice_bitcast_fusion.1
  80.7 19.4 %all-gather.1 = bf16[8,2,2560]{2,1,0:T(2,128)(2,1)S(1)} all-gather(bf16[1,2,2560]{2,1,0:T(2,128)(2,1)S(1)} %maximum_bitcast_fusion), channel_id=1, replica_groups=mesh['seq'=4,'vocab'=8] {'vocab'}, dimensions={0}, use_global_device_ids=true | all-gather | bytes 92160 | tf_op jit(solution)/shard_map/all_gather | solution.py:252
  100.1 0.0 copy-done
  100.1 0.4 fusion.27
  100.5 0.8 reshape.158
  101.3 3.4 %all-to-all-start = ((f32[8,2,2560]{2,1,0:T(2,128)}), f32[8,2,2560]{2,1,0:T(2,128)S(1)}, u32[]{:S(2)}, u32[]{:S(2)}) async-start(f32[8,2,2560]{2,1,0:T(2,128)} %reshape.158), calls=%async_computation | async-start | bytes 327680 | tf_op jit(solution)/shard_map/all_to_all | solution.py:257
  104.7 0.8 slice_bitcast_fusion.2
  105.5 10.3 %all-to-all-done = f32[8,2,2560]{2,1,0:T(2,128)S(1)} async-done(((f32[8,2,2560]{2,1,0:T(2,128)}), f32[8,2,2560]{2,1,0:T(2,128)S(1)}, u32[]{:S(2)}, u32[]{:S(2)}) %all-to-all-start) | async-done | bytes 163872 | tf_op jit(solution)/shard_map/all_to_all | solution.py:257
  115.7 0.1 reduce_sum.46
  115.8 0.0 copy-done.3
  115.8 0.2 fusion.24
  115.9 0.0 copy-done.4
  115.9 0.1 fusion.30
  116.0 14.1 %all-gather.2 = bf16[8,2,2560]{2,1,0:T(2,128)(2,1)S(1)} all-gather(bf16[1,2,2560]{2,1,0:T(2,128)(2,1)S(1)} %fusion.30), channel_id=1, replica_groups=mesh['seq'=4,'vocab'=8] {'vocab'}, dimensions={0}, use_global_device_ids=true | all-gather | bytes 92160 | tf_op jit(solution)/shard_map/all_gather | solution.py:27
  130.2 9.2 %all_gather.21 = bf16[64,2560]{1,0:T(8,128)(2,1)S(1)} all-gather(bf16[16,2560]{1,0:T(8,128)(2,1)S(1)} %reshape.167), channel_id=1, replica_groups=mesh['seq'=4,'vocab'=8] {'seq'}, dimensions={0}, use_global_device_ids=true | all-gather | bytes 409600 | tf_op jit(solution)/shard_map/all_gather | solution.py:28
  139.4 0.1 reshape.159
  139.5 0.1 slice.61
  139.7 18.1 %fusion.44 = (f32[40]{0:T(128)S(1)}, f32[40,8000]{1,0:T(8,128)S(1)}) fusion(bf16[8000,2560]{1,0:T(8,128)(2,1)} %param.25, bf16[8,2560]{1,0:T(8,128)(2,1)S(1)} %bitcast.65, bf16[32,2560]{1,0:T(8,128)(2,1)S(1)} %bitcast.64), kind=kOutput, calls=%fused_computation.75 | convolution fusion | flops 1639129600 | bytes 42444960 | tf_op jit(solution)/shard_map/dot_general | solution.py:267
  157.7 0.4 exponential_reduce_fusion
  158.1 11.1 %all-gather.3 = f32[8,2,40]{2,1,0:T(2,128)S(1)} all-gather(f32[1,2,40]{2,1,0:T(2,128)S(1)} %maximum_bitcast_fusion.1), channel_id=2, replica_groups=mesh['seq'=4,'vocab'=8] {'vocab'}, dimensions={0}, use_global_device_ids=true | all-gather | bytes 2880 | tf_op jit(solution)/shard_map/all_gather | solution.py:27
  169.2 8.2 %all_gather.23 = f32[32,2,40]{2,1,0:T(2,128)S(1)} all-gather(f32[8,2,40]{2,1,0:T(2,128)S(1)} %all-gather.3), channel_id=1, replica_groups=mesh['seq'=4,'vocab'=8] {'seq'}, dimensions={0}, use_global_device_ids=true | all-gather | bytes 12800 | tf_op jit(solution)/shard_map/all_gather | solution.py:28
  177.6 0.1 subtract_convert_fusion
  177.7 0.8 slice.64
  178.5 0.7 slice.65
  179.2 0.0 all-gather.6.cloned.1.call-done
  179.2 0.0 copy-start.1
  179.2 11.0 %fusion.2 = f32[513,2560]{1,0:T(8,128)S(1)} fusion(bf16[2560,2560]{1,0:T(8,128)(2,1)} %all-gather.6.cloned.1.call-done, bf16[1,2560]{1,0:T(2,128)(2,1)S(1)} %bitcast.70, bf16[512,2560]{1,0:T(8,128)(2,1)} %bitcast.74), kind=kOutput, calls=%fused_computation.3 | convolution fusion | flops 6729246720 | bytes 20986880 | tf_op jit(solution)/shard_map/dot_general | solution.py:235
  190.2 0.0 copy-done.1
  190.2 2.3 %fusion.1 = bf16[1,512,2560]{2,1,0:T(8,128)(2,1)} fusion(f32[513,2560]{1,0:T(8,128)S(1)} %fusion.2, bf16[1,512,2560]{2,1,0:T(8,128)(2,1)S(1)} %copy-done.1), kind=kLoop, calls=%fused_computation.2 | loop fusion | flops 3932160 | bytes 10485760 | tf_op jit(solution)/shard_map/convert_element_type | solution.py:243
  192.5 0.6 fusion.29
  (19 shorter events, 0.4 us)
Async XLA Ops:
  7.2 8.5 %copy-start.5 = (bf16[1,2560]{1,0:T(2,128)(2,1)S(1)}, bf16[1,2560]{1,0:T(2,128)(2,1)}, u32[]{:S(2)}) copy-start(bf16[1,2560]{1,0:T(2,128)(2,1)} %param.18) | copy-start | bytes 15364
  7.2 8.6 %copy-start.6 = (bf16[1,512]{1,0:T(2,128)(2,1)S(1)}, bf16[1,512]{1,0:T(2,128)(2,1)}, u32[]{:S(2)}) copy-start(bf16[1,512]{1,0:T(2,128)(2,1)} %param.19) | copy-start | bytes 3076
  7.2 8.7 %copy-start.2 = (bf16[1,2048,512]{2,1,0:T(8,128)(2,1)S(1)}, bf16[1,2048,512]{2,1,0:T(8,128)(2,1)}, u32[]{:S(2)}) copy-start(bf16[1,2048,512]{2,1,0:T(8,128)(2,1)} %param.20) | copy-start | bytes 6291460
  7.2 172.0 %all-gather.6.cloned.1.call-start = ((), (), s32[]{:S(2)}) async-start(), calls=%async_computation.1 | async-start | bytes 14745600 | tf_op jit(solution)/shard_map/all_gather | solution.py:237
  10.0 22.6 %collective-permute-start = (bf16[1,512,512]{2,1,0:T(8,128)(2,1)}, bf16[1,512,512]{2,1,0:T(8,128)(2,1)}, u32[]{:S(2)}, u32[]{:S(2)}) collective-permute-start(bf16[1,512,512]{2,1,0:T(8,128)(2,1)} %get-tuple-element.15), channel_id=1, source_target_pairs={{0,24},{8,0},{16,8},{24,16},{1,25},{9,1},{17,9},{25,17},{2,26},{10... | collective-permute-start | bytes 1572872 | tf_op jit(solution)/shard_map/ppermute | solution.py:23
  13.9 24.7 %collective-permute-start.1 = (bf16[1,512,512]{2,1,0:T(8,128)(2,1)S(1)}, bf16[1,512,512]{2,1,0:T(8,128)(2,1)}, u32[]{:S(2)}, u32[]{:S(2)}) collective-permute-start(bf16[1,512,512]{2,1,0:T(8,128)(2,1)S(1)} %get-tuple-element.16), channel_id=1, source_target_pairs={{0,16},{8,24},{16,0},{24,8},{1,17},{9,25},{17,1},{25,9},{2,18},{10... | collective-permute-start | bytes 1572872 | tf_op jit(solution)/shard_map/ppermute | solution.py:23
  14.4 24.2 %collective-permute-start.2 = (bf16[1,512,512]{2,1,0:T(8,128)(2,1)S(1)}, bf16[1,512,512]{2,1,0:T(8,128)(2,1)}, u32[]{:S(2)}, u32[]{:S(2)}) collective-permute-start(bf16[1,512,512]{2,1,0:T(8,128)(2,1)S(1)} %get-tuple-element.14), channel_id=1, source_target_pairs={{0,8},{8,16},{16,24},{24,0},{1,9},{9,17},{17,25},{25,1},{2,10},{10... | collective-permute-start | bytes 1572872 | tf_op jit(solution)/shard_map/ppermute | solution.py:23
  38.7 61.4 %copy-start = (bf16[320,2560]{1,0:T(8,128)(2,1)S(1)}, bf16[320,2560]{1,0:T(8,128)(2,1)}, u32[]{:S(2)}) copy-start(bf16[320,2560]{1,0:T(8,128)(2,1)} %param.23) | copy-start | bytes 4915204
  79.8 35.9 %copy-start.3 = (bf16[1,2560]{1,0:T(2,128)(2,1)S(1)}, bf16[1,2560]{1,0:T(2,128)(2,1)}, u32[]{:S(2)}) copy-start(bf16[1,2560]{1,0:T(2,128)(2,1)} %param.22) | copy-start | bytes 15364
  79.8 36.1 %copy-start.4 = (f32[2560]{0:T(1024)S(1)}, f32[2560]{0:T(1024)}, u32[]{:S(2)}) copy-start(f32[2560]{0:T(1024)} %param.24) | copy-start | bytes 30724
  101.3 14.4 %all-to-all-start = ((f32[8,2,2560]{2,1,0:T(2,128)}), f32[8,2,2560]{2,1,0:T(2,128)S(1)}, u32[]{:S(2)}, u32[]{:S(2)}) async-start(f32[8,2,2560]{2,1,0:T(2,128)} %reshape.158), calls=%async_computation | async-start | bytes 327680 | tf_op jit(solution)/shard_map/all_to_all | solution.py:257
  179.2 11.0 %copy-start.1 = (bf16[1,512,2560]{2,1,0:T(8,128)(2,1)S(1)}, bf16[1,512,2560]{2,1,0:T(8,128)(2,1)}, u32[]{:S(2)}) copy-start(bf16[1,512,2560]{2,1,0:T(8,128)(2,1)} %param.17) | copy-start | bytes 7864324
Sparse Core Ops, SparseCore 0:
  9.7 128.4 all-gather.5

commit v7 on v3

--- a/solution.py
+++ b/solution.py
@@ -58,15 +58,18 @@
             * scale
         )
         t = j * block + col
-        valid = t >= t0
-        if j == 0:
-            valid = valid & (t > row)
-        if j == n_blocks - 1:
-            valid = valid & (t <= row + WIN)
-        peak_new = jnp.maximum(
-            peak, jnp.max(jnp.where(valid, scores, NEG_BIG), axis=1, keepdims=True)
-        )
-        weights = jnp.where(valid, jnp.exp(scores - peak_new), 0.0)
+        if j == 0 or j == n_blocks - 1:
+            valid = t >= t0
+            if j == 0:
+                valid = valid & (t > row)
+            else:
+                valid = valid & (t <= row + WIN)
+            scores = jnp.where(valid, scores, NEG_BIG)
+        else:
+            key = j * block + lax.broadcasted_iota(jnp.int32, (1, block), 1)
+            scores = scores + jnp.where(key >= t0, 0.0, NEG_BIG)
+        peak_new = jnp.maximum(peak, jnp.max(scores, axis=1, keepdims=True))
+        weights = jnp.exp(scores - peak_new)
         decay = jnp.exp(peak - peak_new)
         denom = denom * decay + jnp.sum(weights, axis=1, keepdims=True)
         accum = accum * decay + jnp.dot(

time: 191 us -> 186 us (0.974)
  blocking collectives: 56.5 us -> 62 us
  waiting for transfers between devices: 35 us -> 30.4 us
  Pallas kernels: 29.6 us -> 26.8 us
  starting transfers between devices: 12.4 us -> 9.72 us
    all_to_all x1, waiting for transfers between devices: 13.3 us -> 8.73 us  [body(): lax.all_to_all(partial.reshape(vocab_count, head_count, D), 'vocab', 0, 0...]
    all_gather x2, blocking collectives: 25.6 us -> 28.9 us  [gather_all(): inner = lax.all_gather(value, 'vocab', axis=0, tiled=True)]
    pallas_call x1, Pallas kernels: 29.6 us -> 26.8 us  [prefill_attention(): pl.pallas_call(kernel, out_shape=jax.ShapeDtypeStruct(pre_query.shape, jn...]
    all_to_all x1, starting transfers between devices: 7.36 us -> 4.69 us  [body(): lax.all_to_all(partial.reshape(vocab_count, head_count, D), 'vocab', 0, 0...]
  transfers between devices with their start and end apart: 5 -> 5, of which waited for: 3 -> 3; matrix products, arithmetic and copies ran while one was open for 14% -> 15% of each run, Pallas kernels for 16% -> 14%
where the time goes in v7:
time: 186 us
  blocking collectives  62 us (33%)
  matrix products  30.7 us (17%)
  waiting for transfers between devices  30.4 us (16%)
  Pallas kernels  26.8 us (14%)
  between operations  15.6 us (8%)
  starting transfers between devices  9.72 us (5%)
  other arithmetic  6.23 us (3%)
  local copies, waits for them, and re-layouts  4.25 us (2%)
    all_gather x2, blocking collectives, gather_all(): inner = lax.all_gather(value, 'vocab', axis=0, tiled=True)  28.9 us
    pallas_call x1, Pallas kernels, prefill_attention(): pl.pallas_call(kernel, out_shape=jax.ShapeDtypeStruct(pre_query.shape, jn...  26.8 us
    ppermute x3, waiting for transfers between devices, from_behind(): return lax.ppermute(value, axis, pairs)  21 us
    dot_general x1, matrix products, body(): lax.dot_general(head_rows, embedding, (((1,), (1,)), ((), ())), preferred...  18.3 us
    all_gather x2, blocking collectives, gather_all(): return lax.all_gather(inner, 'seq', axis=0, tiled=True)  17.3 us
    all_gather x1, blocking collectives, body(): group_rows = lax.all_gather(head_mixed, 'vocab', axis=0, tiled=True)  15.8 us
    dot_general x1, matrix products, body(): jnp.dot(mixed_rows, lax.all_gather(out_weight, 'vocab', axis=0, tiled=Tru...  11 us
    all_to_all x1, waiting for transfers between devices, body(): lax.all_to_all(partial.reshape(vocab_count, head_count, D), 'vocab', 0, 0...  8.73 us
  transfers between devices with their start and end apart: 5, of which 3 were waited for; matrix products, arithmetic and copies ran while one was open for 15% of the time, Pallas kernels for 14%

profile of v7, /device:TPU:0, one launch (start us, length us, event | category | flops | bytes accessed | tf_op | source)
XLA Modules:
  0.0 185.6 jit_solution(8457499400795303860)
XLA Ops:
  7.2 0.0 copy-start.5
  7.2 0.0 copy-start.6
  7.2 0.0 copy-start.2
  7.2 0.0 all-gather.6.cloned.1.call-start
  7.2 0.7 all-gather.6.cloned.1.call-update
  7.9 2.1 %broadcast_select_fusion = (bf16[1,512,512]{2,1,0:T(8,128)(2,1)S(1)}, bf16[1,512,512]{2,1,0:T(8,128)(2,1)S(1)}, bf16[1,512,512]{2,1,0:T(8,128)(2,1)}) fusion(bf16[1,512,512]{2,1,0:T(8,128)(2,1)} %refs_4_.1, bf16[1,512,512]{2,1,0:T(8,128)(2,1)} %refs_0_.1, pred[]{:T(512)S(6)} %le.11, pred[]{:T(512)S(6)} %le.10, pred[]{:T(512)S(6)} %le.9), kind=kLoop, calls=%fused_computation.20 | loop fusion | flops 786432 | bytes 2621443 | tf_op jit(solution)/shard_map/jit(_where)/select_n | solution.py:135
  10.0 3.9 %collective-permute-start = (bf16[1,512,512]{2,1,0:T(8,128)(2,1)}, bf16[1,512,512]{2,1,0:T(8,128)(2,1)}, u32[]{:S(2)}, u32[]{:S(2)}) collective-permute-start(bf16[1,512,512]{2,1,0:T(8,128)(2,1)} %get-tuple-element.10), channel_id=1, source_target_pairs={{0,24},{8,0},{16,8},{24,16},{1,25},{9,1},{17,9},{25,17},{2,26},{10... | collective-permute-start | bytes 1572872 | tf_op jit(solution)/shard_map/ppermute | solution.py:23
  13.9 0.5 collective-permute-start.1
  14.4 0.6 collective-permute-start.2
  15.7 0.0 copy-done.5
  15.8 0.0 copy-done.6
  15.8 0.1 fusion.9
  15.9 0.0 copy-done.2
  15.9 0.5 select_reduce_fusion
  16.4 0.2 fusion.18
  16.7 0.3 fusion.8
  17.6 0.0 copy-start
  17.7 8.9 %collective-permute-done.refs_1_ = bf16[1,512,512]{2,1,0:T(8,128)(2,1)} collective-permute-done((bf16[1,512,512]{2,1,0:T(8,128)(2,1)}, bf16[1,512,512]{2,1,0:T(8,128)(2,1)}, u32[]{:S(2)}, u32[]{:S(2)}) %collective-permute-start) | collective-permute-done | bytes 524320 | tf_op jit(solution)/shard_map/ppermute | solution.py:23
  26.6 12.1 %collective-permute-done.1.refs_2_ = bf16[1,512,512]{2,1,0:T(8,128)(2,1)} collective-permute-done((bf16[1,512,512]{2,1,0:T(8,128)(2,1)S(1)}, bf16[1,512,512]{2,1,0:T(8,128)(2,1)}, u32[]{:S(2)}, u32[]{:S(2)}) %collective-permute-start.1) | collective-permute-done | bytes 524320 | tf_op jit(solution)/shard_map/ppermute | solution.py:23
  38.7 0.0 collective-permute-done.2.refs_3_
  38.7 26.8 %shard_map.156 = bf16[1,512,2560]{2,1,0:T(8,128)(2,1)} custom-call(s32[1]{0:T(128)S(6)} %sub.83.t0_ref, bf16[1,512,2560]{2,1,0:T(8,128)(2,1)} %q_ref.1, bf16[1,512,512]{2,1,0:T(8,128)(2,1)} %refs_0_.1, bf16[1,512,512]{2,1,0:T(8,128)(2,1)} %collective-permute-done.refs_1_, bf16[1,512,512]{2,1,0:T(8,128)(2,1)} %collective-permute-done.1.refs_2_, ...), custom_call_target="tpu_custom_call" | custom-call | flops 13421772800 | bytes 7864320 | tf_op jit(solution)/shard_map/pallas_call | solution.py:91
  65.4 0.0 copy-start.3
  65.4 0.0 copy-start.4
  65.4 0.8 slice_bitcast_fusion.1
  66.3 15.8 %all-gather.1 = bf16[8,2,2560]{2,1,0:T(2,128)(2,1)S(1)} all-gather(bf16[1,2,2560]{2,1,0:T(2,128)(2,1)S(1)} %maximum_bitcast_fusion), channel_id=1, replica_groups=mesh['seq'=4,'vocab'=8] {'vocab'}, dimensions={0}, use_global_device_ids=true | all-gather | bytes 92160 | tf_op jit(solution)/shard_map/all_gather | solution.py:198
  82.2 0.0 copy-done
  82.2 0.4 fusion.27
  82.6 0.8 reshape.158
  83.4 4.7 %all-to-all-start = ((f32[8,2,2560]{2,1,0:T(2,128)}), f32[8,2,2560]{2,1,0:T(2,128)S(1)}, u32[]{:S(2)}, u32[]{:S(2)}) async-start(f32[8,2,2560]{2,1,0:T(2,128)} %reshape.158), calls=%async_computation | async-start | bytes 327680 | tf_op jit(solution)/shard_map/all_to_all | solution.py:203
  88.0 0.8 slice_bitcast_fusion.2
  88.8 8.7 %all-to-all-done = f32[8,2,2560]{2,1,0:T(2,128)S(1)} async-done(((f32[8,2,2560]{2,1,0:T(2,128)}), f32[8,2,2560]{2,1,0:T(2,128)S(1)}, u32[]{:S(2)}, u32[]{:S(2)}) %all-to-all-start) | async-done | bytes 163872 | tf_op jit(solution)/shard_map/all_to_all | solution.py:203
  97.6 0.1 reduce_sum.46
  97.6 0.0 copy-done.3
  97.6 0.2 fusion.24
  97.8 0.0 copy-done.4
  97.8 0.1 fusion.30
  97.9 14.8 %all-gather.2 = bf16[8,2,2560]{2,1,0:T(2,128)(2,1)S(1)} all-gather(bf16[1,2,2560]{2,1,0:T(2,128)(2,1)S(1)} %fusion.30), channel_id=1, replica_groups=mesh['seq'=4,'vocab'=8] {'vocab'}, dimensions={0}, use_global_device_ids=true | all-gather | bytes 92160 | tf_op jit(solution)/shard_map/all_gather | solution.py:27
  112.8 8.7 %all_gather.21 = bf16[64,2560]{1,0:T(8,128)(2,1)S(1)} all-gather(bf16[16,2560]{1,0:T(8,128)(2,1)S(1)} %reshape.167), channel_id=1, replica_groups=mesh['seq'=4,'vocab'=8] {'seq'}, dimensions={0}, use_global_device_ids=true | all-gather | bytes 409600 | tf_op jit(solution)/shard_map/all_gather | solution.py:28
  121.4 0.1 reshape.159
  121.6 0.1 slice.61
  121.7 18.3 %fusion.44 = (f32[40]{0:T(128)S(1)}, f32[40,8000]{1,0:T(8,128)S(1)}) fusion(bf16[8000,2560]{1,0:T(8,128)(2,1)} %param.25, bf16[8,2560]{1,0:T(8,128)(2,1)S(1)} %bitcast.65, bf16[32,2560]{1,0:T(8,128)(2,1)S(1)} %bitcast.64), kind=kOutput, calls=%fused_computation.75 | convolution fusion | flops 1639129600 | bytes 42444960 | tf_op jit(solution)/shard_map/dot_general | solution.py:213
  140.0 0.4 exponential_reduce_fusion
  140.4 14.0 %all-gather.3 = f32[8,2,40]{2,1,0:T(2,128)S(1)} all-gather(f32[1,2,40]{2,1,0:T(2,128)S(1)} %maximum_bitcast_fusion.1), channel_id=2, replica_groups=mesh['seq'=4,'vocab'=8] {'vocab'}, dimensions={0}, use_global_device_ids=true | all-gather | bytes 2880 | tf_op jit(solution)/shard_map/all_gather | solution.py:27
  154.5 8.6 %all_gather.23 = f32[32,2,40]{2,1,0:T(2,128)S(1)} all-gather(f32[8,2,40]{2,1,0:T(2,128)S(1)} %all-gather.3), channel_id=1, replica_groups=mesh['seq'=4,'vocab'=8] {'seq'}, dimensions={0}, use_global_device_ids=true | all-gather | bytes 12800 | tf_op jit(solution)/shard_map/all_gather | solution.py:28
  163.2 0.1 subtract_convert_fusion
  163.4 0.8 slice.64
  164.2 0.7 slice.65
  164.8 0.0 all-gather.6.cloned.1.call-done
  164.8 0.0 copy-start.1
  164.8 11.0 %fusion.2 = f32[513,2560]{1,0:T(8,128)S(1)} fusion(bf16[2560,2560]{1,0:T(8,128)(2,1)} %all-gather.6.cloned.1.call-done, bf16[1,2560]{1,0:T(2,128)(2,1)S(1)} %bitcast.70, bf16[512,2560]{1,0:T(8,128)(2,1)} %bitcast.74), kind=kOutput, calls=%fused_computation.3 | convolution fusion | flops 6729246720 | bytes 20986880 | tf_op jit(solution)/shard_map/dot_general | solution.py:181
  175.9 0.0 copy-done.1
  175.9 2.3 %fusion.1 = bf16[1,512,2560]{2,1,0:T(8,128)(2,1)} fusion(f32[513,2560]{1,0:T(8,128)S(1)} %fusion.2, bf16[1,512,2560]{2,1,0:T(8,128)(2,1)S(1)} %copy-done.1), kind=kLoop, calls=%fused_computation.2 | loop fusion | flops 3932160 | bytes 10485760 | tf_op jit(solution)/shard_map/convert_element_type | solution.py:189
  178.2 0.6 fusion.29
  (19 shorter events, 0.4 us)
Async XLA Ops:
  7.2 8.5 %copy-start.5 = (bf16[1,2560]{1,0:T(2,128)(2,1)S(1)}, bf16[1,2560]{1,0:T(2,128)(2,1)}, u32[]{:S(2)}) copy-start(bf16[1,2560]{1,0:T(2,128)(2,1)} %param.18) | copy-start | bytes 15364
  7.2 8.6 %copy-start.6 = (bf16[1,512]{1,0:T(2,128)(2,1)S(1)}, bf16[1,512]{1,0:T(2,128)(2,1)}, u32[]{:S(2)}) copy-start(bf16[1,512]{1,0:T(2,128)(2,1)} %param.19) | copy-start | bytes 3076
  7.2 8.7 %copy-start.2 = (bf16[1,2048,512]{2,1,0:T(8,128)(2,1)S(1)}, bf16[1,2048,512]{2,1,0:T(8,128)(2,1)}, u32[]{:S(2)}) copy-start(bf16[1,2048,512]{2,1,0:T(8,128)(2,1)} %param.20) | copy-start | bytes 6291460
  7.2 157.6 %all-gather.6.cloned.1.call-start = ((), (), s32[]{:S(2)}) async-start(), calls=%async_computation.1 | async-start | bytes 14745600 | tf_op jit(solution)/shard_map/all_gather | solution.py:183
  10.0 16.5 %collective-permute-start = (bf16[1,512,512]{2,1,0:T(8,128)(2,1)}, bf16[1,512,512]{2,1,0:T(8,128)(2,1)}, u32[]{:S(2)}, u32[]{:S(2)}) collective-permute-start(bf16[1,512,512]{2,1,0:T(8,128)(2,1)} %get-tuple-element.10), channel_id=1, source_target_pairs={{0,24},{8,0},{16,8},{24,16},{1,25},{9,1},{17,9},{25,17},{2,26},{10... | collective-permute-start | bytes 1572872 | tf_op jit(solution)/shard_map/ppermute | solution.py:23
  13.9 24.7 %collective-permute-start.1 = (bf16[1,512,512]{2,1,0:T(8,128)(2,1)S(1)}, bf16[1,512,512]{2,1,0:T(8,128)(2,1)}, u32[]{:S(2)}, u32[]{:S(2)}) collective-permute-start(bf16[1,512,512]{2,1,0:T(8,128)(2,1)S(1)} %get-tuple-element.9), channel_id=1, source_target_pairs={{0,16},{8,24},{16,0},{24,8},{1,17},{9,25},{17,1},{25,9},{2,18},{10... | collective-permute-start | bytes 1572872 | tf_op jit(solution)/shard_map/ppermute | solution.py:23
  14.4 24.2 %collective-permute-start.2 = (bf16[1,512,512]{2,1,0:T(8,128)(2,1)S(1)}, bf16[1,512,512]{2,1,0:T(8,128)(2,1)}, u32[]{:S(2)}, u32[]{:S(2)}) collective-permute-start(bf16[1,512,512]{2,1,0:T(8,128)(2,1)S(1)} %get-tuple-element.8), channel_id=1, source_target_pairs={{0,8},{8,16},{16,24},{24,0},{1,9},{9,17},{17,25},{25,1},{2,10},{10... | collective-permute-start | bytes 1572872 | tf_op jit(solution)/shard_map/ppermute | solution.py:23
  17.6 64.5 %copy-start = (bf16[320,2560]{1,0:T(8,128)(2,1)S(1)}, bf16[320,2560]{1,0:T(8,128)(2,1)}, u32[]{:S(2)}) copy-start(bf16[320,2560]{1,0:T(8,128)(2,1)} %param.23) | copy-start | bytes 4915204
  65.4 32.2 %copy-start.3 = (bf16[1,2560]{1,0:T(2,128)(2,1)S(1)}, bf16[1,2560]{1,0:T(2,128)(2,1)}, u32[]{:S(2)}) copy-start(bf16[1,2560]{1,0:T(2,128)(2,1)} %param.22) | copy-start | bytes 15364
  65.4 32.4 %copy-start.4 = (f32[2560]{0:T(1024)S(1)}, f32[2560]{0:T(1024)}, u32[]{:S(2)}) copy-start(f32[2560]{0:T(1024)} %param.24) | copy-start | bytes 30724
  83.4 14.2 %all-to-all-start = ((f32[8,2,2560]{2,1,0:T(2,128)}), f32[8,2,2560]{2,1,0:T(2,128)S(1)}, u32[]{:S(2)}, u32[]{:S(2)}) async-start(f32[8,2,2560]{2,1,0:T(2,128)} %reshape.158), calls=%async_computation | async-start | bytes 327680 | tf_op jit(solution)/shard_map/all_to_all | solution.py:203
  164.8 11.0 %copy-start.1 = (bf16[1,512,2560]{2,1,0:T(8,128)(2,1)S(1)}, bf16[1,512,2560]{2,1,0:T(8,128)(2,1)}, u32[]{:S(2)}) copy-start(bf16[1,512,2560]{2,1,0:T(8,128)(2,1)} %param.17) | copy-start | bytes 7864324
Sparse Core Ops, SparseCore 0:
  9.7 128.4 all-gather.5

commit v8 on v7

--- a/solution.py
+++ b/solution.py
@@ -26,6 +26,31 @@
 def gather_all(value):
     inner = lax.all_gather(value, "vocab", axis=0, tiled=True)
     return lax.all_gather(inner, "seq", axis=0, tiled=True)
+
+
+def doubling_gather(value, axis, tie=None):
+    count = lax.axis_size(axis)
+    if count & (count - 1):
+        return lax.all_gather(value, axis, axis=0, tiled=True), tie
+    index = lax.axis_index(axis)
+    tie_out = None
+    step = 1
+    while step < count:
+        pairs = [(source, source ^ step) for source in range(count)]
+        theirs = lax.ppermute(value, axis, pairs)
+        if tie is not None:
+            theirs, tie = lax.optimization_barrier((theirs, tie))
+            tie_out, tie = tie, None
+        upper = (index // step) % 2 == 1
+        value = jnp.where(
+            upper,
+            jnp.concatenate([theirs, value], axis=0),
+            jnp.concatenate([value, theirs], axis=0),
+        )
+        step *= 2
+    if tie is not None:
+        return value, tie
+    return value, tie_out
 
 
 def normalize(rows_in, gain):
@@ -215,7 +240,9 @@
     )
     local_peak = jnp.max(logits, axis=1)
     local_sum = jnp.sum(jnp.exp(logits - local_peak[:, None]), axis=1)
-    stats = gather_all(jnp.stack([local_peak, local_sum])[None])
+    own_stats = jnp.stack([local_peak, local_sum])[None]
+    vocab_stats, (pre_out, dec_out) = doubling_gather(own_stats, "vocab", (pre_out, dec_out))
+    stats, _ = doubling_gather(vocab_stats, "seq")
     global_peak = jnp.max(stats[:, 0], axis=0)
     global_sum = jnp.sum(stats[:, 1] * jnp.exp(stats[:, 0] - global_peak[None]), axis=0)
     total = (global_peak + jnp.log(global_sum))[:, None]

time: 186 us -> 181 us (0.973)
  blocking collectives: 62 us -> 40.4 us
  starting transfers between devices: 9.72 us -> 20.8 us
  waiting for transfers between devices: 30.4 us -> 35.4 us
    all_gather x2 -> x1, blocking collectives: 28.9 us -> 14.9 us  [gather_all(): inner = lax.all_gather(value, 'vocab', axis=0, tiled=True)]
    ppermute x0 -> x5, starting transfers between devices: none -> 10.1 us  [doubling_gather(): theirs = lax.ppermute(value, axis, pairs)]
    all_gather x2 -> x1, blocking collectives: 17.3 us -> 8.83 us  [gather_all(): return lax.all_gather(inner, 'seq', axis=0, tiled=True)]
    ppermute x0 -> x5, waiting for transfers between devices: none -> 6.9 us  [doubling_gather(): theirs = lax.ppermute(value, axis, pairs)]
  transfers between devices with their start and end apart: 5 -> 10, of which waited for: 3 -> 8; matrix products, arithmetic and copies ran while one was open for 15% -> 22% of each run, Pallas kernels for 14% -> 15%
where the time goes in v8:
time: 181 us; the launch traced here: 180 us
  blocking collectives  40.4 us (22%)
  waiting for transfers between devices  35.4 us (20%)
  matrix products  30.7 us (17%)
  Pallas kernels  26.8 us (15%)
  starting transfers between devices  20.8 us (11%)
  between operations  15.6 us (9%)
  other arithmetic  6.27 us (3%)
  local copies, waits for them, and re-layouts  4.27 us (2%)
    pallas_call x1, Pallas kernels, prefill_attention(): pl.pallas_call(kernel, out_shape=jax.ShapeDtypeStruct(pre_query.shape, jn...  26.8 us
    ppermute x3, waiting for transfers between devices, from_behind(): return lax.ppermute(value, axis, pairs)  19.1 us
    dot_general x1, matrix products, body(): lax.dot_general(head_rows, embedding, (((1,), (1,)), ((), ())), preferred...  18.3 us
    all_gather x1, blocking collectives, body(): group_rows = lax.all_gather(head_mixed, 'vocab', axis=0, tiled=True)  16.7 us
    all_gather x1, blocking collectives, gather_all(): inner = lax.all_gather(value, 'vocab', axis=0, tiled=True)  14.9 us
    dot_general x1, matrix products, body(): jnp.dot(mixed_rows, lax.all_gather(out_weight, 'vocab', axis=0, tiled=Tru...  11 us
    ppermute x5, starting transfers between devices, doubling_gather(): theirs = lax.ppermute(value, axis, pairs)  10.1 us
    all_gather x1, blocking collectives, gather_all(): return lax.all_gather(inner, 'seq', axis=0, tiled=True)  8.83 us
  transfers between devices with their start and end apart: 10, of which 8 were waited for; matrix products, arithmetic and copies ran while one was open for 22% of the time, Pallas kernels for 15%

profile of v8, /device:TPU:0, one launch (start us, length us, event | category | flops | bytes accessed | tf_op | source)
XLA Modules:
  0.0 180.3 jit_solution(2792688331241111488)
XLA Ops:
  7.2 0.0 copy-start.5
  7.2 0.0 copy-start.6
  7.2 0.0 copy-start.2
  7.2 0.0 all-gather.4.cloned.1.call-start
  7.2 0.7 all-gather.4.cloned.1.call-update
  7.9 2.1 %broadcast_select_fusion = (bf16[1,512,512]{2,1,0:T(8,128)(2,1)}, bf16[1,512,512]{2,1,0:T(8,128)(2,1)S(1)}, bf16[1,512,512]{2,1,0:T(8,128)(2,1)S(1)}) fusion(bf16[1,512,512]{2,1,0:T(8,128)(2,1)} %refs_4_.1, bf16[1,512,512]{2,1,0:T(8,128)(2,1)} %refs_0_.1, pred[]{:T(512)S(6)} %le.11, pred[]{:T(512)S(6)} %le.10, pred[]{:T(512)S(6)} %le.9), kind=kLoop, calls=%fused_computation.20 | loop fusion | flops 786432 | bytes 2621443 | tf_op jit(solution)/shard_map/jit(_where)/select_n | solution.py:160
  10.0 2.9 %collective-permute-start.2 = (bf16[1,512,512]{2,1,0:T(8,128)(2,1)}, bf16[1,512,512]{2,1,0:T(8,128)(2,1)}, u32[]{:S(2)}, u32[]{:S(2)}) collective-permute-start(bf16[1,512,512]{2,1,0:T(8,128)(2,1)} %get-tuple-element.14), channel_id=1, source_target_pairs={{0,8},{8,16},{16,24},{24,0},{1,9},{9,17},{17,25},{25,1},{2,10},{10... | collective-permute-start | bytes 1572872 | tf_op jit(solution)/shard_map/ppermute | solution.py:23
  13.0 1.5 collective-permute-start.1
  14.5 1.4 collective-permute-start
  16.6 0.0 copy-done.5
  16.7 0.0 copy-done.6
  16.7 0.1 fusion.9
  16.8 0.0 copy-done.2
  16.8 0.5 select_reduce_fusion
  18.0 0.2 fusion.18
  18.2 0.3 fusion.8
  18.5 0.0 copy-start
  18.6 8.5 %collective-permute-done.2.refs_3_ = bf16[1,512,512]{2,1,0:T(8,128)(2,1)} collective-permute-done((bf16[1,512,512]{2,1,0:T(8,128)(2,1)}, bf16[1,512,512]{2,1,0:T(8,128)(2,1)}, u32[]{:S(2)}, u32[]{:S(2)}) %collective-permute-start.2) | collective-permute-done | bytes 524320 | tf_op jit(solution)/shard_map/ppermute | solution.py:23
  27.0 10.4 %collective-permute-done.1.refs_2_ = bf16[1,512,512]{2,1,0:T(8,128)(2,1)} collective-permute-done((bf16[1,512,512]{2,1,0:T(8,128)(2,1)S(1)}, bf16[1,512,512]{2,1,0:T(8,128)(2,1)}, u32[]{:S(2)}, u32[]{:S(2)}) %collective-permute-start.1) | collective-permute-done | bytes 524320 | tf_op jit(solution)/shard_map/ppermute | solution.py:23
  37.4 0.3 collective-permute-done.refs_1_
  37.7 26.8 %shard_map.156 = bf16[1,512,2560]{2,1,0:T(8,128)(2,1)} custom-call(s32[1]{0:T(128)S(6)} %sub.104.t0_ref, bf16[1,512,2560]{2,1,0:T(8,128)(2,1)} %q_ref.1, bf16[1,512,512]{2,1,0:T(8,128)(2,1)} %refs_0_.1, bf16[1,512,512]{2,1,0:T(8,128)(2,1)} %collective-permute-done.refs_1_, bf16[1,512,512]{2,1,0:T(8,128)(2,1)} %collective-permute-done.1.refs_2_, ...), custom_call_target="tpu_custom_call" | custom-call | flops 13421772800 | bytes 7864320 | tf_op jit(solution)/shard_map/pallas_call | solution.py:116
  64.5 0.0 copy-start.3
  64.5 0.0 copy-start.4
  64.5 0.8 slice_bitcast_fusion.1
  65.4 16.7 %all-gather = bf16[8,2,2560]{2,1,0:T(2,128)(2,1)S(1)} all-gather(bf16[1,2,2560]{2,1,0:T(2,128)(2,1)S(1)} %maximum_bitcast_fusion), channel_id=1, replica_groups=mesh['seq'=4,'vocab'=8] {'vocab'}, dimensions={0}, use_global_device_ids=true | all-gather | bytes 92160 | tf_op jit(solution)/shard_map/all_gather | solution.py:223
  82.1 0.0 copy-done
  82.1 0.4 fusion.27
  82.5 0.8 reshape.156
  83.3 4.7 %all-to-all-start = ((f32[8,2,2560]{2,1,0:T(2,128)}), f32[8,2,2560]{2,1,0:T(2,128)S(1)}, u32[]{:S(2)}, u32[]{:S(2)}) async-start(f32[8,2,2560]{2,1,0:T(2,128)} %reshape.156), calls=%async_computation | async-start | bytes 327680 | tf_op jit(solution)/shard_map/all_to_all | solution.py:228
  88.1 0.8 slice_bitcast_fusion.2
  88.9 8.6 %all-to-all-done = f32[8,2,2560]{2,1,0:T(2,128)S(1)} async-done(((f32[8,2,2560]{2,1,0:T(2,128)}), f32[8,2,2560]{2,1,0:T(2,128)S(1)}, u32[]{:S(2)}, u32[]{:S(2)}) %all-to-all-start) | async-done | bytes 163872 | tf_op jit(solution)/shard_map/all_to_all | solution.py:228
  97.5 0.1 reduce_sum.46
  97.5 0.0 copy-done.3
  97.5 0.2 fusion.24
  97.7 0.0 copy-done.4
  97.7 0.1 fusion.30
  97.8 14.9 %all-gather.1 = bf16[8,2,2560]{2,1,0:T(2,128)(2,1)S(1)} all-gather(bf16[1,2,2560]{2,1,0:T(2,128)(2,1)S(1)} %fusion.30), channel_id=1, replica_groups=mesh['seq'=4,'vocab'=8] {'vocab'}, dimensions={0}, use_global_device_ids=true | all-gather | bytes 92160 | tf_op jit(solution)/shard_map/all_gather | solution.py:27
  112.8 8.8 %all_gather.14 = bf16[64,2560]{1,0:T(8,128)(2,1)S(1)} all-gather(bf16[16,2560]{1,0:T(8,128)(2,1)S(1)} %reshape.166), channel_id=1, replica_groups=mesh['seq'=4,'vocab'=8] {'seq'}, dimensions={0}, use_global_device_ids=true | all-gather | bytes 409600 | tf_op jit(solution)/shard_map/all_gather | solution.py:28
  121.6 0.1 reshape.157
  121.7 0.1 slice.59
  121.9 18.3 %fusion.44 = (f32[40]{0:T(128)S(1)}, f32[40,8000]{1,0:T(8,128)S(1)}) fusion(bf16[8000,2560]{1,0:T(8,128)(2,1)} %param.25, bf16[8,2560]{1,0:T(8,128)(2,1)S(1)} %bitcast.65, bf16[32,2560]{1,0:T(8,128)(2,1)S(1)} %bitcast.64), kind=kOutput, calls=%fused_computation.80 | convolution fusion | flops 1639129600 | bytes 42444960 | tf_op jit(solution)/shard_map/dot_general | solution.py:238
  140.2 0.4 exponential_reduce_fusion
  140.6 0.1 collective-permute-start.3
  140.7 0.0 all-gather.4.cloned.1.call-done
  140.7 0.0 copy-start.1
  140.7 11.0 %fusion.2 = f32[513,2560]{1,0:T(8,128)S(1)} fusion(bf16[2560,2560]{1,0:T(8,128)(2,1)} %all-gather.4.cloned.1.call-done, bf16[1,2560]{1,0:T(2,128)(2,1)S(1)} %bitcast.70, bf16[512,2560]{1,0:T(8,128)(2,1)} %bitcast.74), kind=kOutput, calls=%fused_computation.3 | convolution fusion | flops 6729246720 | bytes 20986880 | tf_op jit(solution)/shard_map/dot_general | solution.py:206
  151.7 0.0 copy-done.1
  151.8 2.3 %fusion.1 = bf16[1,512,2560]{2,1,0:T(8,128)(2,1)} fusion(f32[513,2560]{1,0:T(8,128)S(1)} %fusion.2, bf16[1,512,2560]{2,1,0:T(8,128)(2,1)S(1)} %copy-done.1), kind=kLoop, calls=%fused_computation.2 | loop fusion | flops 3932160 | bytes 10485760 | tf_op jit(solution)/shard_map/convert_element_type | solution.py:214
  154.0 0.6 fusion.29
  154.7 0.0 collective-permute-done.3
  154.7 2.6 %collective-permute-start.4 = (f32[2,2,40]{2,1,0:T(2,128)S(1)}, f32[2,2,40]{2,1,0:T(2,128)S(1)}, u32[]{:S(2)}, u32[]{:S(2)}) collective-permute-start(f32[2,2,40]{2,1,0:T(2,128)S(1)} %maximum_select_fusion.4), channel_id=1, source_target_pairs={{0,2},{1,3},{2,0},{3,1},{4,6},{5,7},{6,4},{7,5},{8,10},{9,11},{10,... | collective-permute-start | bytes 1928 | tf_op jit(solution)/shard_map/ppermute | solution.py:40
  157.2 1.6 collective-permute-done.4
  158.8 3.7 %collective-permute-start.5 = (f32[4,2,40]{2,1,0:T(2,128)S(1)}, f32[4,2,40]{2,1,0:T(2,128)S(1)}, u32[]{:S(2)}, u32[]{:S(2)}) collective-permute-start(f32[4,2,40]{2,1,0:T(2,128)S(1)} %maximum_select_fusion.3), channel_id=1, source_target_pairs={{0,4},{1,5},{2,6},{3,7},{4,0},{5,1},{6,2},{7,3},{8,12},{9,13},{10,... | collective-permute-start | bytes 3848 | tf_op jit(solution)/shard_map/ppermute | solution.py:40
  162.5 1.6 collective-permute-done.5
  164.1 1.9 %collective-permute-start.6 = (f32[8,2,40]{2,1,0:T(2,128)S(1)}, f32[8,2,40]{2,1,0:T(2,128)S(1)}, u32[]{:S(2)}, u32[]{:S(2)}) collective-permute-start(f32[8,2,40]{2,1,0:T(2,128)S(1)} %maximum_select_fusion.2), channel_id=1, source_target_pairs={{0,8},{8,0},{16,24},{24,16},{1,9},{9,1},{17,25},{25,17},{2,10},{10... | collective-permute-start | bytes 7688 | tf_op jit(solution)/shard_map/ppermute | solution.py:40
  166.0 1.8 %collective-permute-done.6 = f32[8,2,40]{2,1,0:T(2,128)S(1)} collective-permute-done((f32[8,2,40]{2,1,0:T(2,128)S(1)}, f32[8,2,40]{2,1,0:T(2,128)S(1)}, u32[]{:S(2)}, u32[]{:S(2)}) %collective-permute-start.6) | collective-permute-done | bytes 2592 | tf_op jit(solution)/shard_map/ppermute | solution.py:40
  167.9 1.9 %collective-permute-start.7 = (f32[16,2,40]{2,1,0:T(2,128)S(1)}, f32[16,2,40]{2,1,0:T(2,128)S(1)}, u32[]{:S(2)}, u32[]{:S(2)}) collective-permute-start(f32[16,2,40]{2,1,0:T(2,128)S(1)} %maximum_select_fusion.1), channel_id=1, source_target_pairs={{0,16},{8,24},{16,0},{24,8},{1,17},{9,25},{17,1},{25,9},{2,18},{10... | collective-permute-start | bytes 15368 | tf_op jit(solution)/shard_map/ppermute | solution.py:40
  169.8 1.9 %collective-permute-done.7 = f32[16,2,40]{2,1,0:T(2,128)S(1)} collective-permute-done((f32[16,2,40]{2,1,0:T(2,128)S(1)}, f32[16,2,40]{2,1,0:T(2,128)S(1)}, u32[]{:S(2)}, u32[]{:S(2)}) %collective-permute-start.7) | collective-permute-done | bytes 5152 | tf_op jit(solution)/shard_map/ppermute | solution.py:40
  171.8 0.1 subtract_convert_fusion
  171.9 0.7 slice.65
  172.6 0.8 slice.64
  (24 shorter events, 0.4 us)
Async XLA Ops:
  7.2 9.4 %copy-start.5 = (bf16[1,2560]{1,0:T(2,128)(2,1)S(1)}, bf16[1,2560]{1,0:T(2,128)(2,1)}, u32[]{:S(2)}) copy-start(bf16[1,2560]{1,0:T(2,128)(2,1)} %param.18) | copy-start | bytes 15364
  7.2 9.5 %copy-start.6 = (bf16[1,512]{1,0:T(2,128)(2,1)S(1)}, bf16[1,512]{1,0:T(2,128)(2,1)}, u32[]{:S(2)}) copy-start(bf16[1,512]{1,0:T(2,128)(2,1)} %param.19) | copy-start | bytes 3076
  7.2 9.6 %copy-start.2 = (bf16[1,2048,512]{2,1,0:T(8,128)(2,1)S(1)}, bf16[1,2048,512]{2,1,0:T(8,128)(2,1)}, u32[]{:S(2)}) copy-start(bf16[1,2048,512]{2,1,0:T(8,128)(2,1)} %param.20) | copy-start | bytes 6291460
  7.2 133.5 %all-gather.4.cloned.1.call-start = ((), (), s32[]{:S(2)}) async-start(), calls=%async_computation.1 | async-start | bytes 14745600 | tf_op jit(solution)/shard_map/all_gather | solution.py:208
  10.0 17.0 %collective-permute-start.2 = (bf16[1,512,512]{2,1,0:T(8,128)(2,1)}, bf16[1,512,512]{2,1,0:T(8,128)(2,1)}, u32[]{:S(2)}, u32[]{:S(2)}) collective-permute-start(bf16[1,512,512]{2,1,0:T(8,128)(2,1)} %get-tuple-element.14), channel_id=1, source_target_pairs={{0,8},{8,16},{16,24},{24,0},{1,9},{9,17},{17,25},{25,1},{2,10},{10... | collective-permute-start | bytes 1572872 | tf_op jit(solution)/shard_map/ppermute | solution.py:23
  13.0 24.4 %collective-permute-start.1 = (bf16[1,512,512]{2,1,0:T(8,128)(2,1)S(1)}, bf16[1,512,512]{2,1,0:T(8,128)(2,1)}, u32[]{:S(2)}, u32[]{:S(2)}) collective-permute-start(bf16[1,512,512]{2,1,0:T(8,128)(2,1)S(1)} %get-tuple-element.15), channel_id=1, source_target_pairs={{0,16},{8,24},{16,0},{24,8},{1,17},{9,25},{17,1},{25,9},{2,18},{10... | collective-permute-start | bytes 1572872 | tf_op jit(solution)/shard_map/ppermute | solution.py:23
  14.5 23.2 %collective-permute-start = (bf16[1,512,512]{2,1,0:T(8,128)(2,1)S(1)}, bf16[1,512,512]{2,1,0:T(8,128)(2,1)}, u32[]{:S(2)}, u32[]{:S(2)}) collective-permute-start(bf16[1,512,512]{2,1,0:T(8,128)(2,1)S(1)} %get-tuple-element.16), channel_id=1, source_target_pairs={{0,24},{8,0},{16,8},{24,16},{1,25},{9,1},{17,9},{25,17},{2,26},{10... | collective-permute-start | bytes 1572872 | tf_op jit(solution)/shard_map/ppermute | solution.py:23
  18.5 63.6 %copy-start = (bf16[320,2560]{1,0:T(8,128)(2,1)S(1)}, bf16[320,2560]{1,0:T(8,128)(2,1)}, u32[]{:S(2)}) copy-start(bf16[320,2560]{1,0:T(8,128)(2,1)} %param.23) | copy-start | bytes 4915204
  64.5 33.0 %copy-start.3 = (bf16[1,2560]{1,0:T(2,128)(2,1)S(1)}, bf16[1,2560]{1,0:T(2,128)(2,1)}, u32[]{:S(2)}) copy-start(bf16[1,2560]{1,0:T(2,128)(2,1)} %param.22) | copy-start | bytes 15364
  64.5 33.2 %copy-start.4 = (f32[2560]{0:T(1024)S(1)}, f32[2560]{0:T(1024)}, u32[]{:S(2)}) copy-start(f32[2560]{0:T(1024)} %param.24) | copy-start | bytes 30724
  83.3 14.2 %all-to-all-start = ((f32[8,2,2560]{2,1,0:T(2,128)}), f32[8,2,2560]{2,1,0:T(2,128)S(1)}, u32[]{:S(2)}, u32[]{:S(2)}) async-start(f32[8,2,2560]{2,1,0:T(2,128)} %reshape.156), calls=%async_computation | async-start | bytes 327680 | tf_op jit(solution)/shard_map/all_to_all | solution.py:228
  140.6 14.1 %collective-permute-start.3 = (f32[1,2,40]{2,1,0:T(2,128)S(1)}, f32[1,2,40]{2,1,0:T(2,128)S(1)}, u32[]{:S(2)}, u32[]{:S(2)}) collective-permute-start(f32[1,2,40]{2,1,0:T(2,128)S(1)} %maximum_bitcast_fusion.1), channel_id=1, source_target_pairs={{0,1},{1,0},{2,3},{3,2},{4,5},{5,4},{6,7},{7,6},{8,9},{9,8},{10,11... | collective-permute-start | bytes 968 | tf_op jit(solution)/shard_map/ppermute | solution.py:40
  140.7 11.0 %copy-start.1 = (bf16[1,512,2560]{2,1,0:T(8,128)(2,1)S(1)}, bf16[1,512,2560]{2,1,0:T(8,128)(2,1)}, u32[]{:S(2)}) copy-start(bf16[1,512,2560]{2,1,0:T(8,128)(2,1)} %param.17) | copy-start | bytes 7864324
  154.7 4.1 %collective-permute-start.4 = (f32[2,2,40]{2,1,0:T(2,128)S(1)}, f32[2,2,40]{2,1,0:T(2,128)S(1)}, u32[]{:S(2)}, u32[]{:S(2)}) collective-permute-start(f32[2,2,40]{2,1,0:T(2,128)S(1)} %maximum_select_fusion.4), channel_id=1, source_target_pairs={{0,2},{1,3},{2,0},{3,1},{4,6},{5,7},{6,4},{7,5},{8,10},{9,11},{10,... | collective-permute-start | bytes 1928 | tf_op jit(solution)/shard_map/ppermute | solution.py:40
  158.8 5.3 %collective-permute-start.5 = (f32[4,2,40]{2,1,0:T(2,128)S(1)}, f32[4,2,40]{2,1,0:T(2,128)S(1)}, u32[]{:S(2)}, u32[]{:S(2)}) collective-permute-start(f32[4,2,40]{2,1,0:T(2,128)S(1)} %maximum_select_fusion.3), channel_id=1, source_target_pairs={{0,4},{1,5},{2,6},{3,7},{4,0},{5,1},{6,2},{7,3},{8,12},{9,13},{10,... | collective-permute-start | bytes 3848 | tf_op jit(solution)/shard_map/ppermute | solution.py:40
  164.1 3.7 %collective-permute-start.6 = (f32[8,2,40]{2,1,0:T(2,128)S(1)}, f32[8,2,40]{2,1,0:T(2,128)S(1)}, u32[]{:S(2)}, u32[]{:S(2)}) collective-permute-start(f32[8,2,40]{2,1,0:T(2,128)S(1)} %maximum_select_fusion.2), channel_id=1, source_target_pairs={{0,8},{8,0},{16,24},{24,16},{1,9},{9,1},{17,25},{25,17},{2,10},{10... | collective-permute-start | bytes 7688 | tf_op jit(solution)/shard_map/ppermute | solution.py:40
  167.9 3.8 %collective-permute-start.7 = (f32[16,2,40]{2,1,0:T(2,128)S(1)}, f32[16,2,40]{2,1,0:T(2,128)S(1)}, u32[]{:S(2)}, u32[]{:S(2)}) collective-permute-start(f32[16,2,40]{2,1,0:T(2,128)S(1)} %maximum_select_fusion.1), channel_id=1, source_target_pairs={{0,16},{8,24},{16,0},{24,8},{1,17},{9,25},{17,1},{25,9},{2,18},{10... | collective-permute-start | bytes 15368 | tf_op jit(solution)/shard_map/ppermute | solution.py:40
Sparse Core Ops, SparseCore 0:
  9.7 128.4 all-gather.3

commit v9 on v8

--- a/solution.py
+++ b/solution.py
@@ -24,8 +24,8 @@
 
 
 def gather_all(value):
-    inner = lax.all_gather(value, "vocab", axis=0, tiled=True)
-    return lax.all_gather(inner, "seq", axis=0, tiled=True)
+    inner, _ = doubling_gather(value, "vocab")
+    return doubling_gather(inner, "seq")[0]
 
 
 def doubling_gather(value, axis, tie=None):

time: 181 us -> 184 us (1.017)
  waiting for transfers between devices: 35.4 us -> 60.4 us
  blocking collectives: 40.4 us -> 16.7 us
    ppermute x5 -> x10, waiting for transfers between devices: 6.9 us -> 32 us  [doubling_gather(): theirs = lax.ppermute(value, axis, pairs)]
    all_gather x2 -> x0, blocking collectives: 23.7 us -> none  [the longest x1 14.9 us: gather_all(): inner = lax.all_gather(value, 'vocab', axis=0, tiled=True)]
    ppermute x5 -> x10, starting transfers between devices: 10.1 us -> 11.8 us  [doubling_gather(): theirs = lax.ppermute(value, axis, pairs)]
  transfers between devices with their start and end apart: 10 -> 15, of which waited for: 8 -> 13; matrix products, arithmetic and copies ran while one was open for 22% -> 21% of each run, Pallas kernels for 15% -> 15%
where the time goes in v9:
time: 184 us; the launch traced here: 183 us
  waiting for transfers between devices  60.4 us (33%)
  matrix products  30.5 us (17%)
  Pallas kernels  26.8 us (15%)
  starting transfers between devices  22.5 us (12%)
  blocking collectives  16.7 us (9%)
  between operations  15.6 us (8%)
  other arithmetic  6.47 us (4%)
  local copies, waits for them, and re-layouts  4.24 us (2%)
    ppermute x10, waiting for transfers between devices, doubling_gather(): theirs = lax.ppermute(value, axis, pairs)  32 us
    pallas_call x1, Pallas kernels, prefill_attention(): pl.pallas_call(kernel, out_shape=jax.ShapeDtypeStruct(pre_query.shape, jn...  26.8 us
    ppermute x3, waiting for transfers between devices, from_behind(): return lax.ppermute(value, axis, pairs)  19.1 us
    dot_general x1, matrix products, body(): lax.dot_general(head_rows, embedding, (((1,), (1,)), ((), ())), preferred...  18.1 us
    all_gather x1, blocking collectives, body(): group_rows = lax.all_gather(head_mixed, 'vocab', axis=0, tiled=True)  16.7 us
    ppermute x10, starting transfers between devices, doubling_gather(): theirs = lax.ppermute(value, axis, pairs)  11.8 us
    dot_general x1, matrix products, body(): jnp.dot(mixed_rows, lax.all_gather(out_weight, 'vocab', axis=0, tiled=Tru...  11 us
    all_to_all x1, waiting for transfers between devices, body(): lax.all_to_all(partial.reshape(vocab_count, head_count, D), 'vocab', 0, 0...  8.62 us
  transfers between devices with their start and end apart: 15, of which 13 were waited for; matrix products, arithmetic and copies ran while one was open for 21% of the time, Pallas kernels for 15%

profile of v9, /device:TPU:0, one launch (start us, length us, event | category | flops | bytes accessed | tf_op | source)
XLA Modules:
  0.0 183.2 jit_solution(1522584662339089663)
XLA Ops:
  7.2 0.0 copy-start.5
  7.2 0.0 copy-start.6
  7.2 0.0 copy-start.2
  7.2 0.0 all-gather.3.cloned.1.call-start
  7.2 0.7 all-gather.3.cloned.1.call-update
  7.9 2.1 %broadcast_select_fusion = (bf16[1,512,512]{2,1,0:T(8,128)(2,1)}, bf16[1,512,512]{2,1,0:T(8,128)(2,1)S(1)}, bf16[1,512,512]{2,1,0:T(8,128)(2,1)S(1)}) fusion(bf16[1,512,512]{2,1,0:T(8,128)(2,1)} %refs_4_.1, bf16[1,512,512]{2,1,0:T(8,128)(2,1)} %refs_0_.1, pred[]{:T(512)S(6)} %le.11, pred[]{:T(512)S(6)} %le.10, pred[]{:T(512)S(6)} %le.9), kind=kLoop, calls=%fused_computation.20 | loop fusion | flops 786432 | bytes 2621443 | tf_op jit(solution)/shard_map/jit(_where)/select_n | solution.py:160
  10.0 2.9 %collective-permute-start.2 = (bf16[1,512,512]{2,1,0:T(8,128)(2,1)}, bf16[1,512,512]{2,1,0:T(8,128)(2,1)}, u32[]{:S(2)}, u32[]{:S(2)}) collective-permute-start(bf16[1,512,512]{2,1,0:T(8,128)(2,1)} %get-tuple-element.14), channel_id=1, source_target_pairs={{0,8},{8,16},{16,24},{24,0},{1,9},{9,17},{17,25},{25,1},{2,10},{10... | collective-permute-start | bytes 1572872 | tf_op jit(solution)/shard_map/ppermute | solution.py:23
  13.0 1.5 collective-permute-start.1
  14.5 1.4 collective-permute-start
  16.7 0.1 fusion.9
  16.8 0.5 select_reduce_fusion
  18.0 0.2 fusion.18
  18.2 0.3 fusion.8
  18.5 0.0 copy-start
  18.6 8.5 %collective-permute-done.2.refs_3_ = bf16[1,512,512]{2,1,0:T(8,128)(2,1)} collective-permute-done((bf16[1,512,512]{2,1,0:T(8,128)(2,1)}, bf16[1,512,512]{2,1,0:T(8,128)(2,1)}, u32[]{:S(2)}, u32[]{:S(2)}) %collective-permute-start.2) | collective-permute-done | bytes 524320 | tf_op jit(solution)/shard_map/ppermute | solution.py:23
  27.0 10.4 %collective-permute-done.1.refs_2_ = bf16[1,512,512]{2,1,0:T(8,128)(2,1)} collective-permute-done((bf16[1,512,512]{2,1,0:T(8,128)(2,1)S(1)}, bf16[1,512,512]{2,1,0:T(8,128)(2,1)}, u32[]{:S(2)}, u32[]{:S(2)}) %collective-permute-start.1) | collective-permute-done | bytes 524320 | tf_op jit(solution)/shard_map/ppermute | solution.py:23
  37.4 0.3 collective-permute-done.refs_1_
  37.7 26.8 %shard_map.156 = bf16[1,512,2560]{2,1,0:T(8,128)(2,1)} custom-call(s32[1]{0:T(128)S(6)} %sub.112.t0_ref, bf16[1,512,2560]{2,1,0:T(8,128)(2,1)} %q_ref.1, bf16[1,512,512]{2,1,0:T(8,128)(2,1)} %refs_0_.1, bf16[1,512,512]{2,1,0:T(8,128)(2,1)} %collective-permute-done.refs_1_, bf16[1,512,512]{2,1,0:T(8,128)(2,1)} %collective-permute-done.1.refs_2_, ...), custom_call_target="tpu_custom_call" | custom-call | flops 13421772800 | bytes 7864320 | tf_op jit(solution)/shard_map/pallas_call | solution.py:116
  64.5 0.8 slice_bitcast_fusion.1
  65.4 16.7 %all-gather = bf16[8,2,2560]{2,1,0:T(2,128)(2,1)S(1)} all-gather(bf16[1,2,2560]{2,1,0:T(2,128)(2,1)S(1)} %maximum_bitcast_fusion), channel_id=1, replica_groups=mesh['seq'=4,'vocab'=8] {'vocab'}, dimensions={0}, use_global_device_ids=true | all-gather | bytes 92160 | tf_op jit(solution)/shard_map/all_gather | solution.py:223
  82.1 0.0 copy-done
  82.1 0.4 fusion.27
  82.5 0.8 reshape.158
  83.3 4.7 %all-to-all-start = ((f32[8,2,2560]{2,1,0:T(2,128)}), f32[8,2,2560]{2,1,0:T(2,128)S(1)}, u32[]{:S(2)}, u32[]{:S(2)}) async-start(f32[8,2,2560]{2,1,0:T(2,128)} %reshape.158), calls=%async_computation | async-start | bytes 327680 | tf_op jit(solution)/shard_map/all_to_all | solution.py:228
  88.1 0.8 slice_bitcast_fusion.2
  88.9 8.6 %all-to-all-done = f32[8,2,2560]{2,1,0:T(2,128)S(1)} async-done(((f32[8,2,2560]{2,1,0:T(2,128)}), f32[8,2,2560]{2,1,0:T(2,128)S(1)}, u32[]{:S(2)}, u32[]{:S(2)}) %all-to-all-start) | async-done | bytes 163872 | tf_op jit(solution)/shard_map/all_to_all | solution.py:228
  97.5 0.1 reduce_sum.46
  97.5 0.0 copy-done.3
  97.5 0.2 fusion.24
  97.7 0.0 copy-done.4
  97.7 0.1 fusion.26
  97.8 0.1 collective-permute-start.3
  97.9 1.1 collective-permute-done.3
  99.1 1.8 collective-permute-start.4
  100.9 2.6 %collective-permute-done.4 = bf16[4,2560]{1,0:T(4,128)(2,1)S(1)} collective-permute-done((bf16[4,2560]{1,0:T(4,128)(2,1)S(1)}, bf16[4,2560]{1,0:T(4,128)(2,1)S(1)}, u32[]{:S(2)}, u32[]{:S(2)}) %collective-permute-start.4) | collective-permute-done | bytes 20512 | tf_op jit(solution)/shard_map/ppermute | solution.py:40
  103.5 4.9 %collective-permute-start.5 = (bf16[8,2560]{1,0:T(8,128)(2,1)S(1)}, bf16[8,2560]{1,0:T(8,128)(2,1)S(1)}, u32[]{:S(2)}, u32[]{:S(2)}) collective-permute-start(bf16[8,2560]{1,0:T(8,128)(2,1)S(1)} %maximum_select_fusion.3), channel_id=1, source_target_pairs={{0,4},{1,5},{2,6},{3,7},{4,0},{5,1},{6,2},{7,3},{8,12},{9,13},{10,... | collective-permute-start | bytes 122888 | tf_op jit(solution)/shard_map/ppermute | solution.py:40
  108.5 7.6 %collective-permute-done.5 = bf16[8,2560]{1,0:T(8,128)(2,1)S(1)} collective-permute-done((bf16[8,2560]{1,0:T(8,128)(2,1)S(1)}, bf16[8,2560]{1,0:T(8,128)(2,1)S(1)}, u32[]{:S(2)}, u32[]{:S(2)}) %collective-permute-start.5) | collective-permute-done | bytes 40992 | tf_op jit(solution)/shard_map/ppermute | solution.py:40
  116.1 1.2 collective-permute-start.6
  117.3 3.3 %collective-permute-done.6 = bf16[16,2560]{1,0:T(8,128)(2,1)S(1)} collective-permute-done((bf16[16,2560]{1,0:T(8,128)(2,1)S(1)}, bf16[16,2560]{1,0:T(8,128)(2,1)S(1)}, u32[]{:S(2)}, u32[]{:S(2)}) %collective-permute-start.6) | collective-permute-done | bytes 81952 | tf_op jit(solution)/shard_map/ppermute | solution.py:40
  120.6 1.2 collective-permute-start.7
  121.8 4.2 %collective-permute-done.7 = bf16[32,2560]{1,0:T(8,128)(2,1)S(1)} collective-permute-done((bf16[32,2560]{1,0:T(8,128)(2,1)S(1)}, bf16[32,2560]{1,0:T(8,128)(2,1)S(1)}, u32[]{:S(2)}, u32[]{:S(2)}) %collective-permute-start.7) | collective-permute-done | bytes 163872 | tf_op jit(solution)/shard_map/ppermute | solution.py:40
  126.0 0.1 maximum_select_fusion
  126.0 0.1 select_n.206
  126.2 0.1 slice.59
  126.3 18.1 %fusion.43 = (f32[40]{0:T(128)S(1)}, f32[40,8000]{1,0:T(8,128)S(1)}) fusion(bf16[8000,2560]{1,0:T(8,128)(2,1)} %param.25, bf16[8,2560]{1,0:T(8,128)(2,1)S(1)} %bitcast.63, bf16[32,2560]{1,0:T(8,128)(2,1)S(1)} %bitcast.62), kind=kOutput, calls=%fused_computation.84 | convolution fusion | flops 1639129600 | bytes 42444960 | tf_op jit(solution)/shard_map/dot_general | solution.py:238
  144.5 0.4 exponential_reduce_fusion
  144.9 0.1 collective-permute-start.8
  144.9 0.0 all-gather.3.cloned.1.call-done
  145.0 0.0 copy-start.1
  145.0 11.0 %fusion.2 = f32[513,2560]{1,0:T(8,128)S(1)} fusion(bf16[2560,2560]{1,0:T(8,128)(2,1)} %all-gather.3.cloned.1.call-done, bf16[1,2560]{1,0:T(2,128)(2,1)S(1)} %bitcast.68, bf16[512,2560]{1,0:T(8,128)(2,1)} %bitcast.72), kind=kOutput, calls=%fused_computation.3 | convolution fusion | flops 6729246720 | bytes 20986880 | tf_op jit(solution)/shard_map/dot_general | solution.py:206
  156.0 2.3 %fusion.1 = bf16[1,512,2560]{2,1,0:T(8,128)(2,1)} fusion(f32[513,2560]{1,0:T(8,128)S(1)} %fusion.2, bf16[1,512,2560]{2,1,0:T(8,128)(2,1)S(1)} %copy-done.1), kind=kLoop, calls=%fused_computation.2 | loop fusion | flops 3932160 | bytes 10485760 | tf_op jit(solution)/shard_map/convert_element_type | solution.py:214
  158.3 0.6 fusion.29
  158.9 0.0 collective-permute-done.8
  158.9 0.1 collective-permute-start.9
  159.0 3.6 %collective-permute-done.9 = f32[2,2,40]{2,1,0:T(2,128)S(1)} collective-permute-done((f32[2,2,40]{2,1,0:T(2,128)S(1)}, f32[2,2,40]{2,1,0:T(2,128)S(1)}, u32[]{:S(2)}, u32[]{:S(2)}) %collective-permute-start.9) | collective-permute-done | bytes 672 | tf_op jit(solution)/shard_map/ppermute | solution.py:40
  162.6 0.0 collective-permute-start.10
  162.6 4.5 %collective-permute-done.10 = f32[4,2,40]{2,1,0:T(2,128)S(1)} collective-permute-done((f32[4,2,40]{2,1,0:T(2,128)S(1)}, f32[4,2,40]{2,1,0:T(2,128)S(1)}, u32[]{:S(2)}, u32[]{:S(2)}) %collective-permute-start.10) | collective-permute-done | bytes 1312 | tf_op jit(solution)/shard_map/ppermute | solution.py:40
  167.1 1.2 collective-permute-start.11
  168.3 2.5 %collective-permute-done.11 = f32[8,2,40]{2,1,0:T(2,128)S(1)} collective-permute-done((f32[8,2,40]{2,1,0:T(2,128)S(1)}, f32[8,2,40]{2,1,0:T(2,128)S(1)}, u32[]{:S(2)}, u32[]{:S(2)}) %collective-permute-start.11) | collective-permute-done | bytes 2592 | tf_op jit(solution)/shard_map/ppermute | solution.py:40
  170.8 1.2 collective-permute-start.12
  172.0 2.6 %collective-permute-done.12 = f32[16,2,40]{2,1,0:T(2,128)S(1)} collective-permute-done((f32[16,2,40]{2,1,0:T(2,128)S(1)}, f32[16,2,40]{2,1,0:T(2,128)S(1)}, u32[]{:S(2)}, u32[]{:S(2)}) %collective-permute-start.12) | collective-permute-done | bytes 5152 | tf_op jit(solution)/shard_map/ppermute | solution.py:40
  174.8 0.1 subtract_convert_fusion
  174.9 0.7 slice.65
  175.6 0.8 slice.64
  (33 shorter events, 0.5 us)
Async XLA Ops:
  7.2 9.4 %copy-start.5 = (bf16[1,2560]{1,0:T(2,128)(2,1)S(1)}, bf16[1,2560]{1,0:T(2,128)(2,1)}, u32[]{:S(2)}) copy-start(bf16[1,2560]{1,0:T(2,128)(2,1)} %param.18) | copy-start | bytes 15364
  7.2 9.5 %copy-start.6 = (bf16[1,512]{1,0:T(2,128)(2,1)S(1)}, bf16[1,512]{1,0:T(2,128)(2,1)}, u32[]{:S(2)}) copy-start(bf16[1,512]{1,0:T(2,128)(2,1)} %param.19) | copy-start | bytes 3076
  7.2 9.6 %copy-start.2 = (bf16[1,2048,512]{2,1,0:T(8,128)(2,1)S(1)}, bf16[1,2048,512]{2,1,0:T(8,128)(2,1)}, u32[]{:S(2)}) copy-start(bf16[1,2048,512]{2,1,0:T(8,128)(2,1)} %param.20) | copy-start | bytes 6291460
  7.2 137.8 %all-gather.3.cloned.1.call-start = ((), (), s32[]{:S(2)}) async-start(), calls=%async_computation.1 | async-start | bytes 14745600 | tf_op jit(solution)/shard_map/all_gather | solution.py:208
  10.0 17.0 %collective-permute-start.2 = (bf16[1,512,512]{2,1,0:T(8,128)(2,1)}, bf16[1,512,512]{2,1,0:T(8,128)(2,1)}, u32[]{:S(2)}, u32[]{:S(2)}) collective-permute-start(bf16[1,512,512]{2,1,0:T(8,128)(2,1)} %get-tuple-element.14), channel_id=1, source_target_pairs={{0,8},{8,16},{16,24},{24,0},{1,9},{9,17},{17,25},{25,1},{2,10},{10... | collective-permute-start | bytes 1572872 | tf_op jit(solution)/shard_map/ppermute | solution.py:23
  13.0 24.4 %collective-permute-start.1 = (bf16[1,512,512]{2,1,0:T(8,128)(2,1)S(1)}, bf16[1,512,512]{2,1,0:T(8,128)(2,1)}, u32[]{:S(2)}, u32[]{:S(2)}) collective-permute-start(bf16[1,512,512]{2,1,0:T(8,128)(2,1)S(1)} %get-tuple-element.15), channel_id=1, source_target_pairs={{0,16},{8,24},{16,0},{24,8},{1,17},{9,25},{17,1},{25,9},{2,18},{10... | collective-permute-start | bytes 1572872 | tf_op jit(solution)/shard_map/ppermute | solution.py:23
  14.5 23.2 %collective-permute-start = (bf16[1,512,512]{2,1,0:T(8,128)(2,1)S(1)}, bf16[1,512,512]{2,1,0:T(8,128)(2,1)}, u32[]{:S(2)}, u32[]{:S(2)}) collective-permute-start(bf16[1,512,512]{2,1,0:T(8,128)(2,1)S(1)} %get-tuple-element.16), channel_id=1, source_target_pairs={{0,24},{8,0},{16,8},{24,16},{1,25},{9,1},{17,9},{25,17},{2,26},{10... | collective-permute-start | bytes 1572872 | tf_op jit(solution)/shard_map/ppermute | solution.py:23
  18.5 63.6 %copy-start = (bf16[320,2560]{1,0:T(8,128)(2,1)S(1)}, bf16[320,2560]{1,0:T(8,128)(2,1)}, u32[]{:S(2)}) copy-start(bf16[320,2560]{1,0:T(8,128)(2,1)} %param.23) | copy-start | bytes 4915204
  64.5 33.0 %copy-start.3 = (bf16[1,2560]{1,0:T(2,128)(2,1)S(1)}, bf16[1,2560]{1,0:T(2,128)(2,1)}, u32[]{:S(2)}) copy-start(bf16[1,2560]{1,0:T(2,128)(2,1)} %param.22) | copy-start | bytes 15364
  64.5 33.2 %copy-start.4 = (f32[2560]{0:T(1024)S(1)}, f32[2560]{0:T(1024)}, u32[]{:S(2)}) copy-start(f32[2560]{0:T(1024)} %param.24) | copy-start | bytes 30724
  83.3 14.2 %all-to-all-start = ((f32[8,2,2560]{2,1,0:T(2,128)}), f32[8,2,2560]{2,1,0:T(2,128)S(1)}, u32[]{:S(2)}, u32[]{:S(2)}) async-start(f32[8,2,2560]{2,1,0:T(2,128)} %reshape.158), calls=%async_computation | async-start | bytes 327680 | tf_op jit(solution)/shard_map/all_to_all | solution.py:228
  97.8 1.2 collective-permute-start.3
  99.1 4.4 %collective-permute-start.4 = (bf16[4,2560]{1,0:T(4,128)(2,1)S(1)}, bf16[4,2560]{1,0:T(4,128)(2,1)S(1)}, u32[]{:S(2)}, u32[]{:S(2)}) collective-permute-start(bf16[4,2560]{1,0:T(4,128)(2,1)S(1)} %maximum_select_fusion.5), channel_id=1, source_target_pairs={{0,2},{1,3},{2,0},{3,1},{4,6},{5,7},{6,4},{7,5},{8,10},{9,11},{10,... | collective-permute-start | bytes 61448 | tf_op jit(solution)/shard_map/ppermute | solution.py:40
  103.5 12.5 %collective-permute-start.5 = (bf16[8,2560]{1,0:T(8,128)(2,1)S(1)}, bf16[8,2560]{1,0:T(8,128)(2,1)S(1)}, u32[]{:S(2)}, u32[]{:S(2)}) collective-permute-start(bf16[8,2560]{1,0:T(8,128)(2,1)S(1)} %maximum_select_fusion.3), channel_id=1, source_target_pairs={{0,4},{1,5},{2,6},{3,7},{4,0},{5,1},{6,2},{7,3},{8,12},{9,13},{10,... | collective-permute-start | bytes 122888 | tf_op jit(solution)/shard_map/ppermute | solution.py:40
  116.1 4.5 %collective-permute-start.6 = (bf16[16,2560]{1,0:T(8,128)(2,1)S(1)}, bf16[16,2560]{1,0:T(8,128)(2,1)S(1)}, u32[]{:S(2)}, u32[]{:S(2)}) collective-permute-start(bf16[16,2560]{1,0:T(8,128)(2,1)S(1)} %maximum_select_fusion.2), channel_id=1, source_target_pairs={{0,8},{8,0},{16,24},{24,16},{1,9},{9,1},{17,25},{25,17},{2,10},{10... | collective-permute-start | bytes 245768 | tf_op jit(solution)/shard_map/ppermute | solution.py:40
  120.6 5.4 %collective-permute-start.7 = (bf16[32,2560]{1,0:T(8,128)(2,1)S(1)}, bf16[32,2560]{1,0:T(8,128)(2,1)S(1)}, u32[]{:S(2)}, u32[]{:S(2)}) collective-permute-start(bf16[32,2560]{1,0:T(8,128)(2,1)S(1)} %maximum_select_fusion.1), channel_id=1, source_target_pairs={{0,16},{8,24},{16,0},{24,8},{1,17},{9,25},{17,1},{25,9},{2,18},{10... | collective-permute-start | bytes 491528 | tf_op jit(solution)/shard_map/ppermute | solution.py:40
  144.9 14.1 %collective-permute-start.8 = (f32[1,2,40]{2,1,0:T(2,128)S(1)}, f32[1,2,40]{2,1,0:T(2,128)S(1)}, u32[]{:S(2)}, u32[]{:S(2)}) collective-permute-start(f32[1,2,40]{2,1,0:T(2,128)S(1)} %maximum_bitcast_fusion.1), channel_id=1, source_target_pairs={{0,1},{1,0},{2,3},{3,2},{4,5},{5,4},{6,7},{7,6},{8,9},{9,8},{10,11... | collective-permute-start | bytes 968 | tf_op jit(solution)/shard_map/ppermute | solution.py:40
  145.0 11.0 %copy-start.1 = (bf16[1,512,2560]{2,1,0:T(8,128)(2,1)S(1)}, bf16[1,512,2560]{2,1,0:T(8,128)(2,1)}, u32[]{:S(2)}) copy-start(bf16[1,512,2560]{2,1,0:T(8,128)(2,1)} %param.17) | copy-start | bytes 7864324
  158.9 3.7 %collective-permute-start.9 = (f32[2,2,40]{2,1,0:T(2,128)S(1)}, f32[2,2,40]{2,1,0:T(2,128)S(1)}, u32[]{:S(2)}, u32[]{:S(2)}) collective-permute-start(f32[2,2,40]{2,1,0:T(2,128)S(1)} %maximum_select_fusion.9), channel_id=1, source_target_pairs={{0,2},{1,3},{2,0},{3,1},{4,6},{5,7},{6,4},{7,5},{8,10},{9,11},{10,... | collective-permute-start | bytes 1928 | tf_op jit(solution)/shard_map/ppermute | solution.py:40
  162.6 4.5 %collective-permute-start.10 = (f32[4,2,40]{2,1,0:T(2,128)S(1)}, f32[4,2,40]{2,1,0:T(2,128)S(1)}, u32[]{:S(2)}, u32[]{:S(2)}) collective-permute-start(f32[4,2,40]{2,1,0:T(2,128)S(1)} %maximum_select_fusion.8), channel_id=1, source_target_pairs={{0,4},{1,5},{2,6},{3,7},{4,0},{5,1},{6,2},{7,3},{8,12},{9,13},{10,... | collective-permute-start | bytes 3848 | tf_op jit(solution)/shard_map/ppermute | solution.py:40
  167.1 3.7 %collective-permute-start.11 = (f32[8,2,40]{2,1,0:T(2,128)S(1)}, f32[8,2,40]{2,1,0:T(2,128)S(1)}, u32[]{:S(2)}, u32[]{:S(2)}) collective-permute-start(f32[8,2,40]{2,1,0:T(2,128)S(1)} %maximum_select_fusion.7), channel_id=1, source_target_pairs={{0,8},{8,0},{16,24},{24,16},{1,9},{9,1},{17,25},{25,17},{2,10},{10... | collective-permute-start | bytes 7688 | tf_op jit(solution)/shard_map/ppermute | solution.py:40
  170.8 3.8 %collective-permute-start.12 = (f32[16,2,40]{2,1,0:T(2,128)S(1)}, f32[16,2,40]{2,1,0:T(2,128)S(1)}, u32[]{:S(2)}, u32[]{:S(2)}) collective-permute-start(f32[16,2,40]{2,1,0:T(2,128)S(1)} %maximum_select_fusion.6), channel_id=1, source_target_pairs={{0,16},{8,24},{16,0},{24,8},{1,17},{9,25},{17,1},{25,9},{2,18},{10... | collective-permute-start | bytes 15368 | tf_op jit(solution)/shard_map/ppermute | solution.py:40
Sparse Core Ops, SparseCore 0:
  9.7 129.5 all-gather.2

commit v10 on v8

--- a/solution.py
+++ b/solution.py
@@ -59,21 +59,29 @@
     return (values * lax.rsqrt(square_mean + STABILITY_FLOOR) * gain).astype(jnp.bfloat16)
 
 
-def prefill_kernel(t0_ref, q_ref, *refs, n_blocks, block, tq):
-    kv_refs = refs[:n_blocks]
-    o_ref = refs[n_blocks]
+def prefill_kernel(t0_ref, q_ref, *refs, positions, n_blocks, block, tq, carry_in, final):
+    n_in = len(positions)
+    if carry_in:
+        peak_ref, denom_ref, accum_ref = refs[:3]
+        refs = refs[3:]
+    kv_refs = refs[:n_in]
+    out_refs = refs[n_in:]
     r = pl.program_id(0)
     qi = pl.program_id(2)
     t0 = t0_ref[r]
     q = q_ref[0]
     row = qi * tq + lax.broadcasted_iota(jnp.int32, (tq, block), 0)
     col = lax.broadcasted_iota(jnp.int32, (tq, block), 1)
-    peak = jnp.full((tq, 1), NEG_BIG, jnp.float32)
-    denom = jnp.zeros((tq, 1), jnp.float32)
-    accum = jnp.zeros((tq, HEAD_SIZE), jnp.float32)
+    if carry_in:
+        peak = peak_ref[0, 0][:, :1]
+        denom = denom_ref[0, 0][:, :1]
+        accum = accum_ref[0, 0]
+    else:
+        peak = jnp.full((tq, 1), NEG_BIG, jnp.float32)
+        denom = jnp.zeros((tq, 1), jnp.float32)
+        accum = jnp.zeros((tq, HEAD_SIZE), jnp.float32)
     scale = HEAD_SIZE ** (-0.5)
-    for j in range(n_blocks):
-        kv = kv_refs[j]
+    for kv, j in zip(kv_refs, positions):
         keys = kv[0, :, :HEAD_SIZE]
         values = kv[0, :, HEAD_SIZE:]
         scores = (
@@ -101,36 +109,73 @@
             weights.astype(jnp.bfloat16), values, preferred_element_type=jnp.float32
         )
         peak = peak_new
-    o_ref[0] = (accum / denom).astype(o_ref.dtype)
-
-
-def prefill_attention(pre_query, kv_blocks, first_key):
+    if final:
+        out_refs[0][0] = (accum / denom).astype(out_refs[0].dtype)
+    else:
+        out_refs[0][0, 0] = jnp.broadcast_to(peak, (tq, 128))
+        out_refs[1][0, 0] = jnp.broadcast_to(denom, (tq, 128))
+        out_refs[2][0, 0] = accum
+
+
+def prefill_pass(pre_query, kv_blocks, positions, n_blocks, first_key, carry, final):
     local_pre, block_query, _ = pre_query.shape
     block = kv_blocks[0].shape[1]
-    n_blocks = len(kv_blocks)
     tq = min(block_query, 512)
-    kernel = functools.partial(prefill_kernel, n_blocks=n_blocks, block=block, tq=tq)
+    kernel = functools.partial(
+        prefill_kernel,
+        positions=tuple(positions),
+        n_blocks=n_blocks,
+        block=block,
+        tq=tq,
+        carry_in=carry is not None,
+        final=final,
+    )
     kv_spec = pl.BlockSpec((1, block, 2 * HEAD_SIZE), lambda r, h, qi, t0: (r, 0, 0))
     q_spec = pl.BlockSpec((1, tq, HEAD_SIZE), lambda r, h, qi, t0: (r, qi, h))
-    flops = 4 * local_pre * HQ * block_query * block * n_blocks * HEAD_SIZE
+    stat_spec = pl.BlockSpec((1, 1, tq, 128), lambda r, h, qi, t0: (r, h, qi, 0))
+    accum_spec = pl.BlockSpec((1, 1, tq, HEAD_SIZE), lambda r, h, qi, t0: (r, h, qi, 0))
+    stat_shape = jax.ShapeDtypeStruct((local_pre, HQ, block_query, 128), jnp.float32)
+    accum_shape = jax.ShapeDtypeStruct((local_pre, HQ, block_query, HEAD_SIZE), jnp.float32)
+    carry_specs = [] if carry is None else [stat_spec, stat_spec, accum_spec]
+    carry_args = [] if carry is None else list(carry)
+    if final:
+        out_shape = jax.ShapeDtypeStruct(pre_query.shape, jnp.bfloat16)
+        out_specs = q_spec
+    else:
+        out_shape = (stat_shape, stat_shape, accum_shape)
+        out_specs = (stat_spec, stat_spec, accum_spec)
+    n_in = len(kv_blocks)
+    flops = 4 * local_pre * HQ * block_query * block * n_in * HEAD_SIZE
     return pl.pallas_call(
         kernel,
-        out_shape=jax.ShapeDtypeStruct(pre_query.shape, jnp.bfloat16),
+        out_shape=out_shape,
         grid_spec=pltpu.PrefetchScalarGridSpec(
             num_scalar_prefetch=1,
             grid=(local_pre, HQ, block_query // tq),
-            in_specs=[q_spec] + [kv_spec] * n_blocks,
-            out_specs=q_spec,
+            in_specs=[q_spec] + carry_specs + [kv_spec] * n_in,
+            out_specs=out_specs,
         ),
         compiler_params=pltpu.CompilerParams(
             dimension_semantics=("arbitrary", "arbitrary", "arbitrary")
         ),
         cost_estimate=pl.CostEstimate(
             flops=flops,
-            transcendentals=local_pre * HQ * block_query * block * n_blocks,
+            transcendentals=local_pre * HQ * block_query * block * n_in,
             bytes_accessed=2 * pre_query.size * 2 + sum(b.size for b in kv_blocks) * 2,
         ),
-    )(first_key, pre_query, *kv_blocks)
+    )(first_key, pre_query, *carry_args, *kv_blocks)
+
+
+def prefill_attention(pre_query, kv_blocks, first_key):
+    n_blocks = len(kv_blocks)
+    carry = prefill_pass(
+        pre_query, [kv_blocks[0], kv_blocks[-1]], [0, n_blocks - 1], n_blocks,
+        first_key, None, False,
+    )
+    middle = list(range(1, n_blocks - 1))
+    return prefill_pass(
+        pre_query, [kv_blocks[j] for j in middle], middle, n_blocks, first_key, carry, True
+    )
 
 
 def body(

time: 181 us -> 198 us (1.094)
  Pallas kernels: 26.8 us -> 55.8 us
  waiting for transfers between devices: 35.4 us -> 27 us
  starting transfers between devices: 20.8 us -> 15.3 us
    pallas_call x1 -> x2, Pallas kernels: 26.8 us -> 55.8 us  [prefill_pass(): pl.pallas_call(kernel, out_shape=out_shape, grid_spec=pltpu.PrefetchScala...]
    ppermute x3, waiting for transfers between devices: 19.1 us -> 6.87 us  [from_behind(): return lax.ppermute(value, axis, pairs)]
    ppermute x5, starting transfers between devices: 10.1 us -> 6.88 us  [doubling_gather(): theirs = lax.ppermute(value, axis, pairs)]
    ppermute x5, waiting for transfers between devices: 6.9 us -> 9.16 us  [doubling_gather(): theirs = lax.ppermute(value, axis, pairs)]
    all_gather x1, blocking collectives: 16.7 us -> 18.8 us  [body(): group_rows = lax.all_gather(head_mixed, 'vocab', axis=0, tiled=True)]
  transfers between devices with their start and end apart: 10 -> 10, of which waited for: 8 -> 6; matrix products, arithmetic and copies ran while one was open for 22% -> 20% of each run, Pallas kernels for 15% -> 28%
where the time goes in v10:
time: 198 us; the launch traced here: 197 us
  Pallas kernels  55.8 us (28%)
  blocking collectives  42.3 us (21%)
  matrix products  30.4 us (15%)
  waiting for transfers between devices  27 us (14%)
  between operations  15.6 us (8%)
  starting transfers between devices  15.3 us (8%)
  other arithmetic  6.28 us (3%)
  local copies, waits for them, and re-layouts  4.25 us (2%)
    pallas_call x2, Pallas kernels, prefill_pass(): pl.pallas_call(kernel, out_shape=out_shape, grid_spec=pltpu.PrefetchScala...  55.8 us
    all_gather x1, blocking collectives, body(): group_rows = lax.all_gather(head_mixed, 'vocab', axis=0, tiled=True)  18.8 us
    dot_general x1, matrix products, body(): lax.dot_general(head_rows, embedding, (((1,), (1,)), ((), ())), preferred...  18.1 us
    all_gather x1, blocking collectives, gather_all(): inner = lax.all_gather(value, 'vocab', axis=0, tiled=True)  14.1 us
    dot_general x1, matrix products, body(): jnp.dot(mixed_rows, lax.all_gather(out_weight, 'vocab', axis=0, tiled=Tru...  11 us
    all_to_all x1, waiting for transfers between devices, body(): lax.all_to_all(partial.reshape(vocab_count, head_count, D), 'vocab', 0, 0...  10.3 us
    all_gather x1, blocking collectives, gather_all(): return lax.all_gather(inner, 'seq', axis=0, tiled=True)  9.44 us
    ppermute x5, waiting for transfers between devices, doubling_gather(): theirs = lax.ppermute(value, axis, pairs)  9.16 us
  transfers between devices with their start and end apart: 10, of which 6 were waited for; matrix products, arithmetic and copies ran while one was open for 20% of the time, Pallas kernels for 28%

profile of v10, /device:TPU:0, one launch (start us, length us, event | category | flops | bytes accessed | tf_op | source)
XLA Modules:
  0.0 197.0 jit_solution(3220498078691856871)
XLA Ops:
  7.2 0.0 copy-start.5
  7.2 0.0 copy-start.6
  7.2 0.0 copy-start.2
  7.2 0.0 all-gather.4.cloned.1.call-start
  7.2 0.7 all-gather.4.cloned.1.call-update
  7.9 2.1 %broadcast_select_fusion = (bf16[1,512,512]{2,1,0:T(8,128)(2,1)S(1)}, bf16[1,512,512]{2,1,0:T(8,128)(2,1)}, bf16[1,512,512]{2,1,0:T(8,128)(2,1)S(1)}) fusion(bf16[1,512,512]{2,1,0:T(8,128)(2,1)} %refs_1_.1, bf16[1,512,512]{2,1,0:T(8,128)(2,1)} %refs_0_.1, pred[]{:T(512)S(6)} %le.11, pred[]{:T(512)S(6)} %le.9, pred[]{:T(512)S(6)} %le.10), kind=kLoop, calls=%fused_computation.20 | loop fusion | flops 786432 | bytes 2621443 | tf_op jit(solution)/shard_map/jit(_where)/select_n | solution.py:205
  10.0 3.9 %collective-permute-start = (bf16[1,512,512]{2,1,0:T(8,128)(2,1)}, bf16[1,512,512]{2,1,0:T(8,128)(2,1)}, u32[]{:S(2)}, u32[]{:S(2)}) collective-permute-start(bf16[1,512,512]{2,1,0:T(8,128)(2,1)} %get-tuple-element.21), channel_id=1, source_target_pairs={{0,24},{8,0},{16,8},{24,16},{1,25},{9,1},{17,9},{25,17},{2,26},{10... | collective-permute-start | bytes 1572872 | tf_op jit(solution)/shard_map/ppermute | solution.py:23
  13.9 0.5 collective-permute-start.1
  14.4 0.6 collective-permute-start.2
  15.7 0.0 copy-done.5
  15.8 0.0 copy-done.6
  15.8 0.1 fusion.9
  15.9 0.0 copy-done.2
  15.9 0.5 select_reduce_fusion
  16.4 0.2 fusion.18
  16.7 0.3 fusion.8
  17.7 14.1 %shard_map.156 = (f32[1,10,512,128]{3,2,1,0:T(8,128)}, f32[1,10,512,128]{3,2,1,0:T(8,128)}, f32[1,10,512,256]{3,2,1,0:T(8,128)}) custom-call(s32[1]{0:T(128)S(6)} %sub.104.t0_ref, bf16[1,512,2560]{2,1,0:T(8,128)(2,1)} %q_ref.3, bf16[1,512,512]{2,1,0:T(8,128)(2,1)} %refs_0_.1, bf16[1,512,512]{2,1,0:T(8,128)(2,1)} %refs_1_.1), custom_call_target="tpu_custom_call" | custom-call | flops 5368709120 | bytes 6291456 | tf_op jit(solution)/shard_map/pallas_call | solution.py:149
  31.8 0.0 collective-permute-done.refs_3_
  31.8 6.9 %collective-permute-done.1.refs_4_ = bf16[1,512,512]{2,1,0:T(8,128)(2,1)} collective-permute-done((bf16[1,512,512]{2,1,0:T(8,128)(2,1)S(1)}, bf16[1,512,512]{2,1,0:T(8,128)(2,1)}, u32[]{:S(2)}, u32[]{:S(2)}) %collective-permute-start.1) | collective-permute-done | bytes 524320 | tf_op jit(solution)/shard_map/ppermute | solution.py:23
  38.7 0.0 collective-permute-done.2.refs_5_
  38.7 0.0 copy-start
  38.7 41.6 %shard_map.157 = bf16[1,512,2560]{2,1,0:T(8,128)(2,1)} custom-call(s32[1]{0:T(128)S(6)} %sub.104.t0_ref, bf16[1,512,2560]{2,1,0:T(8,128)(2,1)} %q_ref.3, f32[1,10,512,128]{3,2,1,0:T(8,128)} %get-tuple-element.10.refs_0_, f32[1,10,512,128]{3,2,1,0:T(8,128)} %get-tuple-element.11.refs_1_, f32[1,10,512,256]{3,2,1,0:T(8,128)} %get-tuple-element.12.refs_2_, ...), custom_call_target="tpu_custom_call" | custom-call | flops 8053063680 | bytes 6815744 | tf_op jit(solution)/shard_map/pallas_call | solution.py:149
  80.3 0.0 copy-start.3
  80.3 0.0 copy-start.4
  80.3 0.8 slice_bitcast_fusion.1
  81.2 18.8 %all-gather = bf16[8,2,2560]{2,1,0:T(2,128)(2,1)S(1)} all-gather(bf16[1,2,2560]{2,1,0:T(2,128)(2,1)S(1)} %maximum_bitcast_fusion), channel_id=1, replica_groups=mesh['seq'=4,'vocab'=8] {'vocab'}, dimensions={0}, use_global_device_ids=true | all-gather | bytes 92160 | tf_op jit(solution)/shard_map/all_gather | solution.py:268
  100.0 0.0 copy-done
  100.0 0.4 fusion.27
  100.4 0.8 reshape.156
  101.2 3.4 %all-to-all-start = ((f32[8,2,2560]{2,1,0:T(2,128)}), f32[8,2,2560]{2,1,0:T(2,128)S(1)}, u32[]{:S(2)}, u32[]{:S(2)}) async-start(f32[8,2,2560]{2,1,0:T(2,128)} %reshape.156), calls=%async_computation | async-start | bytes 327680 | tf_op jit(solution)/shard_map/all_to_all | solution.py:273
  104.6 0.8 slice_bitcast_fusion.2
  105.4 10.3 %all-to-all-done = f32[8,2,2560]{2,1,0:T(2,128)S(1)} async-done(((f32[8,2,2560]{2,1,0:T(2,128)}), f32[8,2,2560]{2,1,0:T(2,128)S(1)}, u32[]{:S(2)}, u32[]{:S(2)}) %all-to-all-start) | async-done | bytes 163872 | tf_op jit(solution)/shard_map/all_to_all | solution.py:273
  115.7 0.1 reduce_sum.46
  115.7 0.0 copy-done.3
  115.7 0.2 fusion.24
  115.9 0.0 copy-done.4
  115.9 0.1 fusion.30
  116.0 14.1 %all-gather.1 = bf16[8,2,2560]{2,1,0:T(2,128)(2,1)S(1)} all-gather(bf16[1,2,2560]{2,1,0:T(2,128)(2,1)S(1)} %fusion.30), channel_id=1, replica_groups=mesh['seq'=4,'vocab'=8] {'vocab'}, dimensions={0}, use_global_device_ids=true | all-gather | bytes 92160 | tf_op jit(solution)/shard_map/all_gather | solution.py:27
  130.1 9.4 %all_gather.14 = bf16[64,2560]{1,0:T(8,128)(2,1)S(1)} all-gather(bf16[16,2560]{1,0:T(8,128)(2,1)S(1)} %reshape.166), channel_id=1, replica_groups=mesh['seq'=4,'vocab'=8] {'seq'}, dimensions={0}, use_global_device_ids=true | all-gather | bytes 409600 | tf_op jit(solution)/shard_map/all_gather | solution.py:28
  139.6 0.1 reshape.157
  139.7 0.1 slice.59
  139.8 18.1 %fusion.44 = (f32[40]{0:T(128)S(1)}, f32[40,8000]{1,0:T(8,128)S(1)}) fusion(bf16[8000,2560]{1,0:T(8,128)(2,1)} %param.25, bf16[8,2560]{1,0:T(8,128)(2,1)S(1)} %bitcast.65, bf16[32,2560]{1,0:T(8,128)(2,1)S(1)} %bitcast.64), kind=kOutput, calls=%fused_computation.80 | convolution fusion | flops 1639129600 | bytes 42444960 | tf_op jit(solution)/shard_map/dot_general | solution.py:283
  157.9 0.4 exponential_reduce_fusion
  158.3 0.1 collective-permute-start.3
  158.4 0.0 all-gather.4.cloned.1.call-done
  158.4 0.0 copy-start.1
  158.4 11.0 %fusion.2 = f32[513,2560]{1,0:T(8,128)S(1)} fusion(bf16[2560,2560]{1,0:T(8,128)(2,1)} %all-gather.4.cloned.1.call-done, bf16[1,2560]{1,0:T(2,128)(2,1)S(1)} %bitcast.70, bf16[512,2560]{1,0:T(8,128)(2,1)} %bitcast.74), kind=kOutput, calls=%fused_computation.3 | convolution fusion | flops 6729246720 | bytes 20986880 | tf_op jit(solution)/shard_map/dot_general | solution.py:251
  169.5 0.0 copy-done.1
  169.5 2.3 %fusion.1 = bf16[1,512,2560]{2,1,0:T(8,128)(2,1)} fusion(f32[513,2560]{1,0:T(8,128)S(1)} %fusion.2, bf16[1,512,2560]{2,1,0:T(8,128)(2,1)S(1)} %copy-done.1), kind=kLoop, calls=%fused_computation.2 | loop fusion | flops 3932160 | bytes 10485760 | tf_op jit(solution)/shard_map/convert_element_type | solution.py:259
  171.7 0.6 fusion.29
  172.4 0.0 collective-permute-done.3
  172.4 2.4 %collective-permute-start.4 = (f32[2,2,40]{2,1,0:T(2,128)S(1)}, f32[2,2,40]{2,1,0:T(2,128)S(1)}, u32[]{:S(2)}, u32[]{:S(2)}) collective-permute-start(f32[2,2,40]{2,1,0:T(2,128)S(1)} %maximum_select_fusion.4), channel_id=1, source_target_pairs={{0,2},{1,3},{2,0},{3,1},{4,6},{5,7},{6,4},{7,5},{8,10},{9,11},{10,... | collective-permute-start | bytes 1928 | tf_op jit(solution)/shard_map/ppermute | solution.py:40
  174.8 1.6 collective-permute-done.4
  176.3 1.3 collective-permute-start.5
  177.7 3.2 %collective-permute-done.5 = f32[4,2,40]{2,1,0:T(2,128)S(1)} collective-permute-done((f32[4,2,40]{2,1,0:T(2,128)S(1)}, f32[4,2,40]{2,1,0:T(2,128)S(1)}, u32[]{:S(2)}, u32[]{:S(2)}) %collective-permute-start.5) | collective-permute-done | bytes 1312 | tf_op jit(solution)/shard_map/ppermute | solution.py:40
  180.8 1.5 collective-permute-start.6
  182.4 2.2 %collective-permute-done.6 = f32[8,2,40]{2,1,0:T(2,128)S(1)} collective-permute-done((f32[8,2,40]{2,1,0:T(2,128)S(1)}, f32[8,2,40]{2,1,0:T(2,128)S(1)}, u32[]{:S(2)}, u32[]{:S(2)}) %collective-permute-start.6) | collective-permute-done | bytes 2592 | tf_op jit(solution)/shard_map/ppermute | solution.py:40
  184.6 1.6 collective-permute-start.7
  186.1 2.3 %collective-permute-done.7 = f32[16,2,40]{2,1,0:T(2,128)S(1)} collective-permute-done((f32[16,2,40]{2,1,0:T(2,128)S(1)}, f32[16,2,40]{2,1,0:T(2,128)S(1)}, u32[]{:S(2)}, u32[]{:S(2)}) %collective-permute-start.7) | collective-permute-done | bytes 5152 | tf_op jit(solution)/shard_map/ppermute | solution.py:40
  188.5 0.1 subtract_convert_fusion
  188.7 0.8 slice.64
  189.5 0.7 slice.65
  (24 shorter events, 0.4 us)
Async XLA Ops:
  7.2 8.5 %copy-start.5 = (bf16[1,2560]{1,0:T(2,128)(2,1)S(1)}, bf16[1,2560]{1,0:T(2,128)(2,1)}, u32[]{:S(2)}) copy-start(bf16[1,2560]{1,0:T(2,128)(2,1)} %param.18) | copy-start | bytes 15364
  7.2 8.6 %copy-start.6 = (bf16[1,512]{1,0:T(2,128)(2,1)S(1)}, bf16[1,512]{1,0:T(2,128)(2,1)}, u32[]{:S(2)}) copy-start(bf16[1,512]{1,0:T(2,128)(2,1)} %param.19) | copy-start | bytes 3076
  7.2 8.7 %copy-start.2 = (bf16[1,2048,512]{2,1,0:T(8,128)(2,1)S(1)}, bf16[1,2048,512]{2,1,0:T(8,128)(2,1)}, u32[]{:S(2)}) copy-start(bf16[1,2048,512]{2,1,0:T(8,128)(2,1)} %param.20) | copy-start | bytes 6291460
  7.2 151.2 %all-gather.4.cloned.1.call-start = ((), (), s32[]{:S(2)}) async-start(), calls=%async_computation.1 | async-start | bytes 14745600 | tf_op jit(solution)/shard_map/all_gather | solution.py:253
  10.0 21.8 %collective-permute-start = (bf16[1,512,512]{2,1,0:T(8,128)(2,1)}, bf16[1,512,512]{2,1,0:T(8,128)(2,1)}, u32[]{:S(2)}, u32[]{:S(2)}) collective-permute-start(bf16[1,512,512]{2,1,0:T(8,128)(2,1)} %get-tuple-element.21), channel_id=1, source_target_pairs={{0,24},{8,0},{16,8},{24,16},{1,25},{9,1},{17,9},{25,17},{2,26},{10... | collective-permute-start | bytes 1572872 | tf_op jit(solution)/shard_map/ppermute | solution.py:23
  13.9 24.7 %collective-permute-start.1 = (bf16[1,512,512]{2,1,0:T(8,128)(2,1)S(1)}, bf16[1,512,512]{2,1,0:T(8,128)(2,1)}, u32[]{:S(2)}, u32[]{:S(2)}) collective-permute-start(bf16[1,512,512]{2,1,0:T(8,128)(2,1)S(1)} %get-tuple-element.22), channel_id=1, source_target_pairs={{0,16},{8,24},{16,0},{24,8},{1,17},{9,25},{17,1},{25,9},{2,18},{10... | collective-permute-start | bytes 1572872 | tf_op jit(solution)/shard_map/ppermute | solution.py:23
  14.4 24.2 %collective-permute-start.2 = (bf16[1,512,512]{2,1,0:T(8,128)(2,1)S(1)}, bf16[1,512,512]{2,1,0:T(8,128)(2,1)}, u32[]{:S(2)}, u32[]{:S(2)}) collective-permute-start(bf16[1,512,512]{2,1,0:T(8,128)(2,1)S(1)} %get-tuple-element.20), channel_id=1, source_target_pairs={{0,8},{8,16},{16,24},{24,0},{1,9},{9,17},{17,25},{25,1},{2,10},{10... | collective-permute-start | bytes 1572872 | tf_op jit(solution)/shard_map/ppermute | solution.py:23
  38.7 61.3 %copy-start = (bf16[320,2560]{1,0:T(8,128)(2,1)S(1)}, bf16[320,2560]{1,0:T(8,128)(2,1)}, u32[]{:S(2)}) copy-start(bf16[320,2560]{1,0:T(8,128)(2,1)} %param.23) | copy-start | bytes 4915204
  80.3 35.4 %copy-start.3 = (bf16[1,2560]{1,0:T(2,128)(2,1)S(1)}, bf16[1,2560]{1,0:T(2,128)(2,1)}, u32[]{:S(2)}) copy-start(bf16[1,2560]{1,0:T(2,128)(2,1)} %param.22) | copy-start | bytes 15364
  80.3 35.6 %copy-start.4 = (f32[2560]{0:T(1024)S(1)}, f32[2560]{0:T(1024)}, u32[]{:S(2)}) copy-start(f32[2560]{0:T(1024)} %param.24) | copy-start | bytes 30724
  101.2 14.5 %all-to-all-start = ((f32[8,2,2560]{2,1,0:T(2,128)}), f32[8,2,2560]{2,1,0:T(2,128)S(1)}, u32[]{:S(2)}, u32[]{:S(2)}) async-start(f32[8,2,2560]{2,1,0:T(2,128)} %reshape.156), calls=%async_computation | async-start | bytes 327680 | tf_op jit(solution)/shard_map/all_to_all | solution.py:273
  158.3 14.1 %collective-permute-start.3 = (f32[1,2,40]{2,1,0:T(2,128)S(1)}, f32[1,2,40]{2,1,0:T(2,128)S(1)}, u32[]{:S(2)}, u32[]{:S(2)}) collective-permute-start(f32[1,2,40]{2,1,0:T(2,128)S(1)} %maximum_bitcast_fusion.1), channel_id=1, source_target_pairs={{0,1},{1,0},{2,3},{3,2},{4,5},{5,4},{6,7},{7,6},{8,9},{9,8},{10,11... | collective-permute-start | bytes 968 | tf_op jit(solution)/shard_map/ppermute | solution.py:40
  158.4 11.0 %copy-start.1 = (bf16[1,512,2560]{2,1,0:T(8,128)(2,1)S(1)}, bf16[1,512,2560]{2,1,0:T(8,128)(2,1)}, u32[]{:S(2)}) copy-start(bf16[1,512,2560]{2,1,0:T(8,128)(2,1)} %param.17) | copy-start | bytes 7864324
  172.4 3.9 %collective-permute-start.4 = (f32[2,2,40]{2,1,0:T(2,128)S(1)}, f32[2,2,40]{2,1,0:T(2,128)S(1)}, u32[]{:S(2)}, u32[]{:S(2)}) collective-permute-start(f32[2,2,40]{2,1,0:T(2,128)S(1)} %maximum_select_fusion.4), channel_id=1, source_target_pairs={{0,2},{1,3},{2,0},{3,1},{4,6},{5,7},{6,4},{7,5},{8,10},{9,11},{10,... | collective-permute-start | bytes 1928 | tf_op jit(solution)/shard_map/ppermute | solution.py:40
  176.3 4.5 %collective-permute-start.5 = (f32[4,2,40]{2,1,0:T(2,128)S(1)}, f32[4,2,40]{2,1,0:T(2,128)S(1)}, u32[]{:S(2)}, u32[]{:S(2)}) collective-permute-start(f32[4,2,40]{2,1,0:T(2,128)S(1)} %maximum_select_fusion.3), channel_id=1, source_target_pairs={{0,4},{1,5},{2,6},{3,7},{4,0},{5,1},{6,2},{7,3},{8,12},{9,13},{10,... | collective-permute-start | bytes 3848 | tf_op jit(solution)/shard_map/ppermute | solution.py:40
  180.8 3.7 %collective-permute-start.6 = (f32[8,2,40]{2,1,0:T(2,128)S(1)}, f32[8,2,40]{2,1,0:T(2,128)S(1)}, u32[]{:S(2)}, u32[]{:S(2)}) collective-permute-start(f32[8,2,40]{2,1,0:T(2,128)S(1)} %maximum_select_fusion.2), channel_id=1, source_target_pairs={{0,8},{8,0},{16,24},{24,16},{1,9},{9,1},{17,25},{25,17},{2,10},{10... | collective-permute-start | bytes 7688 | tf_op jit(solution)/shard_map/ppermute | solution.py:40
  184.6 3.8 %collective-permute-start.7 = (f32[16,2,40]{2,1,0:T(2,128)S(1)}, f32[16,2,40]{2,1,0:T(2,128)S(1)}, u32[]{:S(2)}, u32[]{:S(2)}) collective-permute-start(f32[16,2,40]{2,1,0:T(2,128)S(1)} %maximum_select_fusion.1), channel_id=1, source_target_pairs={{0,16},{8,24},{16,0},{24,8},{1,17},{9,25},{17,1},{25,9},{2,18},{10... | collective-permute-start | bytes 15368 | tf_op jit(solution)/shard_map/ppermute | solution.py:40
Sparse Core Ops, SparseCore 0:
  9.7 128.4 all-gather.3

commit v11 on v8

--- a/solution.py
+++ b/solution.py
@@ -246,9 +246,10 @@
     global_peak = jnp.max(stats[:, 0], axis=0)
     global_sum = jnp.sum(stats[:, 1] * jnp.exp(stats[:, 0] - global_peak[None]), axis=0)
     total = (global_peak + jnp.log(global_sum))[:, None]
-    log_probs = (logits - total).astype(jnp.bfloat16)
     dec_count = decode_all.shape[0]
-    return (pre_out, dec_out, log_probs[:dec_count], log_probs[dec_count:])
+    dec_logp = (logits[:dec_count] - total[:dec_count]).astype(jnp.bfloat16)
+    pre_logp = (logits[dec_count:] - total[dec_count:]).astype(jnp.bfloat16)
+    return (pre_out, dec_out, dec_logp, pre_logp)
 
 
 def solution(mesh):

time: 181 us -> 181 us (level)
  no operation moved by 1% of the time
where the time goes in v11:
time: 181 us; the launch traced here: 180 us
  blocking collectives  40.4 us (22%)
  waiting for transfers between devices  35.4 us (20%)
  matrix products  30.7 us (17%)
  Pallas kernels  26.8 us (15%)
  starting transfers between devices  20.8 us (11%)
  between operations  15.6 us (9%)
  other arithmetic  7.78 us (4%)
  local copies, waits for them, and re-layouts  2.86 us (2%)
    pallas_call x1, Pallas kernels, prefill_attention(): pl.pallas_call(kernel, out_shape=jax.ShapeDtypeStruct(pre_query.shape, jn...  26.8 us
    ppermute x3, waiting for transfers between devices, from_behind(): return lax.ppermute(value, axis, pairs)  19.1 us
    dot_general x1, matrix products, body(): lax.dot_general(head_rows, embedding, (((1,), (1,)), ((), ())), preferred...  18.3 us
    all_gather x1, blocking collectives, body(): group_rows = lax.all_gather(head_mixed, 'vocab', axis=0, tiled=True)  16.7 us
    all_gather x1, blocking collectives, gather_all(): inner = lax.all_gather(value, 'vocab', axis=0, tiled=True)  14.9 us
    dot_general x1, matrix products, body(): jnp.dot(mixed_rows, lax.all_gather(out_weight, 'vocab', axis=0, tiled=Tru...  11 us
    ppermute x5, starting transfers between devices, doubling_gather(): theirs = lax.ppermute(value, axis, pairs)  10.1 us
    all_gather x1, blocking collectives, gather_all(): return lax.all_gather(inner, 'seq', axis=0, tiled=True)  8.83 us
  transfers between devices with their start and end apart: 10, of which 8 were waited for; matrix products, arithmetic and copies ran while one was open for 22% of the time, Pallas kernels for 15%

profile of v11, /device:TPU:0, one launch (start us, length us, event | category | flops | bytes accessed | tf_op | source)
XLA Modules:
  0.0 180.4 jit_solution(7398273568876830191)
XLA Ops:
  7.2 0.0 copy-start.5
  7.2 0.0 copy-start.6
  7.2 0.0 copy-start.2
  7.2 0.0 all-gather.4.cloned.1.call-start
  7.2 0.7 all-gather.4.cloned.1.call-update
  7.9 2.1 %broadcast_select_fusion = (bf16[1,512,512]{2,1,0:T(8,128)(2,1)}, bf16[1,512,512]{2,1,0:T(8,128)(2,1)S(1)}, bf16[1,512,512]{2,1,0:T(8,128)(2,1)S(1)}) fusion(bf16[1,512,512]{2,1,0:T(8,128)(2,1)} %refs_4_.1, bf16[1,512,512]{2,1,0:T(8,128)(2,1)} %refs_0_.1, pred[]{:T(512)S(6)} %le.11, pred[]{:T(512)S(6)} %le.10, pred[]{:T(512)S(6)} %le.9), kind=kLoop, calls=%fused_computation.21 | loop fusion | flops 786432 | bytes 2621443 | tf_op jit(solution)/shard_map/jit(_where)/select_n | solution.py:160
  10.0 2.9 %collective-permute-start.2 = (bf16[1,512,512]{2,1,0:T(8,128)(2,1)}, bf16[1,512,512]{2,1,0:T(8,128)(2,1)}, u32[]{:S(2)}, u32[]{:S(2)}) collective-permute-start(bf16[1,512,512]{2,1,0:T(8,128)(2,1)} %get-tuple-element.14), channel_id=1, source_target_pairs={{0,8},{8,16},{16,24},{24,0},{1,9},{9,17},{17,25},{25,1},{2,10},{10... | collective-permute-start | bytes 1572872 | tf_op jit(solution)/shard_map/ppermute | solution.py:23
  13.0 1.5 collective-permute-start.1
  14.5 1.4 collective-permute-start
  16.6 0.0 copy-done.5
  16.7 0.0 copy-done.6
  16.7 0.1 fusion.9
  16.8 0.0 copy-done.2
  16.8 0.5 select_reduce_fusion
  18.0 0.2 fusion.20
  18.2 0.3 fusion.8
  18.5 0.0 copy-start
  18.6 8.5 %collective-permute-done.2.refs_3_ = bf16[1,512,512]{2,1,0:T(8,128)(2,1)} collective-permute-done((bf16[1,512,512]{2,1,0:T(8,128)(2,1)}, bf16[1,512,512]{2,1,0:T(8,128)(2,1)}, u32[]{:S(2)}, u32[]{:S(2)}) %collective-permute-start.2) | collective-permute-done | bytes 524320 | tf_op jit(solution)/shard_map/ppermute | solution.py:23
  27.0 10.4 %collective-permute-done.1.refs_2_ = bf16[1,512,512]{2,1,0:T(8,128)(2,1)} collective-permute-done((bf16[1,512,512]{2,1,0:T(8,128)(2,1)S(1)}, bf16[1,512,512]{2,1,0:T(8,128)(2,1)}, u32[]{:S(2)}, u32[]{:S(2)}) %collective-permute-start.1) | collective-permute-done | bytes 524320 | tf_op jit(solution)/shard_map/ppermute | solution.py:23
  37.4 0.3 collective-permute-done.refs_1_
  37.7 26.8 %shard_map.156 = bf16[1,512,2560]{2,1,0:T(8,128)(2,1)} custom-call(s32[1]{0:T(128)S(6)} %sub.112.t0_ref, bf16[1,512,2560]{2,1,0:T(8,128)(2,1)} %q_ref.1, bf16[1,512,512]{2,1,0:T(8,128)(2,1)} %refs_0_.1, bf16[1,512,512]{2,1,0:T(8,128)(2,1)} %collective-permute-done.refs_1_, bf16[1,512,512]{2,1,0:T(8,128)(2,1)} %collective-permute-done.1.refs_2_, ...), custom_call_target="tpu_custom_call" | custom-call | flops 13421772800 | bytes 7864320 | tf_op jit(solution)/shard_map/pallas_call | solution.py:116
  64.5 0.0 copy-start.3
  64.5 0.0 copy-start.4
  64.5 0.8 slice_bitcast_fusion.1
  65.4 16.7 %all-gather = bf16[8,2,2560]{2,1,0:T(2,128)(2,1)S(1)} all-gather(bf16[1,2,2560]{2,1,0:T(2,128)(2,1)S(1)} %maximum_bitcast_fusion), channel_id=1, replica_groups=mesh['seq'=4,'vocab'=8] {'vocab'}, dimensions={0}, use_global_device_ids=true | all-gather | bytes 92160 | tf_op jit(solution)/shard_map/all_gather | solution.py:223
  82.1 0.0 copy-done
  82.1 0.4 fusion.29
  82.5 0.8 reshape.154
  83.3 4.7 %all-to-all-start = ((f32[8,2,2560]{2,1,0:T(2,128)}), f32[8,2,2560]{2,1,0:T(2,128)S(1)}, u32[]{:S(2)}, u32[]{:S(2)}) async-start(f32[8,2,2560]{2,1,0:T(2,128)} %reshape.154), calls=%async_computation | async-start | bytes 327680 | tf_op jit(solution)/shard_map/all_to_all | solution.py:228
  88.1 0.8 slice_bitcast_fusion.2
  88.9 8.6 %all-to-all-done = f32[8,2,2560]{2,1,0:T(2,128)S(1)} async-done(((f32[8,2,2560]{2,1,0:T(2,128)}), f32[8,2,2560]{2,1,0:T(2,128)S(1)}, u32[]{:S(2)}, u32[]{:S(2)}) %all-to-all-start) | async-done | bytes 163872 | tf_op jit(solution)/shard_map/all_to_all | solution.py:228
  97.5 0.1 reduce_sum.46
  97.5 0.0 copy-done.3
  97.5 0.2 fusion.26
  97.7 0.0 copy-done.4
  97.7 0.1 fusion.32
  97.8 14.9 %all-gather.1 = bf16[8,2,2560]{2,1,0:T(2,128)(2,1)S(1)} all-gather(bf16[1,2,2560]{2,1,0:T(2,128)(2,1)S(1)} %fusion.32), channel_id=1, replica_groups=mesh['seq'=4,'vocab'=8] {'vocab'}, dimensions={0}, use_global_device_ids=true | all-gather | bytes 92160 | tf_op jit(solution)/shard_map/all_gather | solution.py:27
  112.8 8.8 %all_gather.14 = bf16[64,2560]{1,0:T(8,128)(2,1)S(1)} all-gather(bf16[16,2560]{1,0:T(8,128)(2,1)S(1)} %reshape.164), channel_id=1, replica_groups=mesh['seq'=4,'vocab'=8] {'seq'}, dimensions={0}, use_global_device_ids=true | all-gather | bytes 409600 | tf_op jit(solution)/shard_map/all_gather | solution.py:28
  121.6 0.1 reshape.155
  121.7 0.1 slice.69
  121.9 18.3 %fusion.46 = (f32[40]{0:T(128)S(1)}, f32[40,8000]{1,0:T(8,128)S(1)}) fusion(bf16[8000,2560]{1,0:T(8,128)(2,1)} %param.25, bf16[8,2560]{1,0:T(8,128)(2,1)S(1)} %bitcast.66, bf16[32,2560]{1,0:T(8,128)(2,1)S(1)} %bitcast.65), kind=kOutput, calls=%fused_computation.83 | convolution fusion | flops 1639129600 | bytes 42444960 | tf_op jit(solution)/shard_map/dot_general | solution.py:238
  140.2 0.4 exponential_reduce_fusion
  140.6 0.1 collective-permute-start.3
  140.7 0.0 all-gather.4.cloned.1.call-done
  140.7 0.0 copy-start.1
  140.7 11.0 %fusion.2 = f32[513,2560]{1,0:T(8,128)S(1)} fusion(bf16[2560,2560]{1,0:T(8,128)(2,1)} %all-gather.4.cloned.1.call-done, bf16[1,2560]{1,0:T(2,128)(2,1)S(1)} %bitcast.71, bf16[512,2560]{1,0:T(8,128)(2,1)} %bitcast.76), kind=kOutput, calls=%fused_computation.3 | convolution fusion | flops 6729246720 | bytes 20986880 | tf_op jit(solution)/shard_map/dot_general | solution.py:206
  151.7 0.0 copy-done.1
  151.8 2.3 %fusion.1 = bf16[1,512,2560]{2,1,0:T(8,128)(2,1)} fusion(f32[513,2560]{1,0:T(8,128)S(1)} %fusion.2, bf16[1,512,2560]{2,1,0:T(8,128)(2,1)S(1)} %copy-done.1), kind=kLoop, calls=%fused_computation.2 | loop fusion | flops 3932160 | bytes 10485760 | tf_op jit(solution)/shard_map/convert_element_type | solution.py:214
  154.0 0.6 fusion.31
  154.7 0.0 collective-permute-done.3
  154.7 2.6 %collective-permute-start.4 = (f32[2,2,40]{2,1,0:T(2,128)S(1)}, f32[2,2,40]{2,1,0:T(2,128)S(1)}, u32[]{:S(2)}, u32[]{:S(2)}) collective-permute-start(f32[2,2,40]{2,1,0:T(2,128)S(1)} %maximum_select_fusion.4), channel_id=1, source_target_pairs={{0,2},{1,3},{2,0},{3,1},{4,6},{5,7},{6,4},{7,5},{8,10},{9,11},{10,... | collective-permute-start | bytes 1928 | tf_op jit(solution)/shard_map/ppermute | solution.py:40
  157.2 1.6 collective-permute-done.4
  158.8 3.7 %collective-permute-start.5 = (f32[4,2,40]{2,1,0:T(2,128)S(1)}, f32[4,2,40]{2,1,0:T(2,128)S(1)}, u32[]{:S(2)}, u32[]{:S(2)}) collective-permute-start(f32[4,2,40]{2,1,0:T(2,128)S(1)} %maximum_select_fusion.3), channel_id=1, source_target_pairs={{0,4},{1,5},{2,6},{3,7},{4,0},{5,1},{6,2},{7,3},{8,12},{9,13},{10,... | collective-permute-start | bytes 3848 | tf_op jit(solution)/shard_map/ppermute | solution.py:40
  162.5 1.6 collective-permute-done.5
  164.1 1.9 %collective-permute-start.6 = (f32[8,2,40]{2,1,0:T(2,128)S(1)}, f32[8,2,40]{2,1,0:T(2,128)S(1)}, u32[]{:S(2)}, u32[]{:S(2)}) collective-permute-start(f32[8,2,40]{2,1,0:T(2,128)S(1)} %maximum_select_fusion.2), channel_id=1, source_target_pairs={{0,8},{8,0},{16,24},{24,16},{1,9},{9,1},{17,25},{25,17},{2,10},{10... | collective-permute-start | bytes 7688 | tf_op jit(solution)/shard_map/ppermute | solution.py:40
  166.0 1.8 %collective-permute-done.6 = f32[8,2,40]{2,1,0:T(2,128)S(1)} collective-permute-done((f32[8,2,40]{2,1,0:T(2,128)S(1)}, f32[8,2,40]{2,1,0:T(2,128)S(1)}, u32[]{:S(2)}, u32[]{:S(2)}) %collective-permute-start.6) | collective-permute-done | bytes 2592 | tf_op jit(solution)/shard_map/ppermute | solution.py:40
  167.9 1.9 %collective-permute-start.7 = (f32[16,2,40]{2,1,0:T(2,128)S(1)}, f32[16,2,40]{2,1,0:T(2,128)S(1)}, u32[]{:S(2)}, u32[]{:S(2)}) collective-permute-start(f32[16,2,40]{2,1,0:T(2,128)S(1)} %maximum_select_fusion.1), channel_id=1, source_target_pairs={{0,16},{8,24},{16,0},{24,8},{1,17},{9,25},{17,1},{25,9},{2,18},{10... | collective-permute-start | bytes 15368 | tf_op jit(solution)/shard_map/ppermute | solution.py:40
  169.8 1.9 %collective-permute-done.7 = f32[16,2,40]{2,1,0:T(2,128)S(1)} collective-permute-done((f32[16,2,40]{2,1,0:T(2,128)S(1)}, f32[16,2,40]{2,1,0:T(2,128)S(1)}, u32[]{:S(2)}, u32[]{:S(2)}) %collective-permute-start.7) | collective-permute-done | bytes 5152 | tf_op jit(solution)/shard_map/ppermute | solution.py:40
  171.8 0.1 slice.66
  171.9 0.7 fusion.15
  172.6 0.9 fusion.14
  (24 shorter events, 0.4 us)
Async XLA Ops:
  7.2 9.4 %copy-start.5 = (bf16[1,2560]{1,0:T(2,128)(2,1)S(1)}, bf16[1,2560]{1,0:T(2,128)(2,1)}, u32[]{:S(2)}) copy-start(bf16[1,2560]{1,0:T(2,128)(2,1)} %param.18) | copy-start | bytes 15364
  7.2 9.5 %copy-start.6 = (bf16[1,512]{1,0:T(2,128)(2,1)S(1)}, bf16[1,512]{1,0:T(2,128)(2,1)}, u32[]{:S(2)}) copy-start(bf16[1,512]{1,0:T(2,128)(2,1)} %param.19) | copy-start | bytes 3076
  7.2 9.6 %copy-start.2 = (bf16[1,2048,512]{2,1,0:T(8,128)(2,1)S(1)}, bf16[1,2048,512]{2,1,0:T(8,128)(2,1)}, u32[]{:S(2)}) copy-start(bf16[1,2048,512]{2,1,0:T(8,128)(2,1)} %param.20) | copy-start | bytes 6291460
  7.2 133.5 %all-gather.4.cloned.1.call-start = ((), (), s32[]{:S(2)}) async-start(), calls=%async_computation.1 | async-start | bytes 14745600 | tf_op jit(solution)/shard_map/all_gather | solution.py:208
  10.0 17.0 %collective-permute-start.2 = (bf16[1,512,512]{2,1,0:T(8,128)(2,1)}, bf16[1,512,512]{2,1,0:T(8,128)(2,1)}, u32[]{:S(2)}, u32[]{:S(2)}) collective-permute-start(bf16[1,512,512]{2,1,0:T(8,128)(2,1)} %get-tuple-element.14), channel_id=1, source_target_pairs={{0,8},{8,16},{16,24},{24,0},{1,9},{9,17},{17,25},{25,1},{2,10},{10... | collective-permute-start | bytes 1572872 | tf_op jit(solution)/shard_map/ppermute | solution.py:23
  13.0 24.4 %collective-permute-start.1 = (bf16[1,512,512]{2,1,0:T(8,128)(2,1)S(1)}, bf16[1,512,512]{2,1,0:T(8,128)(2,1)}, u32[]{:S(2)}, u32[]{:S(2)}) collective-permute-start(bf16[1,512,512]{2,1,0:T(8,128)(2,1)S(1)} %get-tuple-element.15), channel_id=1, source_target_pairs={{0,16},{8,24},{16,0},{24,8},{1,17},{9,25},{17,1},{25,9},{2,18},{10... | collective-permute-start | bytes 1572872 | tf_op jit(solution)/shard_map/ppermute | solution.py:23
  14.5 23.2 %collective-permute-start = (bf16[1,512,512]{2,1,0:T(8,128)(2,1)S(1)}, bf16[1,512,512]{2,1,0:T(8,128)(2,1)}, u32[]{:S(2)}, u32[]{:S(2)}) collective-permute-start(bf16[1,512,512]{2,1,0:T(8,128)(2,1)S(1)} %get-tuple-element.16), channel_id=1, source_target_pairs={{0,24},{8,0},{16,8},{24,16},{1,25},{9,1},{17,9},{25,17},{2,26},{10... | collective-permute-start | bytes 1572872 | tf_op jit(solution)/shard_map/ppermute | solution.py:23
  18.5 63.6 %copy-start = (bf16[320,2560]{1,0:T(8,128)(2,1)S(1)}, bf16[320,2560]{1,0:T(8,128)(2,1)}, u32[]{:S(2)}) copy-start(bf16[320,2560]{1,0:T(8,128)(2,1)} %param.23) | copy-start | bytes 4915204
  64.5 33.0 %copy-start.3 = (bf16[1,2560]{1,0:T(2,128)(2,1)S(1)}, bf16[1,2560]{1,0:T(2,128)(2,1)}, u32[]{:S(2)}) copy-start(bf16[1,2560]{1,0:T(2,128)(2,1)} %param.22) | copy-start | bytes 15364
  64.5 33.2 %copy-start.4 = (f32[2560]{0:T(1024)S(1)}, f32[2560]{0:T(1024)}, u32[]{:S(2)}) copy-start(f32[2560]{0:T(1024)} %param.24) | copy-start | bytes 30724
  83.3 14.2 %all-to-all-start = ((f32[8,2,2560]{2,1,0:T(2,128)}), f32[8,2,2560]{2,1,0:T(2,128)S(1)}, u32[]{:S(2)}, u32[]{:S(2)}) async-start(f32[8,2,2560]{2,1,0:T(2,128)} %reshape.154), calls=%async_computation | async-start | bytes 327680 | tf_op jit(solution)/shard_map/all_to_all | solution.py:228
  140.6 14.1 %collective-permute-start.3 = (f32[1,2,40]{2,1,0:T(2,128)S(1)}, f32[1,2,40]{2,1,0:T(2,128)S(1)}, u32[]{:S(2)}, u32[]{:S(2)}) collective-permute-start(f32[1,2,40]{2,1,0:T(2,128)S(1)} %maximum_bitcast_fusion.1), channel_id=1, source_target_pairs={{0,1},{1,0},{2,3},{3,2},{4,5},{5,4},{6,7},{7,6},{8,9},{9,8},{10,11... | collective-permute-start | bytes 968 | tf_op jit(solution)/shard_map/ppermute | solution.py:40
  140.7 11.0 %copy-start.1 = (bf16[1,512,2560]{2,1,0:T(8,128)(2,1)S(1)}, bf16[1,512,2560]{2,1,0:T(8,128)(2,1)}, u32[]{:S(2)}) copy-start(bf16[1,512,2560]{2,1,0:T(8,128)(2,1)} %param.17) | copy-start | bytes 7864324
  154.7 4.1 %collective-permute-start.4 = (f32[2,2,40]{2,1,0:T(2,128)S(1)}, f32[2,2,40]{2,1,0:T(2,128)S(1)}, u32[]{:S(2)}, u32[]{:S(2)}) collective-permute-start(f32[2,2,40]{2,1,0:T(2,128)S(1)} %maximum_select_fusion.4), channel_id=1, source_target_pairs={{0,2},{1,3},{2,0},{3,1},{4,6},{5,7},{6,4},{7,5},{8,10},{9,11},{10,... | collective-permute-start | bytes 1928 | tf_op jit(solution)/shard_map/ppermute | solution.py:40
  158.8 5.3 %collective-permute-start.5 = (f32[4,2,40]{2,1,0:T(2,128)S(1)}, f32[4,2,40]{2,1,0:T(2,128)S(1)}, u32[]{:S(2)}, u32[]{:S(2)}) collective-permute-start(f32[4,2,40]{2,1,0:T(2,128)S(1)} %maximum_select_fusion.3), channel_id=1, source_target_pairs={{0,4},{1,5},{2,6},{3,7},{4,0},{5,1},{6,2},{7,3},{8,12},{9,13},{10,... | collective-permute-start | bytes 3848 | tf_op jit(solution)/shard_map/ppermute | solution.py:40
  164.1 3.7 %collective-permute-start.6 = (f32[8,2,40]{2,1,0:T(2,128)S(1)}, f32[8,2,40]{2,1,0:T(2,128)S(1)}, u32[]{:S(2)}, u32[]{:S(2)}) collective-permute-start(f32[8,2,40]{2,1,0:T(2,128)S(1)} %maximum_select_fusion.2), channel_id=1, source_target_pairs={{0,8},{8,0},{16,24},{24,16},{1,9},{9,1},{17,25},{25,17},{2,10},{10... | collective-permute-start | bytes 7688 | tf_op jit(solution)/shard_map/ppermute | solution.py:40
  167.9 3.8 %collective-permute-start.7 = (f32[16,2,40]{2,1,0:T(2,128)S(1)}, f32[16,2,40]{2,1,0:T(2,128)S(1)}, u32[]{:S(2)}, u32[]{:S(2)}) collective-permute-start(f32[16,2,40]{2,1,0:T(2,128)S(1)} %maximum_select_fusion.1), channel_id=1, source_target_pairs={{0,16},{8,24},{16,0},{24,8},{1,17},{9,25},{17,1},{25,9},{2,18},{10... | collective-permute-start | bytes 15368 | tf_op jit(solution)/shard_map/ppermute | solution.py:40
Sparse Core Ops, SparseCore 0:
  9.7 128.4 all-gather.3

commit v12 on v11

--- a/solution.py
+++ b/solution.py
@@ -108,7 +108,7 @@
     local_pre, block_query, _ = pre_query.shape
     block = kv_blocks[0].shape[1]
     n_blocks = len(kv_blocks)
-    tq = min(block_query, 512)
+    tq = min(block_query, 256)
     kernel = functools.partial(prefill_kernel, n_blocks=n_blocks, block=block, tq=tq)
     kv_spec = pl.BlockSpec((1, block, 2 * HEAD_SIZE), lambda r, h, qi, t0: (r, 0, 0))
     q_spec = pl.BlockSpec((1, tq, HEAD_SIZE), lambda r, h, qi, t0: (r, qi, h))

time: 181 us -> 189 us (1.044)
  waiting for transfers between devices: 35.4 us -> 42.8 us
  Pallas kernels: 26.8 us -> 31 us
  starting transfers between devices: 20.8 us -> 17.4 us
    all_to_all x1, waiting for transfers between devices: 8.6 us -> 13.3 us  [body(): lax.all_to_all(partial.reshape(vocab_count, head_count, D), 'vocab', 0, 0...]
    pallas_call x1, Pallas kernels: 26.8 us -> 31 us  [prefill_attention(): pl.pallas_call(kernel, out_shape=jax.ShapeDtypeStruct(pre_query.shape, jn...]
    ppermute x5, starting transfers between devices: 10.1 us -> 6.79 us  [doubling_gather(): theirs = lax.ppermute(value, axis, pairs)]
    ppermute x5, waiting for transfers between devices: 6.9 us -> 9.62 us  [doubling_gather(): theirs = lax.ppermute(value, axis, pairs)]
  transfers between devices with their start and end apart: 10 -> 10, of which waited for: 8 -> 8; matrix products, arithmetic and copies ran while one was open for 22% -> 21% of each run, Pallas kernels for 15% -> 16%
where the time goes in v12:
time: 189 us; the launch traced here: 188 us
  waiting for transfers between devices  42.8 us (23%)
  blocking collectives  40.2 us (21%)
  Pallas kernels  31 us (16%)
  matrix products  30.5 us (16%)
  starting transfers between devices  17.4 us (9%)
  between operations  15.6 us (8%)
  other arithmetic  7.78 us (4%)
  local copies, waits for them, and re-layouts  2.85 us (2%)
    pallas_call x1, Pallas kernels, prefill_attention(): pl.pallas_call(kernel, out_shape=jax.ShapeDtypeStruct(pre_query.shape, jn...  31 us
    ppermute x3, waiting for transfers between devices, from_behind(): return lax.ppermute(value, axis, pairs)  19.1 us
    dot_general x1, matrix products, body(): lax.dot_general(head_rows, embedding, (((1,), (1,)), ((), ())), preferred...  18.2 us
    all_gather x1, blocking collectives, body(): group_rows = lax.all_gather(head_mixed, 'vocab', axis=0, tiled=True)  16.7 us
    all_gather x1, blocking collectives, gather_all(): inner = lax.all_gather(value, 'vocab', axis=0, tiled=True)  14.2 us
    all_to_all x1, waiting for transfers between devices, body(): lax.all_to_all(partial.reshape(vocab_count, head_count, D), 'vocab', 0, 0...  13.3 us
    dot_general x1, matrix products, body(): jnp.dot(mixed_rows, lax.all_gather(out_weight, 'vocab', axis=0, tiled=Tru...  11 us
    ppermute x5, waiting for transfers between devices, doubling_gather(): theirs = lax.ppermute(value, axis, pairs)  9.62 us
  transfers between devices with their start and end apart: 10, of which 8 were waited for; matrix products, arithmetic and copies ran while one was open for 21% of the time, Pallas kernels for 16%

profile of v12, /device:TPU:0, one launch (start us, length us, event | category | flops | bytes accessed | tf_op | source)
XLA Modules:
  0.0 188.2 jit_solution(10371941352466901396)
XLA Ops:
  7.2 0.0 copy-start.5
  7.2 0.0 copy-start.6
  7.2 0.0 copy-start.2
  7.2 0.0 all-gather.4.cloned.1.call-start
  7.2 0.7 all-gather.4.cloned.1.call-update
  7.9 2.1 %broadcast_select_fusion = (bf16[1,512,512]{2,1,0:T(8,128)(2,1)}, bf16[1,512,512]{2,1,0:T(8,128)(2,1)S(1)}, bf16[1,512,512]{2,1,0:T(8,128)(2,1)S(1)}) fusion(bf16[1,512,512]{2,1,0:T(8,128)(2,1)} %refs_4_.1, bf16[1,512,512]{2,1,0:T(8,128)(2,1)} %refs_0_.1, pred[]{:T(512)S(6)} %le.11, pred[]{:T(512)S(6)} %le.10, pred[]{:T(512)S(6)} %le.9), kind=kLoop, calls=%fused_computation.21 | loop fusion | flops 786432 | bytes 2621443 | tf_op jit(solution)/shard_map/jit(_where)/select_n | solution.py:160
  10.0 2.9 %collective-permute-start.2 = (bf16[1,512,512]{2,1,0:T(8,128)(2,1)}, bf16[1,512,512]{2,1,0:T(8,128)(2,1)}, u32[]{:S(2)}, u32[]{:S(2)}) collective-permute-start(bf16[1,512,512]{2,1,0:T(8,128)(2,1)} %get-tuple-element.14), channel_id=1, source_target_pairs={{0,8},{8,16},{16,24},{24,0},{1,9},{9,17},{17,25},{25,1},{2,10},{10... | collective-permute-start | bytes 1572872 | tf_op jit(solution)/shard_map/ppermute | solution.py:23
  13.0 1.5 collective-permute-start.1
  14.5 1.4 collective-permute-start
  16.6 0.0 copy-done.5
  16.7 0.0 copy-done.6
  16.7 0.1 fusion.9
  16.8 0.0 copy-done.2
  16.8 0.5 select_reduce_fusion
  18.0 0.2 fusion.20
  18.2 0.3 fusion.8
  18.5 0.0 copy-start
  18.6 8.5 %collective-permute-done.2.refs_3_ = bf16[1,512,512]{2,1,0:T(8,128)(2,1)} collective-permute-done((bf16[1,512,512]{2,1,0:T(8,128)(2,1)}, bf16[1,512,512]{2,1,0:T(8,128)(2,1)}, u32[]{:S(2)}, u32[]{:S(2)}) %collective-permute-start.2) | collective-permute-done | bytes 524320 | tf_op jit(solution)/shard_map/ppermute | solution.py:23
  27.0 10.4 %collective-permute-done.1.refs_2_ = bf16[1,512,512]{2,1,0:T(8,128)(2,1)} collective-permute-done((bf16[1,512,512]{2,1,0:T(8,128)(2,1)S(1)}, bf16[1,512,512]{2,1,0:T(8,128)(2,1)}, u32[]{:S(2)}, u32[]{:S(2)}) %collective-permute-start.1) | collective-permute-done | bytes 524320 | tf_op jit(solution)/shard_map/ppermute | solution.py:23
  37.4 0.3 collective-permute-done.refs_1_
  37.7 31.0 %shard_map.156 = bf16[1,512,2560]{2,1,0:T(8,128)(2,1)} custom-call(s32[1]{0:T(128)S(6)} %sub.112.t0_ref, bf16[1,512,2560]{2,1,0:T(8,128)(2,1)} %q_ref.1, bf16[1,512,512]{2,1,0:T(8,128)(2,1)} %refs_0_.1, bf16[1,512,512]{2,1,0:T(8,128)(2,1)} %collective-permute-done.refs_1_, bf16[1,512,512]{2,1,0:T(8,128)(2,1)} %collective-permute-done.1.refs_2_, ...), custom_call_target="tpu_custom_call" | custom-call | flops 13421772800 | bytes 7864320 | tf_op jit(solution)/shard_map/pallas_call | solution.py:116
  68.7 0.0 copy-start.3
  68.7 0.0 copy-start.4
  68.7 0.8 slice_bitcast_fusion.1
  69.6 16.7 %all-gather = bf16[8,2,2560]{2,1,0:T(2,128)(2,1)S(1)} all-gather(bf16[1,2,2560]{2,1,0:T(2,128)(2,1)S(1)} %maximum_bitcast_fusion), channel_id=1, replica_groups=mesh['seq'=4,'vocab'=8] {'vocab'}, dimensions={0}, use_global_device_ids=true | all-gather | bytes 92160 | tf_op jit(solution)/shard_map/all_gather | solution.py:223
  86.3 0.0 copy-done
  86.3 0.4 fusion.29
  86.7 0.8 reshape.154
  87.4 4.7 %all-to-all-start = ((f32[8,2,2560]{2,1,0:T(2,128)}), f32[8,2,2560]{2,1,0:T(2,128)S(1)}, u32[]{:S(2)}, u32[]{:S(2)}) async-start(f32[8,2,2560]{2,1,0:T(2,128)} %reshape.154), calls=%async_computation | async-start | bytes 327680 | tf_op jit(solution)/shard_map/all_to_all | solution.py:228
  92.1 0.8 slice_bitcast_fusion.2
  92.9 13.3 %all-to-all-done = f32[8,2,2560]{2,1,0:T(2,128)S(1)} async-done(((f32[8,2,2560]{2,1,0:T(2,128)}), f32[8,2,2560]{2,1,0:T(2,128)S(1)}, u32[]{:S(2)}, u32[]{:S(2)}) %all-to-all-start) | async-done | bytes 163872 | tf_op jit(solution)/shard_map/all_to_all | solution.py:228
  106.3 0.1 reduce_sum.46
  106.3 0.0 copy-done.3
  106.3 0.2 fusion.26
  106.5 0.0 copy-done.4
  106.5 0.1 fusion.32
  106.6 14.2 %all-gather.1 = bf16[8,2,2560]{2,1,0:T(2,128)(2,1)S(1)} all-gather(bf16[1,2,2560]{2,1,0:T(2,128)(2,1)S(1)} %fusion.32), channel_id=1, replica_groups=mesh['seq'=4,'vocab'=8] {'vocab'}, dimensions={0}, use_global_device_ids=true | all-gather | bytes 92160 | tf_op jit(solution)/shard_map/all_gather | solution.py:27
  120.9 9.3 %all_gather.14 = bf16[64,2560]{1,0:T(8,128)(2,1)S(1)} all-gather(bf16[16,2560]{1,0:T(8,128)(2,1)S(1)} %reshape.164), channel_id=1, replica_groups=mesh['seq'=4,'vocab'=8] {'seq'}, dimensions={0}, use_global_device_ids=true | all-gather | bytes 409600 | tf_op jit(solution)/shard_map/all_gather | solution.py:28
  130.2 0.1 reshape.155
  130.3 0.1 slice.69
  130.5 18.2 %fusion.46 = (f32[40]{0:T(128)S(1)}, f32[40,8000]{1,0:T(8,128)S(1)}) fusion(bf16[8000,2560]{1,0:T(8,128)(2,1)} %param.25, bf16[8,2560]{1,0:T(8,128)(2,1)S(1)} %bitcast.66, bf16[32,2560]{1,0:T(8,128)(2,1)S(1)} %bitcast.65), kind=kOutput, calls=%fused_computation.83 | convolution fusion | flops 1639129600 | bytes 42444960 | tf_op jit(solution)/shard_map/dot_general | solution.py:238
  148.7 0.4 exponential_reduce_fusion
  149.1 0.1 collective-permute-start.3
  149.1 0.0 all-gather.4.cloned.1.call-done
  149.2 0.0 copy-start.1
  149.2 11.0 %fusion.2 = f32[513,2560]{1,0:T(8,128)S(1)} fusion(bf16[2560,2560]{1,0:T(8,128)(2,1)} %all-gather.4.cloned.1.call-done, bf16[1,2560]{1,0:T(2,128)(2,1)S(1)} %bitcast.71, bf16[512,2560]{1,0:T(8,128)(2,1)} %bitcast.76), kind=kOutput, calls=%fused_computation.3 | convolution fusion | flops 6729246720 | bytes 20986880 | tf_op jit(solution)/shard_map/dot_general | solution.py:206
  160.2 0.0 copy-done.1
  160.2 2.3 %fusion.1 = bf16[1,512,2560]{2,1,0:T(8,128)(2,1)} fusion(f32[513,2560]{1,0:T(8,128)S(1)} %fusion.2, bf16[1,512,2560]{2,1,0:T(8,128)(2,1)S(1)} %copy-done.1), kind=kLoop, calls=%fused_computation.2 | loop fusion | flops 3932160 | bytes 10485760 | tf_op jit(solution)/shard_map/convert_element_type | solution.py:214
  162.5 0.6 fusion.31
  163.1 0.0 collective-permute-done.3
  163.1 2.7 %collective-permute-start.4 = (f32[2,2,40]{2,1,0:T(2,128)S(1)}, f32[2,2,40]{2,1,0:T(2,128)S(1)}, u32[]{:S(2)}, u32[]{:S(2)}) collective-permute-start(f32[2,2,40]{2,1,0:T(2,128)S(1)} %maximum_select_fusion.4), channel_id=1, source_target_pairs={{0,2},{1,3},{2,0},{3,1},{4,6},{5,7},{6,4},{7,5},{8,10},{9,11},{10,... | collective-permute-start | bytes 1928 | tf_op jit(solution)/shard_map/ppermute | solution.py:40
  165.9 1.6 collective-permute-done.4
  167.4 0.9 collective-permute-start.5
  168.4 3.6 %collective-permute-done.5 = f32[4,2,40]{2,1,0:T(2,128)S(1)} collective-permute-done((f32[4,2,40]{2,1,0:T(2,128)S(1)}, f32[4,2,40]{2,1,0:T(2,128)S(1)}, u32[]{:S(2)}, u32[]{:S(2)}) %collective-permute-start.5) | collective-permute-done | bytes 1312 | tf_op jit(solution)/shard_map/ppermute | solution.py:40
  172.0 1.5 collective-permute-start.6
  173.5 2.2 %collective-permute-done.6 = f32[8,2,40]{2,1,0:T(2,128)S(1)} collective-permute-done((f32[8,2,40]{2,1,0:T(2,128)S(1)}, f32[8,2,40]{2,1,0:T(2,128)S(1)}, u32[]{:S(2)}, u32[]{:S(2)}) %collective-permute-start.6) | collective-permute-done | bytes 2592 | tf_op jit(solution)/shard_map/ppermute | solution.py:40
  175.7 1.5 collective-permute-start.7
  177.2 2.3 %collective-permute-done.7 = f32[16,2,40]{2,1,0:T(2,128)S(1)} collective-permute-done((f32[16,2,40]{2,1,0:T(2,128)S(1)}, f32[16,2,40]{2,1,0:T(2,128)S(1)}, u32[]{:S(2)}, u32[]{:S(2)}) %collective-permute-start.7) | collective-permute-done | bytes 5152 | tf_op jit(solution)/shard_map/ppermute | solution.py:40
  179.6 0.1 slice.66
  179.7 0.7 fusion.15
  180.4 0.9 fusion.14
  (24 shorter events, 0.4 us)
Async XLA Ops:
  7.2 9.4 %copy-start.5 = (bf16[1,2560]{1,0:T(2,128)(2,1)S(1)}, bf16[1,2560]{1,0:T(2,128)(2,1)}, u32[]{:S(2)}) copy-start(bf16[1,2560]{1,0:T(2,128)(2,1)} %param.18) | copy-start | bytes 15364
  7.2 9.5 %copy-start.6 = (bf16[1,512]{1,0:T(2,128)(2,1)S(1)}, bf16[1,512]{1,0:T(2,128)(2,1)}, u32[]{:S(2)}) copy-start(bf16[1,512]{1,0:T(2,128)(2,1)} %param.19) | copy-start | bytes 3076
  7.2 9.6 %copy-start.2 = (bf16[1,2048,512]{2,1,0:T(8,128)(2,1)S(1)}, bf16[1,2048,512]{2,1,0:T(8,128)(2,1)}, u32[]{:S(2)}) copy-start(bf16[1,2048,512]{2,1,0:T(8,128)(2,1)} %param.20) | copy-start | bytes 6291460
  7.2 142.0 %all-gather.4.cloned.1.call-start = ((), (), s32[]{:S(2)}) async-start(), calls=%async_computation.1 | async-start | bytes 14745600 | tf_op jit(solution)/shard_map/all_gather | solution.py:208
  10.0 17.0 %collective-permute-start.2 = (bf16[1,512,512]{2,1,0:T(8,128)(2,1)}, bf16[1,512,512]{2,1,0:T(8,128)(2,1)}, u32[]{:S(2)}, u32[]{:S(2)}) collective-permute-start(bf16[1,512,512]{2,1,0:T(8,128)(2,1)} %get-tuple-element.14), channel_id=1, source_target_pairs={{0,8},{8,16},{16,24},{24,0},{1,9},{9,17},{17,25},{25,1},{2,10},{10... | collective-permute-start | bytes 1572872 | tf_op jit(solution)/shard_map/ppermute | solution.py:23
  13.0 24.4 %collective-permute-start.1 = (bf16[1,512,512]{2,1,0:T(8,128)(2,1)S(1)}, bf16[1,512,512]{2,1,0:T(8,128)(2,1)}, u32[]{:S(2)}, u32[]{:S(2)}) collective-permute-start(bf16[1,512,512]{2,1,0:T(8,128)(2,1)S(1)} %get-tuple-element.15), channel_id=1, source_target_pairs={{0,16},{8,24},{16,0},{24,8},{1,17},{9,25},{17,1},{25,9},{2,18},{10... | collective-permute-start | bytes 1572872 | tf_op jit(solution)/shard_map/ppermute | solution.py:23
  14.5 23.2 %collective-permute-start = (bf16[1,512,512]{2,1,0:T(8,128)(2,1)S(1)}, bf16[1,512,512]{2,1,0:T(8,128)(2,1)}, u32[]{:S(2)}, u32[]{:S(2)}) collective-permute-start(bf16[1,512,512]{2,1,0:T(8,128)(2,1)S(1)} %get-tuple-element.16), channel_id=1, source_target_pairs={{0,24},{8,0},{16,8},{24,16},{1,25},{9,1},{17,9},{25,17},{2,26},{10... | collective-permute-start | bytes 1572872 | tf_op jit(solution)/shard_map/ppermute | solution.py:23
  18.5 67.7 %copy-start = (bf16[320,2560]{1,0:T(8,128)(2,1)S(1)}, bf16[320,2560]{1,0:T(8,128)(2,1)}, u32[]{:S(2)}) copy-start(bf16[320,2560]{1,0:T(8,128)(2,1)} %param.23) | copy-start | bytes 4915204
  68.7 37.6 %copy-start.3 = (bf16[1,2560]{1,0:T(2,128)(2,1)S(1)}, bf16[1,2560]{1,0:T(2,128)(2,1)}, u32[]{:S(2)}) copy-start(bf16[1,2560]{1,0:T(2,128)(2,1)} %param.22) | copy-start | bytes 15364
  68.7 37.8 %copy-start.4 = (f32[2560]{0:T(1024)S(1)}, f32[2560]{0:T(1024)}, u32[]{:S(2)}) copy-start(f32[2560]{0:T(1024)} %param.24) | copy-start | bytes 30724
  87.4 18.8 %all-to-all-start = ((f32[8,2,2560]{2,1,0:T(2,128)}), f32[8,2,2560]{2,1,0:T(2,128)S(1)}, u32[]{:S(2)}, u32[]{:S(2)}) async-start(f32[8,2,2560]{2,1,0:T(2,128)} %reshape.154), calls=%async_computation | async-start | bytes 327680 | tf_op jit(solution)/shard_map/all_to_all | solution.py:228
  149.1 14.1 %collective-permute-start.3 = (f32[1,2,40]{2,1,0:T(2,128)S(1)}, f32[1,2,40]{2,1,0:T(2,128)S(1)}, u32[]{:S(2)}, u32[]{:S(2)}) collective-permute-start(f32[1,2,40]{2,1,0:T(2,128)S(1)} %maximum_bitcast_fusion.1), channel_id=1, source_target_pairs={{0,1},{1,0},{2,3},{3,2},{4,5},{5,4},{6,7},{7,6},{8,9},{9,8},{10,11... | collective-permute-start | bytes 968 | tf_op jit(solution)/shard_map/ppermute | solution.py:40
  149.2 11.0 %copy-start.1 = (bf16[1,512,2560]{2,1,0:T(8,128)(2,1)S(1)}, bf16[1,512,2560]{2,1,0:T(8,128)(2,1)}, u32[]{:S(2)}) copy-start(bf16[1,512,2560]{2,1,0:T(8,128)(2,1)} %param.17) | copy-start | bytes 7864324
  163.1 4.3 %collective-permute-start.4 = (f32[2,2,40]{2,1,0:T(2,128)S(1)}, f32[2,2,40]{2,1,0:T(2,128)S(1)}, u32[]{:S(2)}, u32[]{:S(2)}) collective-permute-start(f32[2,2,40]{2,1,0:T(2,128)S(1)} %maximum_select_fusion.4), channel_id=1, source_target_pairs={{0,2},{1,3},{2,0},{3,1},{4,6},{5,7},{6,4},{7,5},{8,10},{9,11},{10,... | collective-permute-start | bytes 1928 | tf_op jit(solution)/shard_map/ppermute | solution.py:40
  167.4 4.5 %collective-permute-start.5 = (f32[4,2,40]{2,1,0:T(2,128)S(1)}, f32[4,2,40]{2,1,0:T(2,128)S(1)}, u32[]{:S(2)}, u32[]{:S(2)}) collective-permute-start(f32[4,2,40]{2,1,0:T(2,128)S(1)} %maximum_select_fusion.3), channel_id=1, source_target_pairs={{0,4},{1,5},{2,6},{3,7},{4,0},{5,1},{6,2},{7,3},{8,12},{9,13},{10,... | collective-permute-start | bytes 3848 | tf_op jit(solution)/shard_map/ppermute | solution.py:40
  172.0 3.7 %collective-permute-start.6 = (f32[8,2,40]{2,1,0:T(2,128)S(1)}, f32[8,2,40]{2,1,0:T(2,128)S(1)}, u32[]{:S(2)}, u32[]{:S(2)}) collective-permute-start(f32[8,2,40]{2,1,0:T(2,128)S(1)} %maximum_select_fusion.2), channel_id=1, source_target_pairs={{0,8},{8,0},{16,24},{24,16},{1,9},{9,1},{17,25},{25,17},{2,10},{10... | collective-permute-start | bytes 7688 | tf_op jit(solution)/shard_map/ppermute | solution.py:40
  175.7 3.8 %collective-permute-start.7 = (f32[16,2,40]{2,1,0:T(2,128)S(1)}, f32[16,2,40]{2,1,0:T(2,128)S(1)}, u32[]{:S(2)}, u32[]{:S(2)}) collective-permute-start(f32[16,2,40]{2,1,0:T(2,128)S(1)} %maximum_select_fusion.1), channel_id=1, source_target_pairs={{0,16},{8,24},{16,0},{24,8},{1,17},{9,25},{17,1},{25,9},{2,18},{10... | collective-permute-start | bytes 15368 | tf_op jit(solution)/shard_map/ppermute | solution.py:40
Sparse Core Ops, SparseCore 0:
  9.7 128.3 all-gather.3

commit v13 on v8

--- a/solution.py
+++ b/solution.py
@@ -220,9 +220,9 @@
     head_count = local_dec + local_pre
     head_mixed = jnp.concatenate([dec_mixed, pre_mixed_3d[:, block_query - 1, :]], axis=0)
     head_resid = jnp.concatenate([dec_resid, pre_resid[:, block_query - 1, :]], axis=0)
-    group_rows = lax.all_gather(head_mixed, "vocab", axis=0, tiled=True)
-    own_columns = lax.dynamic_slice_in_dim(
-        group_rows, vocab_index * weight_rows, weight_rows, axis=1
+    column_blocks = head_mixed.reshape(head_count, vocab_count, weight_rows).transpose(1, 0, 2)
+    own_columns = lax.all_to_all(column_blocks, "vocab", 0, 0, tiled=True).reshape(
+        vocab_count * head_count, weight_rows
     )
     partial = jnp.dot(own_columns, out_weight, preferred_element_type=jnp.float32)
     pieces = lax.all_to_all(

time: 181 us -> 179 us (0.989)
  waiting for transfers between devices: 35.4 us -> 45 us
  starting transfers between devices: 20.8 us -> 14.6 us
  blocking collectives: 40.4 us -> 35 us
    all_gather x1 -> x0, blocking collectives: 16.7 us -> none  [body(): group_rows = lax.all_gather(head_mixed, 'vocab', axis=0, tiled=True)]
    all_to_all x0 -> x1, blocking collectives: none -> 10.4 us  [body(): lax.all_to_all(column_blocks, 'vocab', 0, 0, tiled=True)]
    ppermute x5, starting transfers between devices: 10.1 us -> 3.91 us  [doubling_gather(): theirs = lax.ppermute(value, axis, pairs)]
    ppermute x5, waiting for transfers between devices: 6.9 us -> 11.8 us  [doubling_gather(): theirs = lax.ppermute(value, axis, pairs)]
    all_to_all x1, waiting for transfers between devices: 8.6 us -> 13.4 us  [body(): lax.all_to_all(partial.reshape(vocab_count, head_count, D), 'vocab', 0, 0...]
where the time goes in v13:
time: 179 us; the launch traced here: 178 us
  waiting for transfers between devices  45 us (25%)
  blocking collectives  35 us (20%)
  matrix products  30.6 us (17%)
  Pallas kernels  26.8 us (15%)
  between operations  15.6 us (9%)
  starting transfers between devices  14.6 us (8%)
  other arithmetic  6.29 us (4%)
  local copies, waits for them, and re-layouts  4.46 us (2%)
    pallas_call x1, Pallas kernels, prefill_attention(): pl.pallas_call(kernel, out_shape=jax.ShapeDtypeStruct(pre_query.shape, jn...  26.8 us
    ppermute x3, waiting for transfers between devices, from_behind(): return lax.ppermute(value, axis, pairs)  19.1 us
    dot_general x1, matrix products, body(): lax.dot_general(head_rows, embedding, (((1,), (1,)), ((), ())), preferred...  18.3 us
    all_gather x1, blocking collectives, gather_all(): inner = lax.all_gather(value, 'vocab', axis=0, tiled=True)  15.2 us
    all_to_all x1, waiting for transfers between devices, body(): lax.all_to_all(partial.reshape(vocab_count, head_count, D), 'vocab', 0, 0...  13.4 us
    ppermute x5, waiting for transfers between devices, doubling_gather(): theirs = lax.ppermute(value, axis, pairs)  11.8 us
    dot_general x1, matrix products, body(): jnp.dot(mixed_rows, lax.all_gather(out_weight, 'vocab', axis=0, tiled=Tru...  11 us
    all_to_all x1, blocking collectives, body(): lax.all_to_all(column_blocks, 'vocab', 0, 0, tiled=True)  10.4 us
  transfers between devices with their start and end apart: 10, of which 8 were waited for; matrix products, arithmetic and copies ran while one was open for 22% of the time, Pallas kernels for 15%

profile of v13, /device:TPU:0, one launch (start us, length us, event | category | flops | bytes accessed | tf_op | source)
XLA Modules:
  0.0 178.4 jit_solution(4215128172284716663)
XLA Ops:
  7.2 0.0 copy-start.5
  7.2 0.0 copy-start.6
  7.2 0.0 copy-start.2
  7.2 0.0 all-gather.3.cloned.1.call-start
  7.2 0.7 all-gather.3.cloned.1.call-update
  7.9 2.1 %broadcast_select_fusion = (bf16[1,512,512]{2,1,0:T(8,128)(2,1)}, bf16[1,512,512]{2,1,0:T(8,128)(2,1)S(1)}, bf16[1,512,512]{2,1,0:T(8,128)(2,1)S(1)}) fusion(bf16[1,512,512]{2,1,0:T(8,128)(2,1)} %refs_4_.1, bf16[1,512,512]{2,1,0:T(8,128)(2,1)} %refs_0_.1, pred[]{:T(512)S(6)} %le.11, pred[]{:T(512)S(6)} %le.10, pred[]{:T(512)S(6)} %le.9), kind=kLoop, calls=%fused_computation.21 | loop fusion | flops 786432 | bytes 2621443 | tf_op jit(solution)/shard_map/jit(_where)/select_n | solution.py:160
  10.0 2.9 %collective-permute-start.2 = (bf16[1,512,512]{2,1,0:T(8,128)(2,1)}, bf16[1,512,512]{2,1,0:T(8,128)(2,1)}, u32[]{:S(2)}, u32[]{:S(2)}) collective-permute-start(bf16[1,512,512]{2,1,0:T(8,128)(2,1)} %get-tuple-element.14), channel_id=1, source_target_pairs={{0,8},{8,16},{16,24},{24,0},{1,9},{9,17},{17,25},{25,1},{2,10},{10... | collective-permute-start | bytes 1572872 | tf_op jit(solution)/shard_map/ppermute | solution.py:23
  13.0 1.5 collective-permute-start.1
  14.5 1.4 collective-permute-start
  16.6 0.0 copy-done.5
  16.7 0.0 copy-done.6
  16.7 0.1 fusion.10
  16.8 0.0 copy-done.2
  16.8 0.5 select_reduce_fusion
  17.3 0.2 fusion.19
  18.2 0.3 fusion.9
  18.5 0.1 concatenate.63
  18.6 0.0 copy-start
  18.6 8.4 %collective-permute-done.2.refs_3_ = bf16[1,512,512]{2,1,0:T(8,128)(2,1)} collective-permute-done((bf16[1,512,512]{2,1,0:T(8,128)(2,1)}, bf16[1,512,512]{2,1,0:T(8,128)(2,1)}, u32[]{:S(2)}, u32[]{:S(2)}) %collective-permute-start.2) | collective-permute-done | bytes 524320 | tf_op jit(solution)/shard_map/ppermute | solution.py:23
  27.0 10.4 %collective-permute-done.1.refs_2_ = bf16[1,512,512]{2,1,0:T(8,128)(2,1)} collective-permute-done((bf16[1,512,512]{2,1,0:T(8,128)(2,1)S(1)}, bf16[1,512,512]{2,1,0:T(8,128)(2,1)}, u32[]{:S(2)}, u32[]{:S(2)}) %collective-permute-start.1) | collective-permute-done | bytes 524320 | tf_op jit(solution)/shard_map/ppermute | solution.py:23
  37.4 0.3 collective-permute-done.refs_1_
  37.7 26.8 %shard_map.156 = bf16[1,512,2560]{2,1,0:T(8,128)(2,1)} custom-call(s32[1]{0:T(128)S(6)} %sub.104.t0_ref, bf16[1,512,2560]{2,1,0:T(8,128)(2,1)} %q_ref.1, bf16[1,512,512]{2,1,0:T(8,128)(2,1)} %refs_0_.1, bf16[1,512,512]{2,1,0:T(8,128)(2,1)} %collective-permute-done.refs_1_, bf16[1,512,512]{2,1,0:T(8,128)(2,1)} %collective-permute-done.1.refs_2_, ...), custom_call_target="tpu_custom_call" | custom-call | flops 13421772800 | bytes 7864320 | tf_op jit(solution)/shard_map/pallas_call | solution.py:116
  64.5 0.0 copy-start.3
  64.6 0.0 copy-start.4
  64.6 0.8 slice_reduce_fusion
  65.4 0.1 concatenate.64
  65.5 10.4 %all_to_all.10 = bf16[8,2,320]{2,1,0:T(2,128)(2,1)S(1)} all-to-all(bf16[8,2,320]{2,1,0:T(2,128)(2,1)S(1)} %maximum_bitcast_fusion), channel_id=1, replica_groups=mesh['seq'=4,'vocab'=8] {'vocab'}, dimensions={0} | all-to-all | bytes 20480 | tf_op jit(solution)/shard_map/all_to_all | solution.py:224
  75.9 0.0 copy-done
  75.9 0.3 fusion.6
  76.2 0.8 copy.23
  77.0 4.7 %all-to-all-start.1 = ((f32[8,2,2560]{2,1,0:T(2,128)}), f32[8,2,2560]{2,1,0:T(2,128)S(1)}, u32[]{:S(2)}, u32[]{:S(2)}) async-start(f32[8,2,2560]{2,1,0:T(2,128)} %copy.23), calls=%async_computation.1 | async-start | bytes 327680 | tf_op jit(solution)/shard_map/all_to_all | solution.py:228
  81.8 0.8 slice_bitcast_fusion.1
  82.6 13.4 %all-to-all-done.1 = f32[8,2,2560]{2,1,0:T(2,128)S(1)} async-done(((f32[8,2,2560]{2,1,0:T(2,128)}), f32[8,2,2560]{2,1,0:T(2,128)S(1)}, u32[]{:S(2)}, u32[]{:S(2)}) %all-to-all-start.1) | async-done | bytes 163872 | tf_op jit(solution)/shard_map/all_to_all | solution.py:228
  96.0 0.1 reduce_sum.46
  96.0 0.0 copy-done.3
  96.0 0.2 fusion.25
  96.2 0.0 copy-done.4
  96.2 0.1 fusion.30
  96.3 15.2 %all-gather = bf16[8,2,2560]{2,1,0:T(2,128)(2,1)S(1)} all-gather(bf16[1,2,2560]{2,1,0:T(2,128)(2,1)S(1)} %fusion.30), channel_id=1, replica_groups=mesh['seq'=4,'vocab'=8] {'vocab'}, dimensions={0}, use_global_device_ids=true | all-gather | bytes 92160 | tf_op jit(solution)/shard_map/all_gather | solution.py:27
  111.6 9.5 %all_gather.10 = bf16[64,2560]{1,0:T(8,128)(2,1)S(1)} all-gather(bf16[16,2560]{1,0:T(8,128)(2,1)S(1)} %reshape.169), channel_id=1, replica_groups=mesh['seq'=4,'vocab'=8] {'seq'}, dimensions={0}, use_global_device_ids=true | all-gather | bytes 409600 | tf_op jit(solution)/shard_map/all_gather | solution.py:28
  121.0 0.1 reshape.161
  121.2 0.1 slice.59
  121.3 18.3 %fusion.43 = (f32[40]{0:T(128)S(1)}, f32[40,8000]{1,0:T(8,128)S(1)}) fusion(bf16[8000,2560]{1,0:T(8,128)(2,1)} %param.25, bf16[8,2560]{1,0:T(8,128)(2,1)S(1)} %bitcast.64, bf16[32,2560]{1,0:T(8,128)(2,1)S(1)} %bitcast.63), kind=kOutput, calls=%fused_computation.79 | convolution fusion | flops 1639129600 | bytes 42444960 | tf_op jit(solution)/shard_map/dot_general | solution.py:238
  139.6 0.4 exponential_reduce_fusion
  140.0 0.1 collective-permute-start.3
  140.1 0.0 all-gather.3.cloned.1.call-done
  140.1 0.0 copy-start.1
  140.1 11.0 %fusion.2 = f32[513,2560]{1,0:T(8,128)S(1)} fusion(bf16[2560,2560]{1,0:T(8,128)(2,1)} %all-gather.3.cloned.1.call-done, bf16[1,2560]{1,0:T(2,128)(2,1)S(1)} %bitcast.69, bf16[512,2560]{1,0:T(8,128)(2,1)} %bitcast.73), kind=kOutput, calls=%fused_computation.3 | convolution fusion | flops 6729246720 | bytes 20986880 | tf_op jit(solution)/shard_map/dot_general | solution.py:206
  151.2 0.0 copy-done.1
  151.2 2.3 %fusion.1 = bf16[1,512,2560]{2,1,0:T(8,128)(2,1)} fusion(f32[513,2560]{1,0:T(8,128)S(1)} %fusion.2, bf16[1,512,2560]{2,1,0:T(8,128)(2,1)S(1)} %copy-done.1), kind=kLoop, calls=%fused_computation.2 | loop fusion | flops 3932160 | bytes 10485760 | tf_op jit(solution)/shard_map/convert_element_type | solution.py:214
  153.5 0.6 fusion.29
  154.1 0.0 collective-permute-done.3
  154.1 0.9 collective-permute-start.4
  154.9 2.8 %collective-permute-done.4 = f32[2,2,40]{2,1,0:T(2,128)S(1)} collective-permute-done((f32[2,2,40]{2,1,0:T(2,128)S(1)}, f32[2,2,40]{2,1,0:T(2,128)S(1)}, u32[]{:S(2)}, u32[]{:S(2)}) %collective-permute-start.4) | collective-permute-done | bytes 672 | tf_op jit(solution)/shard_map/ppermute | solution.py:40
  157.7 1.9 %collective-permute-start.5 = (f32[4,2,40]{2,1,0:T(2,128)S(1)}, f32[4,2,40]{2,1,0:T(2,128)S(1)}, u32[]{:S(2)}, u32[]{:S(2)}) collective-permute-start(f32[4,2,40]{2,1,0:T(2,128)S(1)} %maximum_select_fusion.3), channel_id=1, source_target_pairs={{0,4},{1,5},{2,6},{3,7},{4,0},{5,1},{6,2},{7,3},{8,12},{9,13},{10,... | collective-permute-start | bytes 3848 | tf_op jit(solution)/shard_map/ppermute | solution.py:40
  159.6 2.6 %collective-permute-done.5 = f32[4,2,40]{2,1,0:T(2,128)S(1)} collective-permute-done((f32[4,2,40]{2,1,0:T(2,128)S(1)}, f32[4,2,40]{2,1,0:T(2,128)S(1)}, u32[]{:S(2)}, u32[]{:S(2)}) %collective-permute-start.5) | collective-permute-done | bytes 1312 | tf_op jit(solution)/shard_map/ppermute | solution.py:40
  162.3 0.6 collective-permute-start.6
  162.8 3.2 %collective-permute-done.6 = f32[8,2,40]{2,1,0:T(2,128)S(1)} collective-permute-done((f32[8,2,40]{2,1,0:T(2,128)S(1)}, f32[8,2,40]{2,1,0:T(2,128)S(1)}, u32[]{:S(2)}, u32[]{:S(2)}) %collective-permute-start.6) | collective-permute-done | bytes 2592 | tf_op jit(solution)/shard_map/ppermute | solution.py:40
  166.0 0.6 collective-permute-start.7
  166.6 3.2 %collective-permute-done.7 = f32[16,2,40]{2,1,0:T(2,128)S(1)} collective-permute-done((f32[16,2,40]{2,1,0:T(2,128)S(1)}, f32[16,2,40]{2,1,0:T(2,128)S(1)}, u32[]{:S(2)}, u32[]{:S(2)}) %collective-permute-start.7) | collective-permute-done | bytes 5152 | tf_op jit(solution)/shard_map/ppermute | solution.py:40
  169.9 0.1 subtract_convert_fusion
  170.1 0.7 slice.65
  170.7 0.8 slice.64
  (23 shorter events, 0.4 us)
Async XLA Ops:
  7.2 9.4 %copy-start.5 = (bf16[1,2560]{1,0:T(2,128)(2,1)S(1)}, bf16[1,2560]{1,0:T(2,128)(2,1)}, u32[]{:S(2)}) copy-start(bf16[1,2560]{1,0:T(2,128)(2,1)} %param.18) | copy-start | bytes 15364
  7.2 9.5 %copy-start.6 = (bf16[1,512]{1,0:T(2,128)(2,1)S(1)}, bf16[1,512]{1,0:T(2,128)(2,1)}, u32[]{:S(2)}) copy-start(bf16[1,512]{1,0:T(2,128)(2,1)} %param.19) | copy-start | bytes 3076
  7.2 9.6 %copy-start.2 = (bf16[1,2048,512]{2,1,0:T(8,128)(2,1)S(1)}, bf16[1,2048,512]{2,1,0:T(8,128)(2,1)}, u32[]{:S(2)}) copy-start(bf16[1,2048,512]{2,1,0:T(8,128)(2,1)} %param.20) | copy-start | bytes 6291460
  7.2 132.9 %all-gather.3.cloned.1.call-start = ((), (), s32[]{:S(2)}) async-start(), calls=%async_computation.2 | async-start | bytes 14745600 | tf_op jit(solution)/shard_map/all_gather | solution.py:208
  10.0 17.0 %collective-permute-start.2 = (bf16[1,512,512]{2,1,0:T(8,128)(2,1)}, bf16[1,512,512]{2,1,0:T(8,128)(2,1)}, u32[]{:S(2)}, u32[]{:S(2)}) collective-permute-start(bf16[1,512,512]{2,1,0:T(8,128)(2,1)} %get-tuple-element.14), channel_id=1, source_target_pairs={{0,8},{8,16},{16,24},{24,0},{1,9},{9,17},{17,25},{25,1},{2,10},{10... | collective-permute-start | bytes 1572872 | tf_op jit(solution)/shard_map/ppermute | solution.py:23
  13.0 24.4 %collective-permute-start.1 = (bf16[1,512,512]{2,1,0:T(8,128)(2,1)S(1)}, bf16[1,512,512]{2,1,0:T(8,128)(2,1)}, u32[]{:S(2)}, u32[]{:S(2)}) collective-permute-start(bf16[1,512,512]{2,1,0:T(8,128)(2,1)S(1)} %get-tuple-element.15), channel_id=1, source_target_pairs={{0,16},{8,24},{16,0},{24,8},{1,17},{9,25},{17,1},{25,9},{2,18},{10... | collective-permute-start | bytes 1572872 | tf_op jit(solution)/shard_map/ppermute | solution.py:23
  14.5 23.2 %collective-permute-start = (bf16[1,512,512]{2,1,0:T(8,128)(2,1)S(1)}, bf16[1,512,512]{2,1,0:T(8,128)(2,1)}, u32[]{:S(2)}, u32[]{:S(2)}) collective-permute-start(bf16[1,512,512]{2,1,0:T(8,128)(2,1)S(1)} %get-tuple-element.16), channel_id=1, source_target_pairs={{0,24},{8,0},{16,8},{24,16},{1,25},{9,1},{17,9},{25,17},{2,26},{10... | collective-permute-start | bytes 1572872 | tf_op jit(solution)/shard_map/ppermute | solution.py:23
  18.6 57.3 %copy-start = (bf16[320,2560]{1,0:T(8,128)(2,1)S(1)}, bf16[320,2560]{1,0:T(8,128)(2,1)}, u32[]{:S(2)}) copy-start(bf16[320,2560]{1,0:T(8,128)(2,1)} %param.23) | copy-start | bytes 4915204
  64.5 31.5 %copy-start.3 = (bf16[1,2560]{1,0:T(2,128)(2,1)S(1)}, bf16[1,2560]{1,0:T(2,128)(2,1)}, u32[]{:S(2)}) copy-start(bf16[1,2560]{1,0:T(2,128)(2,1)} %param.22) | copy-start | bytes 15364
  64.6 31.7 %copy-start.4 = (f32[2560]{0:T(1024)S(1)}, f32[2560]{0:T(1024)}, u32[]{:S(2)}) copy-start(f32[2560]{0:T(1024)} %param.24) | copy-start | bytes 30724
  77.0 18.9 %all-to-all-start.1 = ((f32[8,2,2560]{2,1,0:T(2,128)}), f32[8,2,2560]{2,1,0:T(2,128)S(1)}, u32[]{:S(2)}, u32[]{:S(2)}) async-start(f32[8,2,2560]{2,1,0:T(2,128)} %copy.23), calls=%async_computation.1 | async-start | bytes 327680 | tf_op jit(solution)/shard_map/all_to_all | solution.py:228
  140.0 14.1 %collective-permute-start.3 = (f32[1,2,40]{2,1,0:T(2,128)S(1)}, f32[1,2,40]{2,1,0:T(2,128)S(1)}, u32[]{:S(2)}, u32[]{:S(2)}) collective-permute-start(f32[1,2,40]{2,1,0:T(2,128)S(1)} %maximum_bitcast_fusion.1), channel_id=1, source_target_pairs={{0,1},{1,0},{2,3},{3,2},{4,5},{5,4},{6,7},{7,6},{8,9},{9,8},{10,11... | collective-permute-start | bytes 968 | tf_op jit(solution)/shard_map/ppermute | solution.py:40
  140.1 11.0 %copy-start.1 = (bf16[1,512,2560]{2,1,0:T(8,128)(2,1)S(1)}, bf16[1,512,2560]{2,1,0:T(8,128)(2,1)}, u32[]{:S(2)}) copy-start(bf16[1,512,2560]{2,1,0:T(8,128)(2,1)} %param.17) | copy-start | bytes 7864324
  154.1 3.7 %collective-permute-start.4 = (f32[2,2,40]{2,1,0:T(2,128)S(1)}, f32[2,2,40]{2,1,0:T(2,128)S(1)}, u32[]{:S(2)}, u32[]{:S(2)}) collective-permute-start(f32[2,2,40]{2,1,0:T(2,128)S(1)} %maximum_select_fusion.4), channel_id=1, source_target_pairs={{0,2},{1,3},{2,0},{3,1},{4,6},{5,7},{6,4},{7,5},{8,10},{9,11},{10,... | collective-permute-start | bytes 1928 | tf_op jit(solution)/shard_map/ppermute | solution.py:40
  157.7 4.5 %collective-permute-start.5 = (f32[4,2,40]{2,1,0:T(2,128)S(1)}, f32[4,2,40]{2,1,0:T(2,128)S(1)}, u32[]{:S(2)}, u32[]{:S(2)}) collective-permute-start(f32[4,2,40]{2,1,0:T(2,128)S(1)} %maximum_select_fusion.3), channel_id=1, source_target_pairs={{0,4},{1,5},{2,6},{3,7},{4,0},{5,1},{6,2},{7,3},{8,12},{9,13},{10,... | collective-permute-start | bytes 3848 | tf_op jit(solution)/shard_map/ppermute | solution.py:40
  162.3 3.7 %collective-permute-start.6 = (f32[8,2,40]{2,1,0:T(2,128)S(1)}, f32[8,2,40]{2,1,0:T(2,128)S(1)}, u32[]{:S(2)}, u32[]{:S(2)}) collective-permute-start(f32[8,2,40]{2,1,0:T(2,128)S(1)} %maximum_select_fusion.2), channel_id=1, source_target_pairs={{0,8},{8,0},{16,24},{24,16},{1,9},{9,1},{17,25},{25,17},{2,10},{10... | collective-permute-start | bytes 7688 | tf_op jit(solution)/shard_map/ppermute | solution.py:40
  166.0 3.8 %collective-permute-start.7 = (f32[16,2,40]{2,1,0:T(2,128)S(1)}, f32[16,2,40]{2,1,0:T(2,128)S(1)}, u32[]{:S(2)}, u32[]{:S(2)}) collective-permute-start(f32[16,2,40]{2,1,0:T(2,128)S(1)} %maximum_select_fusion.1), channel_id=1, source_target_pairs={{0,16},{8,24},{16,0},{24,8},{1,17},{9,25},{17,1},{25,9},{2,18},{10... | collective-permute-start | bytes 15368 | tf_op jit(solution)/shard_map/ppermute | solution.py:40
Sparse Core Ops, SparseCore 0:
  9.7 128.0 all-gather.2

commit v14 on v13

--- a/solution.py
+++ b/solution.py
@@ -230,8 +230,9 @@
     )
     head_proj = jnp.sum(pieces, axis=0)
     head_in = (head_resid.astype(jnp.float32) + head_proj).astype(jnp.bfloat16)
-    everyone = gather_all(normalize(head_in, norm_gain))
-    layout = everyone.reshape(seq_count, vocab_count, head_count, D)
+    by_seq = lax.all_gather(normalize(head_in, norm_gain), "seq", axis=0, tiled=True)
+    everyone = lax.all_gather(by_seq, "vocab", axis=0, tiled=True)
+    layout = everyone.reshape(vocab_count, seq_count, head_count, D).transpose(1, 0, 2, 3)
     decode_all = layout[:, :, :local_dec].reshape(-1, D)
     prefill_every_request = layout[seq_count - 1, :, local_dec:].reshape(-1, D)
     head_rows = jnp.concatenate([decode_all, prefill_every_request], axis=0)

time: 179 us -> 180 us (level)
  starting transfers between devices: 14.6 us -> 17.8 us
  waiting for transfers between devices: 45 us -> 42 us
    ppermute x5, starting transfers between devices: 3.91 us -> 7.19 us  [doubling_gather(): theirs = lax.ppermute(value, axis, pairs)]
    ppermute x5, waiting for transfers between devices: 11.8 us -> 8.9 us  [doubling_gather(): theirs = lax.ppermute(value, axis, pairs)]
where the time goes in v14:
time: 180 us
  waiting for transfers between devices  42 us (23%)
  blocking collectives  36.2 us (20%)
  matrix products  30.6 us (17%)
  Pallas kernels  26.8 us (15%)
  starting transfers between devices  17.8 us (10%)
  between operations  15.6 us (9%)
  other arithmetic  6.29 us (3%)
  local copies, waits for them, and re-layouts  4.53 us (3%)
    pallas_call x1, Pallas kernels, prefill_attention(): pl.pallas_call(kernel, out_shape=jax.ShapeDtypeStruct(pre_query.shape, jn...  26.8 us
    ppermute x3, waiting for transfers between devices, from_behind(): return lax.ppermute(value, axis, pairs)  19.1 us
    dot_general x1, matrix products, body(): lax.dot_general(head_rows, embedding, (((1,), (1,)), ((), ())), preferred...  18.3 us
    all_gather x1, blocking collectives, body(): everyone = lax.all_gather(by_seq, 'vocab', axis=0, tiled=True)  17.5 us
    all_to_all x1, waiting for transfers between devices, body(): lax.all_to_all(partial.reshape(vocab_count, head_count, D), 'vocab', 0, 0...  13.4 us
    dot_general x1, matrix products, body(): jnp.dot(mixed_rows, lax.all_gather(out_weight, 'vocab', axis=0, tiled=Tru...  11 us
    all_to_all x1, blocking collectives, body(): lax.all_to_all(column_blocks, 'vocab', 0, 0, tiled=True)  10.4 us
    ppermute x5, waiting for transfers between devices, doubling_gather(): theirs = lax.ppermute(value, axis, pairs)  8.9 us
  transfers between devices with their start and end apart: 10, of which 8 were waited for; matrix products, arithmetic and copies ran while one was open for 22% of the time, Pallas kernels for 15%

profile of v14, /device:TPU:0, one launch (start us, length us, event | category | flops | bytes accessed | tf_op | source)
XLA Modules:
  0.0 179.9 jit_solution(12400312416642934763)
XLA Ops:
  7.2 0.0 copy-start.5
  7.2 0.0 copy-start.6
  7.2 0.0 copy-start.2
  7.2 0.0 all-gather.3.cloned.1.call-start
  7.2 0.7 all-gather.3.cloned.1.call-update
  7.9 2.1 %broadcast_select_fusion = (bf16[1,512,512]{2,1,0:T(8,128)(2,1)}, bf16[1,512,512]{2,1,0:T(8,128)(2,1)S(1)}, bf16[1,512,512]{2,1,0:T(8,128)(2,1)S(1)}) fusion(bf16[1,512,512]{2,1,0:T(8,128)(2,1)} %refs_4_.1, bf16[1,512,512]{2,1,0:T(8,128)(2,1)} %refs_0_.1, pred[]{:T(512)S(6)} %le.11, pred[]{:T(512)S(6)} %le.10, pred[]{:T(512)S(6)} %le.9), kind=kLoop, calls=%fused_computation.21 | loop fusion | flops 786432 | bytes 2621443 | tf_op jit(solution)/shard_map/jit(_where)/select_n | solution.py:160
  10.0 2.9 %collective-permute-start.2 = (bf16[1,512,512]{2,1,0:T(8,128)(2,1)}, bf16[1,512,512]{2,1,0:T(8,128)(2,1)}, u32[]{:S(2)}, u32[]{:S(2)}) collective-permute-start(bf16[1,512,512]{2,1,0:T(8,128)(2,1)} %get-tuple-element.14), channel_id=1, source_target_pairs={{0,8},{8,16},{16,24},{24,0},{1,9},{9,17},{17,25},{25,1},{2,10},{10... | collective-permute-start | bytes 1572872 | tf_op jit(solution)/shard_map/ppermute | solution.py:23
  13.0 1.5 collective-permute-start.1
  14.5 1.4 collective-permute-start
  16.6 0.0 copy-done.5
  16.7 0.0 copy-done.6
  16.7 0.1 fusion.10
  16.8 0.0 copy-done.2
  16.8 0.5 select_reduce_fusion
  17.3 0.2 fusion.19
  18.2 0.3 fusion.9
  18.5 0.1 concatenate.63
  18.6 0.0 copy-start
  18.6 8.4 %collective-permute-done.2.refs_3_ = bf16[1,512,512]{2,1,0:T(8,128)(2,1)} collective-permute-done((bf16[1,512,512]{2,1,0:T(8,128)(2,1)}, bf16[1,512,512]{2,1,0:T(8,128)(2,1)}, u32[]{:S(2)}, u32[]{:S(2)}) %collective-permute-start.2) | collective-permute-done | bytes 524320 | tf_op jit(solution)/shard_map/ppermute | solution.py:23
  27.0 10.4 %collective-permute-done.1.refs_2_ = bf16[1,512,512]{2,1,0:T(8,128)(2,1)} collective-permute-done((bf16[1,512,512]{2,1,0:T(8,128)(2,1)S(1)}, bf16[1,512,512]{2,1,0:T(8,128)(2,1)}, u32[]{:S(2)}, u32[]{:S(2)}) %collective-permute-start.1) | collective-permute-done | bytes 524320 | tf_op jit(solution)/shard_map/ppermute | solution.py:23
  37.4 0.3 collective-permute-done.refs_1_
  37.7 26.8 %shard_map.156 = bf16[1,512,2560]{2,1,0:T(8,128)(2,1)} custom-call(s32[1]{0:T(128)S(6)} %sub.104.t0_ref, bf16[1,512,2560]{2,1,0:T(8,128)(2,1)} %q_ref.1, bf16[1,512,512]{2,1,0:T(8,128)(2,1)} %refs_0_.1, bf16[1,512,512]{2,1,0:T(8,128)(2,1)} %collective-permute-done.refs_1_, bf16[1,512,512]{2,1,0:T(8,128)(2,1)} %collective-permute-done.1.refs_2_, ...), custom_call_target="tpu_custom_call" | custom-call | flops 13421772800 | bytes 7864320 | tf_op jit(solution)/shard_map/pallas_call | solution.py:116
  64.5 0.0 copy-start.3
  64.6 0.0 copy-start.4
  64.6 0.8 slice_reduce_fusion
  65.4 0.1 concatenate.64
  65.5 10.4 %all_to_all.10 = bf16[8,2,320]{2,1,0:T(2,128)(2,1)S(1)} all-to-all(bf16[8,2,320]{2,1,0:T(2,128)(2,1)S(1)} %maximum_bitcast_fusion), channel_id=1, replica_groups=mesh['seq'=4,'vocab'=8] {'vocab'}, dimensions={0} | all-to-all | bytes 20480 | tf_op jit(solution)/shard_map/all_to_all | solution.py:224
  75.9 0.0 copy-done
  75.9 0.3 fusion.6
  76.2 0.8 copy.24
  77.0 4.7 %all-to-all-start.1 = ((f32[8,2,2560]{2,1,0:T(2,128)}), f32[8,2,2560]{2,1,0:T(2,128)S(1)}, u32[]{:S(2)}, u32[]{:S(2)}) async-start(f32[8,2,2560]{2,1,0:T(2,128)} %copy.24), calls=%async_computation.1 | async-start | bytes 327680 | tf_op jit(solution)/shard_map/all_to_all | solution.py:228
  81.8 0.8 slice_bitcast_fusion.1
  82.6 13.4 %all-to-all-done.1 = f32[8,2,2560]{2,1,0:T(2,128)S(1)} async-done(((f32[8,2,2560]{2,1,0:T(2,128)}), f32[8,2,2560]{2,1,0:T(2,128)S(1)}, u32[]{:S(2)}, u32[]{:S(2)}) %all-to-all-start.1) | async-done | bytes 163872 | tf_op jit(solution)/shard_map/all_to_all | solution.py:228
  96.0 0.1 reduce_sum.46
  96.0 0.0 copy-done.3
  96.0 0.2 fusion.25
  96.2 0.0 copy-done.4
  96.2 0.1 fusion.30
  96.3 8.3 %all-gather = bf16[4,2,2560]{2,1,0:T(2,128)(2,1)S(1)} all-gather(bf16[1,2,2560]{2,1,0:T(2,128)(2,1)S(1)} %fusion.30), channel_id=1, replica_groups=mesh['seq'=4,'vocab'=8] {'seq'}, dimensions={0}, use_global_device_ids=true | all-gather | bytes 51200 | tf_op jit(solution)/shard_map/all_gather | solution.py:233
  104.6 17.5 %all_gather.10 = bf16[64,2560]{1,0:T(8,128)(2,1)S(1)} all-gather(bf16[8,2560]{1,0:T(8,128)(2,1)S(1)} %reshape.169), channel_id=1, replica_groups=mesh['seq'=4,'vocab'=8] {'vocab'}, dimensions={0}, use_global_device_ids=true | all-gather | bytes 368640 | tf_op jit(solution)/shard_map/all_gather | solution.py:234
  122.2 0.1 reshape.161
  122.3 0.1 slice.59
  122.4 0.1 copy.34
  122.5 18.3 %fusion.43 = (f32[40]{0:T(128)S(1)}, f32[40,8000]{1,0:T(8,128)S(1)}) fusion(bf16[8000,2560]{1,0:T(8,128)(2,1)} %param.25, bf16[8,2560]{1,0:T(8,128)(2,1)S(1)} %bitcast.66, bf16[32,2560]{1,0:T(8,128)(2,1)S(1)} %bitcast.65), kind=kOutput, calls=%fused_computation.79 | convolution fusion | flops 1639129600 | bytes 42444960 | tf_op jit(solution)/shard_map/dot_general | solution.py:239
  140.8 0.4 exponential_reduce_fusion
  141.2 0.4 collective-permute-start.3
  141.7 0.0 all-gather.3.cloned.1.call-done
  141.7 0.0 copy-start.1
  141.7 11.0 %fusion.2 = f32[513,2560]{1,0:T(8,128)S(1)} fusion(bf16[2560,2560]{1,0:T(8,128)(2,1)} %all-gather.3.cloned.1.call-done, bf16[1,2560]{1,0:T(2,128)(2,1)S(1)} %bitcast.71, bf16[512,2560]{1,0:T(8,128)(2,1)} %bitcast.75), kind=kOutput, calls=%fused_computation.3 | convolution fusion | flops 6729246720 | bytes 20986880 | tf_op jit(solution)/shard_map/dot_general | solution.py:206
  152.7 0.0 copy-done.1
  152.7 2.3 %fusion.1 = bf16[1,512,2560]{2,1,0:T(8,128)(2,1)} fusion(f32[513,2560]{1,0:T(8,128)S(1)} %fusion.2, bf16[1,512,2560]{2,1,0:T(8,128)(2,1)S(1)} %copy-done.1), kind=kLoop, calls=%fused_computation.2 | loop fusion | flops 3932160 | bytes 10485760 | tf_op jit(solution)/shard_map/convert_element_type | solution.py:214
  155.0 0.6 fusion.29
  155.6 0.0 collective-permute-done.3
  155.6 1.0 collective-permute-start.4
  156.6 2.7 %collective-permute-done.4 = f32[2,2,40]{2,1,0:T(2,128)S(1)} collective-permute-done((f32[2,2,40]{2,1,0:T(2,128)S(1)}, f32[2,2,40]{2,1,0:T(2,128)S(1)}, u32[]{:S(2)}, u32[]{:S(2)}) %collective-permute-start.4) | collective-permute-done | bytes 672 | tf_op jit(solution)/shard_map/ppermute | solution.py:40
  159.2 1.8 %collective-permute-start.5 = (f32[4,2,40]{2,1,0:T(2,128)S(1)}, f32[4,2,40]{2,1,0:T(2,128)S(1)}, u32[]{:S(2)}, u32[]{:S(2)}) collective-permute-start(f32[4,2,40]{2,1,0:T(2,128)S(1)} %maximum_select_fusion.3), channel_id=1, source_target_pairs={{0,4},{1,5},{2,6},{3,7},{4,0},{5,1},{6,2},{7,3},{8,12},{9,13},{10,... | collective-permute-start | bytes 3848 | tf_op jit(solution)/shard_map/ppermute | solution.py:40
  161.0 2.7 %collective-permute-done.5 = f32[4,2,40]{2,1,0:T(2,128)S(1)} collective-permute-done((f32[4,2,40]{2,1,0:T(2,128)S(1)}, f32[4,2,40]{2,1,0:T(2,128)S(1)}, u32[]{:S(2)}, u32[]{:S(2)}) %collective-permute-start.5) | collective-permute-done | bytes 1312 | tf_op jit(solution)/shard_map/ppermute | solution.py:40
  163.8 2.0 %collective-permute-start.6 = (f32[8,2,40]{2,1,0:T(2,128)S(1)}, f32[8,2,40]{2,1,0:T(2,128)S(1)}, u32[]{:S(2)}, u32[]{:S(2)}) collective-permute-start(f32[8,2,40]{2,1,0:T(2,128)S(1)} %maximum_select_fusion.2), channel_id=1, source_target_pairs={{0,8},{8,0},{16,24},{24,16},{1,9},{9,1},{17,25},{25,17},{2,10},{10... | collective-permute-start | bytes 7688 | tf_op jit(solution)/shard_map/ppermute | solution.py:40
  165.8 1.7 collective-permute-done.6
  167.5 2.0 %collective-permute-start.7 = (f32[16,2,40]{2,1,0:T(2,128)S(1)}, f32[16,2,40]{2,1,0:T(2,128)S(1)}, u32[]{:S(2)}, u32[]{:S(2)}) collective-permute-start(f32[16,2,40]{2,1,0:T(2,128)S(1)} %maximum_select_fusion.1), channel_id=1, source_target_pairs={{0,16},{8,24},{16,0},{24,8},{1,17},{9,25},{17,1},{25,9},{2,18},{10... | collective-permute-start | bytes 15368 | tf_op jit(solution)/shard_map/ppermute | solution.py:40
  169.5 1.8 %collective-permute-done.7 = f32[16,2,40]{2,1,0:T(2,128)S(1)} collective-permute-done((f32[16,2,40]{2,1,0:T(2,128)S(1)}, f32[16,2,40]{2,1,0:T(2,128)S(1)}, u32[]{:S(2)}, u32[]{:S(2)}) %collective-permute-start.7) | collective-permute-done | bytes 5152 | tf_op jit(solution)/shard_map/ppermute | solution.py:40
  171.4 0.1 subtract_convert_fusion
  171.6 0.7 slice.65
  172.2 0.8 slice.64
  (22 shorter events, 0.3 us)
Async XLA Ops:
  7.2 9.4 %copy-start.5 = (bf16[1,2560]{1,0:T(2,128)(2,1)S(1)}, bf16[1,2560]{1,0:T(2,128)(2,1)}, u32[]{:S(2)}) copy-start(bf16[1,2560]{1,0:T(2,128)(2,1)} %param.18) | copy-start | bytes 15364
  7.2 9.5 %copy-start.6 = (bf16[1,512]{1,0:T(2,128)(2,1)S(1)}, bf16[1,512]{1,0:T(2,128)(2,1)}, u32[]{:S(2)}) copy-start(bf16[1,512]{1,0:T(2,128)(2,1)} %param.19) | copy-start | bytes 3076
  7.2 9.6 %copy-start.2 = (bf16[1,2048,512]{2,1,0:T(8,128)(2,1)S(1)}, bf16[1,2048,512]{2,1,0:T(8,128)(2,1)}, u32[]{:S(2)}) copy-start(bf16[1,2048,512]{2,1,0:T(8,128)(2,1)} %param.20) | copy-start | bytes 6291460
  7.2 134.5 %all-gather.3.cloned.1.call-start = ((), (), s32[]{:S(2)}) async-start(), calls=%async_computation.2 | async-start | bytes 14745600 | tf_op jit(solution)/shard_map/all_gather | solution.py:208
  10.0 17.0 %collective-permute-start.2 = (bf16[1,512,512]{2,1,0:T(8,128)(2,1)}, bf16[1,512,512]{2,1,0:T(8,128)(2,1)}, u32[]{:S(2)}, u32[]{:S(2)}) collective-permute-start(bf16[1,512,512]{2,1,0:T(8,128)(2,1)} %get-tuple-element.14), channel_id=1, source_target_pairs={{0,8},{8,16},{16,24},{24,0},{1,9},{9,17},{17,25},{25,1},{2,10},{10... | collective-permute-start | bytes 1572872 | tf_op jit(solution)/shard_map/ppermute | solution.py:23
  13.0 24.4 %collective-permute-start.1 = (bf16[1,512,512]{2,1,0:T(8,128)(2,1)S(1)}, bf16[1,512,512]{2,1,0:T(8,128)(2,1)}, u32[]{:S(2)}, u32[]{:S(2)}) collective-permute-start(bf16[1,512,512]{2,1,0:T(8,128)(2,1)S(1)} %get-tuple-element.15), channel_id=1, source_target_pairs={{0,16},{8,24},{16,0},{24,8},{1,17},{9,25},{17,1},{25,9},{2,18},{10... | collective-permute-start | bytes 1572872 | tf_op jit(solution)/shard_map/ppermute | solution.py:23
  14.5 23.2 %collective-permute-start = (bf16[1,512,512]{2,1,0:T(8,128)(2,1)S(1)}, bf16[1,512,512]{2,1,0:T(8,128)(2,1)}, u32[]{:S(2)}, u32[]{:S(2)}) collective-permute-start(bf16[1,512,512]{2,1,0:T(8,128)(2,1)S(1)} %get-tuple-element.16), channel_id=1, source_target_pairs={{0,24},{8,0},{16,8},{24,16},{1,25},{9,1},{17,9},{25,17},{2,26},{10... | collective-permute-start | bytes 1572872 | tf_op jit(solution)/shard_map/ppermute | solution.py:23
  18.6 57.3 %copy-start = (bf16[320,2560]{1,0:T(8,128)(2,1)S(1)}, bf16[320,2560]{1,0:T(8,128)(2,1)}, u32[]{:S(2)}) copy-start(bf16[320,2560]{1,0:T(8,128)(2,1)} %param.23) | copy-start | bytes 4915204
  64.5 31.5 %copy-start.3 = (bf16[1,2560]{1,0:T(2,128)(2,1)S(1)}, bf16[1,2560]{1,0:T(2,128)(2,1)}, u32[]{:S(2)}) copy-start(bf16[1,2560]{1,0:T(2,128)(2,1)} %param.22) | copy-start | bytes 15364
  64.6 31.7 %copy-start.4 = (f32[2560]{0:T(1024)S(1)}, f32[2560]{0:T(1024)}, u32[]{:S(2)}) copy-start(f32[2560]{0:T(1024)} %param.24) | copy-start | bytes 30724
  77.0 18.9 %all-to-all-start.1 = ((f32[8,2,2560]{2,1,0:T(2,128)}), f32[8,2,2560]{2,1,0:T(2,128)S(1)}, u32[]{:S(2)}, u32[]{:S(2)}) async-start(f32[8,2,2560]{2,1,0:T(2,128)} %copy.24), calls=%async_computation.1 | async-start | bytes 327680 | tf_op jit(solution)/shard_map/all_to_all | solution.py:228
  141.2 14.3 %collective-permute-start.3 = (f32[1,2,40]{2,1,0:T(2,128)S(1)}, f32[1,2,40]{2,1,0:T(2,128)S(1)}, u32[]{:S(2)}, u32[]{:S(2)}) collective-permute-start(f32[1,2,40]{2,1,0:T(2,128)S(1)} %maximum_bitcast_fusion.1), channel_id=1, source_target_pairs={{0,1},{1,0},{2,3},{3,2},{4,5},{5,4},{6,7},{7,6},{8,9},{9,8},{10,11... | collective-permute-start | bytes 968 | tf_op jit(solution)/shard_map/ppermute | solution.py:40
  141.7 11.0 %copy-start.1 = (bf16[1,512,2560]{2,1,0:T(8,128)(2,1)S(1)}, bf16[1,512,2560]{2,1,0:T(8,128)(2,1)}, u32[]{:S(2)}) copy-start(bf16[1,512,2560]{2,1,0:T(8,128)(2,1)} %param.17) | copy-start | bytes 7864324
  155.6 3.7 %collective-permute-start.4 = (f32[2,2,40]{2,1,0:T(2,128)S(1)}, f32[2,2,40]{2,1,0:T(2,128)S(1)}, u32[]{:S(2)}, u32[]{:S(2)}) collective-permute-start(f32[2,2,40]{2,1,0:T(2,128)S(1)} %maximum_select_fusion.4), channel_id=1, source_target_pairs={{0,2},{1,3},{2,0},{3,1},{4,6},{5,7},{6,4},{7,5},{8,10},{9,11},{10,... | collective-permute-start | bytes 1928 | tf_op jit(solution)/shard_map/ppermute | solution.py:40
  159.2 4.5 %collective-permute-start.5 = (f32[4,2,40]{2,1,0:T(2,128)S(1)}, f32[4,2,40]{2,1,0:T(2,128)S(1)}, u32[]{:S(2)}, u32[]{:S(2)}) collective-permute-start(f32[4,2,40]{2,1,0:T(2,128)S(1)} %maximum_select_fusion.3), channel_id=1, source_target_pairs={{0,4},{1,5},{2,6},{3,7},{4,0},{5,1},{6,2},{7,3},{8,12},{9,13},{10,... | collective-permute-start | bytes 3848 | tf_op jit(solution)/shard_map/ppermute | solution.py:40
  163.8 3.7 %collective-permute-start.6 = (f32[8,2,40]{2,1,0:T(2,128)S(1)}, f32[8,2,40]{2,1,0:T(2,128)S(1)}, u32[]{:S(2)}, u32[]{:S(2)}) collective-permute-start(f32[8,2,40]{2,1,0:T(2,128)S(1)} %maximum_select_fusion.2), channel_id=1, source_target_pairs={{0,8},{8,0},{16,24},{24,16},{1,9},{9,1},{17,25},{25,17},{2,10},{10... | collective-permute-start | bytes 7688 | tf_op jit(solution)/shard_map/ppermute | solution.py:40
  167.5 3.8 %collective-permute-start.7 = (f32[16,2,40]{2,1,0:T(2,128)S(1)}, f32[16,2,40]{2,1,0:T(2,128)S(1)}, u32[]{:S(2)}, u32[]{:S(2)}) collective-permute-start(f32[16,2,40]{2,1,0:T(2,128)S(1)} %maximum_select_fusion.1), channel_id=1, source_target_pairs={{0,16},{8,24},{16,0},{24,8},{1,17},{9,25},{17,1},{25,9},{2,18},{10... | collective-permute-start | bytes 15368 | tf_op jit(solution)/shard_map/ppermute | solution.py:40
Sparse Core Ops, SparseCore 0:
  9.7 130.0 all-gather.2
